TPU v7x, 512 devices: a whole 4x8x8 slice. The times are simulated.
512 devices in a mesh: op: 16 (over y, core), sec: 32 (over x, z).
Axes of the slice: x: 4, y: 8, z: 8, core: 2. Of those that a mesh axis runs over, the one named last changes fastest.
Arguments:
- wavefunction: bfloat16 [128, 64, 1024], P('sec'), may hold values from -6 to 6
- left_env: bfloat16 [128, 128, 64, 64], P('op', 'sec'), may hold values from -0.75 to 0.75
- right_env: bfloat16 [64, 128, 64, 64], P('op', 'sec'), may hold values from -0.75 to 0.75
- local_ops: bfloat16 [128, 4, 16, 16], P('op'), may hold values from -0.0625 to 0.0625
- dest_sector: int32 [128, 128], P('op'), may hold values from 0 to 127, as said below
- right_bond: int32 [128, 4], P('op'), may hold values from 0 to 3
Outputs:
- new_vector: bfloat16 [128, 64, 1024], P('sec', 'op')
Inputs may be any that keep to these rules, and one draw needn't show every extreme that they name: `dest_sector`: for each operator group (rows a with equal a // 8) and each block of 4 source sectors, exactly 1 of those 32 entries fall into each block of 4 destination sectors.
All inputs are finite; a program needn't handle non-finite values.
Results may differ from a plain program's by a relative error of at most 0.018.
Values may be sent and summed in bfloat16 or wider, within the bound.
No kernel may reach another device: no remote copies, remote signals or barrier semaphores. Data moves between devices by JAX's collectives and lax.ppermute only.
A program may use at most 128 MiB of HBM per device.

v0:
```python
import jax
import jax.numpy as jnp
from jax import lax
from jax.sharding import PartitionSpec as P


def body(wavefunction, left_env, right_env, local_ops, dest_sector, right_bond):
    sec_blocks, block_rows, block_width = wavefunction.shape
    left_count = left_env.shape[0]
    physical = block_width // block_rows
    sec_count = lax.axis_size("sec")
    op_count = lax.axis_size("op")
    item_count = left_count * sec_blocks
    per_peer = item_count // sec_count
    own_sec = lax.axis_index("sec")
    moved = jnp.einsum("asij,sjx->asix", left_env, wavefunction, preferred_element_type=jnp.float32)
    moved = moved.astype(jnp.bfloat16).reshape(item_count, block_rows, block_width)
    everyone = (
        dest_sector.reshape(left_count, sec_count, sec_blocks)
        .transpose(1, 0, 2)
        .reshape(sec_count, item_count)
    )
    target_dev = everyone // sec_blocks
    target_loc = everyone % sec_blocks
    counter = jnp.arange(item_count, dtype=jnp.int32)
    orders = jnp.argsort(target_dev * item_count + counter[None, :], axis=1)
    own_order = lax.dynamic_index_in_dim(orders, own_sec, 0, keepdims=False)
    outgoing = jnp.take(moved, own_order, axis=0).reshape(
        sec_count, per_peer, block_rows, block_width
    )
    incoming = lax.all_to_all(outgoing, "sec", split_axis=0, concat_axis=0, tiled=True)
    incoming = incoming.reshape(item_count, block_rows, physical, block_rows)
    picked = lax.dynamic_slice_in_dim(orders, own_sec * per_peer, per_peer, 1)
    bond_index = (picked // sec_blocks).reshape(item_count)
    sector_index = jnp.take_along_axis(target_loc, picked, axis=1).reshape(item_count)
    bond_hot = bond_index[:, None] == jnp.arange(left_count, dtype=jnp.int32)[None, :]
    sector_hot = sector_index[:, None] == jnp.arange(sec_blocks, dtype=jnp.int32)[None, :]
    flat_env = right_env.reshape(-1, block_rows, block_rows)
    all_ops = jnp.einsum(
        "na,atpq->ntpq",
        bond_hot.astype(jnp.bfloat16),
        local_ops,
        preferred_element_type=jnp.float32,
    ).astype(jnp.bfloat16)
    mixed = jnp.einsum(
        "ntpq,nlqr->nlptr", all_ops, incoming, preferred_element_type=jnp.float32
    ).astype(jnp.bfloat16)
    bond_right = jnp.sum(jnp.where(bond_hot[:, :, None], right_bond[None, :, :], 0), axis=1)
    chosen = jnp.take(flat_env, bond_right * sec_blocks + sector_index[:, None], axis=0)
    accum = jnp.einsum("nlptr,ntsr->nlps", mixed, chosen, preferred_element_type=jnp.float32)
    partial_value = jnp.dot(
        sector_hot.astype(jnp.float32).T,
        accum.reshape(item_count, -1),
        precision=lax.Precision.HIGHEST,
        preferred_element_type=jnp.float32,
    )
    partial_value = partial_value.reshape(sec_blocks, block_rows, block_width)
    summed = lax.psum(partial_value.astype(jnp.bfloat16), "op").astype(jnp.float32)
    row_share = block_rows // op_count
    summed = lax.dynamic_slice_in_dim(summed, lax.axis_index("op") * row_share, row_share, 1)
    return summed.astype(jnp.bfloat16)


def solution(mesh):
    return jax.shard_map(
        body,
        mesh=mesh,
        in_specs=(
            P("sec", None, None),
            P("op", "sec", None, None),
            P("op", "sec", None, None),
            P("op", None, None, None),
            P("op", None),
            P("op", None),
        ),
        out_specs=P("sec", "op", None),
        check_vma=False,
    )
```

profile of v0, /device:TPU:1, one launch (start us, length us, event | category | flops | bytes accessed | tf_op | source)
XLA Modules:
  0.0 371.0 jit_solution(3560896886313633219)
XLA Ops:
  6.5 0.0 copy-start
  6.5 0.8 copy.47
  7.4 0.1 copy.48
  7.5 0.1 copy.49
  7.6 0.1 copy.53
  7.7 0.8 sort.17
  8.5 0.2 dynamic-slice_reduce_fusion
  8.7 0.0 copy-done
  8.7 2.3 convert_bitcast_fusion.1
  11.0 2.4 copy.55
  13.4 5.0 %gather_fusion = bf16[32,64,1024]{2,1,0:T(8,128)(2,1)} fusion(bf16[32,64,1024]{2,1,0:T(8,128)(2,1)} %bitcast.80, s32[1024]{0:T(1024)S(1)} %pad_clamp_fusion.1), kind=kCustom, calls=%fused_computation | custom fusion | bytes 8388736 | tf_op jit(solution)/shard_map/jit(_take)/gather | solution.py:28
  18.4 4.6 %fusion.9 = bf16[32,1,64,1024]{3,2,1,0:T(8,128)(2,1)} fusion(bf16[32,64,1024]{2,1,0:T(8,128)(2,1)} %gather_fusion, pred[32]{0:T(512)(128)(4,1)S(1)} %compare_and_fusion.1), kind=kLoop, calls=%fused_computation.12 | loop fusion | flops 2097152 | bytes 8388640 | tf_op jit(solution)/shard_map/jit(_take)/select_n | solution.py:28
  23.0 0.0 copy-start.4
  23.0 0.0 copy-start.3
  23.0 0.0 copy-start.2
  23.0 14.0 %all-to-all-start = ((bf16[32,1,64,1024]{3,2,1,0:T(8,128)(2,1)}), bf16[32,1,64,1024]{3,2,1,0:T(8,128)(2,1)}, u32[]{:S(2)}, u32[]{:S(2)}) async-start(bf16[32,1,64,1024]{3,2,1,0:T(8,128)(2,1)} %fusion.9), calls=%async_computation | async-start | bytes 8388608 | tf_op jit(solution)/shard_map/all_to_all | solution.py:31
  37.0 0.0 all-reduce.2.cloned.1.call-start
  37.0 0.7 gather_fusion.2
  37.8 0.0 copy-done.4
  37.8 0.1 select_reduce_fusion
  37.9 0.1 copy.59
  38.0 0.1 copy.60
  38.1 0.1 reshape.179
  38.2 0.0 copy-done.3
  38.2 0.3 fusion.16
  38.5 0.9 copy.68
  39.4 0.0 copy-done.2
  39.4 1.0 gather_fusion.1
  40.4 89.2 %all-to-all-done = bf16[32,1,64,1024]{3,2,1,0:T(8,128)(2,1)} async-done(((bf16[32,1,64,1024]{3,2,1,0:T(8,128)(2,1)}), bf16[32,1,64,1024]{3,2,1,0:T(8,128)(2,1)}, u32[]{:S(2)}, u32[]{:S(2)}) %all-to-all-start) | async-done | bytes 4194336 | tf_op jit(solution)/shard_map/all_to_all | solution.py:31
  129.6 11.6 %reshape.196 = bf16[32,64,16,64,1]{3,2,1,0,4:T(8,128)(2,1)} reshape(bf16[32,1,64,1024]{3,2,1,0:T(8,128)(2,1)} %all-to-all-done) | data formatting | bytes 8388608 | tf_op jit(solution)/shard_map/reshape | solution.py:32
  141.2 18.0 %convert_bitcast_fusion = bf16[32,64,16,4,64]{4,2,3,1,0:T(8,128)(2,1)} fusion(bf16[32,4,16,16,1]{3,2,1,4,0:T(8,128)(2,1)S(1)} %copy.68, bf16[32,64,16,64,1]{3,2,1,0,4:T(8,128)(2,1)} %reshape.196), kind=kOutput, calls=%fused_computation.5 | convolution fusion | flops 276824064 | bytes 21037056 | tf_op jit(solution)/shard_map/ntpq,nlqr->nlptr/dot_general | solution.py:45
  159.2 51.0 %fusion.2 = f32[32,64,16,64]{3,1,2,0:T(8,128)} fusion(bf16[32,64,16,4,64]{4,2,3,1,0:T(8,128)(2,1)} %convert_bitcast_fusion, bf16[32,4,64,64]{3,2,1,0:T(8,128)(2,1)S(1)} %bitcast.82, pred[32,4]{1,0:T(8,128)(4,1)S(1)} %copy.59), kind=kOutput, calls=%fused_computation.6 | convolution fusion | flops 1074266112 | bytes 26214528 | tf_op jit(solution)/shard_map/nlptr,ntsr->nlps/dot_general | solution.py:50
  210.2 18.4 %copy.62 = f32[32,64,16,64]{3,2,1,0:T(8,128)} copy(f32[32,64,16,64]{3,1,2,0:T(8,128)} %fusion.2) | data formatting | bytes 16777216 | tf_op jit(solution)/shard_map/nlptr,ntsr->nlps/dot_general | solution.py:50
  228.6 10.9 %reshape.168 = f32[32,65536]{1,0:T(8,128)} reshape(f32[32,64,16,64]{3,2,1,0:T(8,128)} %copy.62) | data formatting | bytes 16777216 | tf_op jit(solution)/shard_map/reshape | solution.py:53
  239.5 0.0 copy-start.1
  239.5 7.0 %fusion.13 = bf16[4,64,1024]{2,0,1:T(4,128)(2,1)} fusion(f32[4,64,8,1024]{3,2,1,0:T(8,128)} %bitcast.79, s32[32]{0:T(128)S(1)} %get-tuple-element.7), kind=kOutput, calls=%fused_computation.17 | convolution fusion | flops 100925568 | bytes 8913024 | tf_op jit(solution)/shard_map/dot_general | solution.py:51
  246.5 0.0 all-reduce.2.cloned.1.call-update
  246.6 116.2 %all-reduce.2.cloned.1.call-done = bf16[4,64,1024]{2,0,1:T(4,128)(2,1)} async-done(((bf16[4,64,1024]{2,0,1:T(4,128)(2,1)}), bf16[4,64,1024]{2,0,1:T(4,128)(2,1)}) %all-reduce.2.cloned.1.call-update) | async-done | bytes 524304 | tf_op jit(solution)/shard_map/psum | solution.py:58
  362.8 0.8 convert_convert_fusion
  363.6 0.6 copy.64
  364.2 0.0 copy-done.1
  (13 shorter events, 0.1 us)
Async XLA Ops:
  6.5 2.2 copy-start
  23.0 14.8 %copy-start.4 = (s32[8,4]{0,1:T(4,128)S(1)}, s32[8,4]{0,1:T(4,128)}, u32[]{:S(2)}) copy-start(s32[8,4]{0,1:T(4,128)} %param.11) | copy-start | bytes 388
  23.0 15.2 %copy-start.3 = (bf16[8,4,16,16]{3,2,1,0:T(8,128)(2,1)S(1)}, bf16[8,4,16,16]{3,2,1,0:T(8,128)(2,1)}, u32[]{:S(2)}) copy-start(bf16[8,4,16,16]{3,2,1,0:T(8,128)(2,1)} %param.9) | copy-start | bytes 49156
  23.0 16.4 %copy-start.2 = (bf16[4,4,64,64]{3,2,1,0:T(8,128)(2,1)S(1)}, bf16[4,4,64,64]{3,2,1,0:T(8,128)(2,1)}, u32[]{:S(2)}) copy-start(bf16[4,4,64,64]{3,2,1,0:T(8,128)(2,1)} %param.8) | copy-start | bytes 393220
  23.0 106.6 %all-to-all-start = ((bf16[32,1,64,1024]{3,2,1,0:T(8,128)(2,1)}), bf16[32,1,64,1024]{3,2,1,0:T(8,128)(2,1)}, u32[]{:S(2)}, u32[]{:S(2)}) async-start(bf16[32,1,64,1024]{3,2,1,0:T(8,128)(2,1)} %fusion.9), calls=%async_computation | async-start | bytes 8388608 | tf_op jit(solution)/shard_map/all_to_all | solution.py:31
  37.0 325.8 %all-reduce.2.cloned.1.call-start = ((), (), s32[]{:S(2)}) async-start(), calls=%async_computation.1 | async-start | bytes 1048576 | tf_op jit(solution)/shard_map/psum | solution.py:58
  239.5 124.7 %copy-start.1 = (bf16[4,64,1024]{2,1,0:T(8,128)(2,1)S(1)}, bf16[4,64,1024]{2,1,0:T(8,128)(2,1)}, u32[]{:S(2)}) copy-start(bf16[4,64,1024]{2,1,0:T(8,128)(2,1)} %param.6) | copy-start | bytes 1572868
Sparse Core Ops, SparseCore 0:
  246.7 116.0 all-reduce.1
where the time goes:
time: 372 us; the launch traced here: 371 us
  waiting for transfers between devices  205 us (55%)
  matrix products  78.6 us (21%)
  local copies, waits for them, and re-layouts  53 us (14%)
  starting transfers between devices  14 us (4%)
  between operations  13.6 us (4%)
  other arithmetic  6.41 us (2%)
    psum x1, waiting for transfers between devices, body(): lax.psum(partial_value.astype(jnp.bfloat16), 'op').astype(jnp.float32)  116 us
    all_to_all x1, waiting for transfers between devices, body(): lax.all_to_all(outgoing, 'sec', split_axis=0, concat_axis=0, tiled=True)  89.2 us
    dot_general x1, matrix products, body(): jnp.einsum('nlptr,ntsr->nlps', mixed, chosen, preferred_element_type=jnp....  51 us
    dot_general x1, local copies, waits for them, and re-layouts, body(): jnp.einsum('nlptr,ntsr->nlps', mixed, chosen, preferred_element_type=jnp....  18.4 us
    dot_general x1, matrix products, body(): jnp.einsum('ntpq,nlqr->nlptr', all_ops, incoming, preferred_element_type=...  18 us
    all_to_all x1, starting transfers between devices, body(): lax.all_to_all(outgoing, 'sec', split_axis=0, concat_axis=0, tiled=True)  14 us
    reshape x1, local copies, waits for them, and re-layouts, body(): incoming = incoming.reshape(item_count, block_rows, physical, block_rows)  11.6 us
    reshape x1, local copies, waits for them, and re-layouts, body(): accum.reshape(item_count, -1)  10.9 us
  transfers between devices with their start and end apart: 2, of which 2 were waited for; matrix products, arithmetic and copies ran while one was open for 1% of the time, Pallas kernels for 0%

commit v1 on v0

v1 whole, which is shorter than its diff:
```python
import jax
import jax.numpy as jnp
from jax import lax
from jax.sharding import PartitionSpec as P


def body(wavefunction, left_env, right_env, local_ops, dest_sector, right_bond):
    sec_blocks, rows, width = wavefunction.shape
    left_count = left_env.shape[0]
    right_count = right_env.shape[0]
    terms = local_ops.shape[1]
    physical = width // rows
    sec_count = lax.axis_size("sec")
    op_count = lax.axis_size("op")
    own_sec = lax.axis_index("sec")
    f32 = jnp.float32
    bf16 = jnp.bfloat16

    own_dest = lax.dynamic_slice_in_dim(dest_sector, own_sec * sec_blocks, sec_blocks, 1)
    target = own_dest // sec_blocks
    peers = jnp.arange(sec_count, dtype=jnp.int32)
    send_hot = (target[:, :, None] == peers[None, None, :]).astype(bf16)
    chosen_left = jnp.einsum(
        "ask,asij->kisj", send_hot, left_env, preferred_element_type=f32
    ).astype(bf16)
    outgoing = jnp.einsum(
        "kisj,sjx->kix", chosen_left, wavefunction, preferred_element_type=f32
    ).astype(bf16)
    incoming = lax.all_to_all(outgoing, "sec", 0, 0, tiled=True)
    incoming = incoming.reshape(sec_count, rows, physical, rows)

    grid = dest_sector.reshape(left_count, sec_count, sec_blocks)
    mine = (grid // sec_blocks) == own_sec
    bond_hot = jnp.sum(mine, axis=2).T.astype(bf16)
    local_dest = jnp.sum(jnp.where(mine, grid % sec_blocks, 0), axis=(0, 2))
    dest_hot = local_dest[:, None] == jnp.arange(sec_blocks, dtype=jnp.int32)[None, :]
    item_ops = jnp.einsum(
        "ia,atpq->itpq", bond_hot, local_ops, preferred_element_type=f32
    ).astype(bf16)
    item_bond = jnp.einsum(
        "ia,at->it", bond_hot.astype(f32), right_bond.astype(f32)
    ).astype(jnp.int32)
    env_hot = (
        (item_bond[:, :, None, None] == jnp.arange(right_count, dtype=jnp.int32)[None, None, :, None])
        & dest_hot[:, None, None, :]
    ).astype(bf16)
    item_env = jnp.einsum(
        "itbd,bdmr->itmr", env_hot, right_env, preferred_element_type=f32
    ).astype(bf16)
    mixed = jnp.einsum(
        "itpq,ilqr->itlpr", item_ops, incoming, preferred_element_type=f32
    ).astype(bf16)
    accum = jnp.einsum("itlpr,itmr->ilpm", mixed, item_env, preferred_element_type=f32)
    partial_value = jnp.einsum(
        "id,ilpm->dlpm",
        dest_hot.astype(f32),
        accum,
        precision=lax.Precision.HIGHEST,
        preferred_element_type=f32,
    )
    share = rows // op_count
    pieces = partial_value.astype(bf16).reshape(sec_blocks, op_count, share, width)
    pieces = pieces.transpose(1, 0, 2, 3)
    gathered = lax.all_to_all(pieces, "op", 0, 0, tiled=True)
    summed = jnp.sum(gathered.astype(f32), axis=0)
    return summed.astype(bf16)


def solution(mesh):
    return jax.shard_map(
        body,
        mesh=mesh,
        in_specs=(
            P("sec", None, None),
            P("op", "sec", None, None),
            P("op", "sec", None, None),
            P("op", None, None, None),
            P("op", None),
            P("op", None),
        ),
        out_specs=P("sec", "op", None),
        check_vma=False,
    )
```

time: 372 us -> 230 us (0.62)
  waiting for transfers between devices: 205 us -> 89.9 us
  local copies, waits for them, and re-layouts: 53 us -> 13.7 us
  blocking collectives: 0 us -> 29.6 us
  between operations: 13.6 us -> 0.17 us
  other arithmetic: 6.41 us -> 1.95 us
    psum x1 -> x0, waiting for transfers between devices: 116 us -> none  [body(): lax.psum(partial_value.astype(jnp.bfloat16), 'op').astype(jnp.float32)]
    all_to_all x0 -> x1, blocking collectives: none -> 29.6 us  [body(): gathered = lax.all_to_all(pieces, 'op', 0, 0, tiled=True)]
    dot_general x1 -> x0, local copies, waits for them, and re-layouts: 18.4 us -> none  [body(): jnp.einsum('nlptr,ntsr->nlps', mixed, chosen, preferred_element_type=jnp....]
    reshape x3 -> x2, local copies, waits for them, and re-layouts: 22.5 us -> 12.2 us  [the longest x1 11.6 us: body(): incoming = incoming.reshape(sec_count, rows, physical, rows)]
    gather x3 -> x0, local copies, waits for them, and re-layouts: 6.64 us -> none  [the longest x1 4.97 us: body(): jnp.take(moved, own_order, axis=0)]
    select_n x4 -> x1, other arithmetic: 4.67 us -> 0.82 us  [body(): target = own_dest // sec_blocks]
    dot_general x5 -> x8, matrix products: 78.6 us -> 80 us  [the longest x1 31.9 us: body(): jnp.einsum('itlpr,itmr->ilpm', mixed, item_env, preferred_element_type=f32)]
  transfers between devices with their start and end apart: 2 -> 1, of which waited for: 2 -> 1; matrix products, arithmetic and copies ran while one was open for 1% -> 1% of each run, Pallas kernels for 0% -> 0%
where the time goes in v1:
time: 230 us; the launch traced here: 229 us
  waiting for transfers between devices  89.9 us (39%)
  matrix products  80 us (35%)
  blocking collectives  29.6 us (13%)
  starting transfers between devices  14 us (6%)
  local copies, waits for them, and re-layouts  13.7 us (6%)
    all_to_all x1, waiting for transfers between devices, body(): incoming = lax.all_to_all(outgoing, 'sec', 0, 0, tiled=True)  89.9 us
    dot_general x1, matrix products, body(): jnp.einsum('itlpr,itmr->ilpm', mixed, item_env, preferred_element_type=f32)  31.9 us
    all_to_all x1, blocking collectives, body(): gathered = lax.all_to_all(pieces, 'op', 0, 0, tiled=True)  29.6 us
    dot_general x1, matrix products, body(): jnp.einsum('id,ilpm->dlpm', dest_hot.astype(f32), accum, precision=lax.Pr...  23.2 us
    dot_general x1, matrix products, body(): jnp.einsum('itpq,ilqr->itlpr', item_ops, incoming, preferred_element_type...  18 us
    all_to_all x1, starting transfers between devices, body(): incoming = lax.all_to_all(outgoing, 'sec', 0, 0, tiled=True)  14 us
    reshape x1, local copies, waits for them, and re-layouts, body(): incoming = incoming.reshape(sec_count, rows, physical, rows)  11.6 us
  transfers between devices with their start and end apart: 1, of which 1 were waited for; matrix products, arithmetic and copies ran while one was open for 1% of the time, Pallas kernels for 0%

profile of v1, /device:TPU:1, one launch (start us, length us, event | category | flops | bytes accessed | tf_op | source)
XLA Modules:
  0.0 229.3 jit_solution(2096543701093025990)
XLA Ops:
  0.0 0.0 copy-start
  0.0 0.8 add_select_fusion.1
  0.8 0.1 copy.11
  0.9 1.9 convert_bitcast_fusion.1
  2.8 0.0 copy-done
  2.8 0.0 copy-start.3
  2.8 0.0 copy-start.2
  2.8 0.0 copy-start.4
  2.8 0.0 copy-start.5
  2.8 3.7 %bitcast_convert_fusion = bf16[32,64,1024]{2,1,0:T(8,128)(2,1)} fusion(bf16[32,64,4,64]{3,0,1,2:T(8,128)(2,1)S(1)} %convert_bitcast_fusion.1, bf16[4,64,1024]{2,1,0:T(8,128)(2,1)S(1)} %copy-done), kind=kOutput, calls=%fused_computation.7 | convolution fusion | flops 1075838976 | bytes 5767168 | tf_op jit(solution)/shard_map/kisj,sjx->kix/dot_general | solution.py:26
  6.5 14.0 %all-to-all-start = ((bf16[32,64,1024]{2,1,0:T(8,128)(2,1)}), bf16[32,64,1024]{2,1,0:T(8,128)(2,1)}, u32[]{:S(2)}, u32[]{:S(2)}) async-start(bf16[32,64,1024]{2,1,0:T(8,128)(2,1)} %bitcast_convert_fusion), calls=%async_computation | async-start | bytes 8388608 | tf_op jit(solution)/shard_map/all_to_all | solution.py:29
  20.6 0.0 copy-done.3
  20.6 0.1 copy.14
  20.7 0.1 reduce_sum.38
  20.8 0.1 reduce_sum.39
  20.9 0.1 convert_reduce_fusion
  21.1 0.0 copy-done.2
  21.1 0.3 fusion.14
  21.4 0.9 copy.28
  22.3 0.0 copy-done.4
  22.3 0.1 convolution_convert_fusion.1
  22.4 0.0 copy-done.5
  22.4 0.9 fusion.10
  23.3 89.9 %all-to-all-done = bf16[32,64,1024]{2,1,0:T(8,128)(2,1)} async-done(((bf16[32,64,1024]{2,1,0:T(8,128)(2,1)}), bf16[32,64,1024]{2,1,0:T(8,128)(2,1)}, u32[]{:S(2)}, u32[]{:S(2)}) %all-to-all-start) | async-done | bytes 4194336 | tf_op jit(solution)/shard_map/all_to_all | solution.py:29
  113.2 11.6 %reshape.42 = bf16[32,64,16,64,1]{3,2,1,0,4:T(8,128)(2,1)} reshape(bf16[32,64,1024]{2,1,0:T(8,128)(2,1)} %all-to-all-done) | data formatting | bytes 8388608 | tf_op jit(solution)/shard_map/reshape | solution.py:30
  124.7 18.0 %convert_bitcast_fusion = bf16[32,4,64,16,64]{4,3,1,2,0:T(8,128)(2,1)} fusion(bf16[32,4,16,16,1]{3,2,1,4,0:T(8,128)(2,1)S(1)} %copy.28, bf16[32,64,16,64,1]{3,2,1,0,4:T(8,128)(2,1)} %reshape.42), kind=kOutput, calls=%fused_computation.2 | convolution fusion | flops 276824064 | bytes 21037056 | tf_op jit(solution)/shard_map/itpq,ilqr->itlpr/dot_general | solution.py:50
  142.8 0.0 copy-start.1
  142.8 31.9 %fusion.4 = f32[32,64,16,64]{3,1,2,0:T(8,128)} fusion(bf16[32,4,64,16,64]{4,3,1,2,0:T(8,128)(2,1)} %convert_bitcast_fusion, bf16[32,4,64,64,1]{3,0,2,1,4:T(8,128)(2,1)S(1)} %fusion.10), kind=kOutput, calls=%fused_computation.5 | convolution fusion | flops 1073741824 | bytes 26214400 | tf_op jit(solution)/shard_map/itlpr,itmr->ilpm/dot_general | solution.py:53
  174.6 23.2 %fusion.11 = bf16[4,64,16,64]{3,0,2,1:T(4,128)(2,1)S(1)} fusion(f32[32,64,16,64]{3,1,2,0:T(8,128)} %fusion.4, s32[32]{0:T(128)S(1)} %reduce_sum.39), kind=kOutput, calls=%fused_computation.13 | convolution fusion | flops 100925568 | bytes 8913024 | tf_op jit(solution)/shard_map/id,ilpm->dlpm/dot_general | solution.py:54
  197.9 0.1 copy.22
  198.0 0.6 reshape.37
  198.6 0.2 copy.23
  198.9 29.6 %all_to_all.10 = bf16[16,4,4,1024]{3,2,1,0:T(4,128)(2,1)S(1)} all-to-all(bf16[16,4,4,1024]{3,2,1,0:T(4,128)(2,1)S(1)} %copy.23), channel_id=1, replica_groups=mesh['op'=16,'sec'=32] {'op'}, dimensions={0} | all-to-all | bytes 1048576 | tf_op jit(solution)/shard_map/all_to_all | solution.py:64
  228.5 0.8 reduce_sum.41
  229.3 0.0 copy-done.1
  (3 shorter events, 0.0 us)
Async XLA Ops:
  0.0 2.8 %copy-start = (bf16[4,64,1024]{2,1,0:T(8,128)(2,1)S(1)}, bf16[4,64,1024]{2,1,0:T(8,128)(2,1)}, u32[]{:S(2)}) copy-start(bf16[4,64,1024]{2,1,0:T(8,128)(2,1)} %param.6) | copy-start | bytes 1572868
  2.8 17.8 %copy-start.3 = (s32[8,128]{1,0:T(8,128)S(1)}, s32[8,128]{1,0:T(8,128)}, u32[]{:S(2)}) copy-start(s32[8,128]{1,0:T(8,128)} %param.10) | copy-start | bytes 12292
  2.8 18.3 %copy-start.2 = (bf16[8,4,16,16]{3,2,1,0:T(8,128)(2,1)S(1)}, bf16[8,4,16,16]{3,2,1,0:T(8,128)(2,1)}, u32[]{:S(2)}) copy-start(bf16[8,4,16,16]{3,2,1,0:T(8,128)(2,1)} %param.9) | copy-start | bytes 49156
  2.8 19.5 %copy-start.4 = (s32[8,4]{0,1:T(4,128)S(1)}, s32[8,4]{0,1:T(4,128)}, u32[]{:S(2)}) copy-start(s32[8,4]{0,1:T(4,128)} %param.11) | copy-start | bytes 388
  2.8 19.6 %copy-start.5 = (bf16[4,4,64,64]{3,2,1,0:T(8,128)(2,1)S(1)}, bf16[4,4,64,64]{3,2,1,0:T(8,128)(2,1)}, u32[]{:S(2)}) copy-start(bf16[4,4,64,64]{3,2,1,0:T(8,128)(2,1)} %param.8) | copy-start | bytes 393220
  6.5 106.6 %all-to-all-start = ((bf16[32,64,1024]{2,1,0:T(8,128)(2,1)}), bf16[32,64,1024]{2,1,0:T(8,128)(2,1)}, u32[]{:S(2)}, u32[]{:S(2)}) async-start(bf16[32,64,1024]{2,1,0:T(8,128)(2,1)} %bitcast_convert_fusion), calls=%async_computation | async-start | bytes 8388608 | tf_op jit(solution)/shard_map/all_to_all | solution.py:29
  142.8 86.6 %copy-start.1 = (bf16[4,64,1024]{2,1,0:T(8,128)(2,1)S(1)}, bf16[4,64,1024]{2,1,0:T(8,128)(2,1)}, u32[]{:S(2)}) copy-start(bf16[4,64,1024]{2,1,0:T(8,128)(2,1)} %param.6) | copy-start | bytes 1572868

commit v2 on v1

--- a/solution.py
+++ b/solution.py
@@ -2,6 +2,9 @@
 import jax.numpy as jnp
 from jax import lax
 from jax.sharding import PartitionSpec as P
+
+
+CHUNKS = 4
 
 
 def body(wavefunction, left_env, right_env, local_ops, dest_sector, right_bond):
@@ -26,9 +29,6 @@
     outgoing = jnp.einsum(
         "kisj,sjx->kix", chosen_left, wavefunction, preferred_element_type=f32
     ).astype(bf16)
-    incoming = lax.all_to_all(outgoing, "sec", 0, 0, tiled=True)
-    incoming = incoming.reshape(sec_count, rows, physical, rows)
-
     grid = dest_sector.reshape(left_count, sec_count, sec_blocks)
     mine = (grid // sec_blocks) == own_sec
     bond_hot = jnp.sum(mine, axis=2).T.astype(bf16)
@@ -47,17 +47,36 @@
     item_env = jnp.einsum(
         "itbd,bdmr->itmr", env_hot, right_env, preferred_element_type=f32
     ).astype(bf16)
-    mixed = jnp.einsum(
-        "itpq,ilqr->itlpr", item_ops, incoming, preferred_element_type=f32
-    ).astype(bf16)
-    accum = jnp.einsum("itlpr,itmr->ilpm", mixed, item_env, preferred_element_type=f32)
-    partial_value = jnp.einsum(
-        "id,ilpm->dlpm",
-        dest_hot.astype(f32),
-        accum,
-        precision=lax.Precision.HIGHEST,
-        preferred_element_type=f32,
-    )
+
+    chunk = rows // CHUNKS
+    def process(received):
+        incoming = received.reshape(sec_count, chunk, physical, rows)
+        mixed = jnp.einsum(
+            "itpq,ilqr->itlpr", item_ops, incoming, preferred_element_type=f32
+        ).astype(bf16)
+        accum = jnp.einsum("itlpr,itmr->ilpm", mixed, item_env, preferred_element_type=f32)
+        return jnp.stack(
+            [
+                jnp.sum(jnp.where(dest_hot[:, d, None, None, None], accum, 0.0), axis=0)
+                for d in range(sec_blocks)
+            ]
+        )
+
+    def send(c):
+        return lax.all_to_all(outgoing[:, c * chunk:(c + 1) * chunk], "sec", 0, 0, tiled=True)
+
+    received = send(0)
+    parts = []
+    for c in range(CHUNKS):
+        upcoming = None
+        if c + 1 < CHUNKS:
+            piece = outgoing[:, (c + 1) * chunk:(c + 2) * chunk]
+            if parts:
+                piece, parts[-1] = lax.optimization_barrier((piece, parts[-1]))
+            upcoming = lax.all_to_all(piece, "sec", 0, 0, tiled=True)
+        parts.append(process(received))
+        received = upcoming
+    partial_value = jnp.concatenate(parts, axis=1)
     share = rows // op_count
     pieces = partial_value.astype(bf16).reshape(sec_blocks, op_count, share, width)
     pieces = pieces.transpose(1, 0, 2, 3)

time: 230 us -> 208 us (0.904)
  matrix products: 80 us -> 41 us
  waiting for transfers between devices: 89.9 us -> 57 us
  blocking collectives: 29.6 us -> 62.2 us
  starting transfers between devices: 14 us -> 31.1 us
    dot_general x3 -> x4, matrix products: 73.1 us -> 33.9 us  [process(): jnp.einsum('itlpr,itmr->ilpm', mixed, item_env, preferred_element_type=f32)]
    all_to_all x0 -> x1, blocking collectives: none -> 33 us  [body(): upcoming = lax.all_to_all(piece, 'sec', 0, 0, tiled=True)]
    all_to_all x1 -> x3, waiting for transfers between devices: 89.9 us -> 57 us  [the longest x2 34.1 us: body(): upcoming = lax.all_to_all(piece, 'sec', 0, 0, tiled=True)]
    all_to_all x1 -> x3, starting transfers between devices: 14 us -> 31.1 us  [the longest x2 17.2 us: body(): upcoming = lax.all_to_all(piece, 'sec', 0, 0, tiled=True)]
    reshape x2 -> x4, local copies, waits for them, and re-layouts: 12.2 us -> 9.33 us  [process(): incoming = received.reshape(sec_count, chunk, physical, rows)]
    slice x0 -> x1, local copies, waits for them, and re-layouts: none -> 2.32 us  [send(): outgoing[:, c * chunk:(c + 1) * chunk]]
  transfers between devices with their start and end apart: 1 -> 3, of which waited for: 1 -> 3; matrix products, arithmetic and copies ran while one was open for 1% -> 8% of each run, Pallas kernels for 0% -> 0%
where the time goes in v2:
time: 208 us
  blocking collectives  62.2 us (30%)
  waiting for transfers between devices  57 us (27%)
  matrix products  41 us (20%)
  starting transfers between devices  31.1 us (15%)
  local copies, waits for them, and re-layouts  13.7 us (7%)
  other arithmetic  2.4 us (1%)
    all_to_all x2, waiting for transfers between devices, body(): upcoming = lax.all_to_all(piece, 'sec', 0, 0, tiled=True)  34.1 us
    dot_general x4, matrix products, process(): jnp.einsum('itlpr,itmr->ilpm', mixed, item_env, preferred_element_type=f32)  33.9 us
    all_to_all x1, blocking collectives, body(): upcoming = lax.all_to_all(piece, 'sec', 0, 0, tiled=True)  33 us
    all_to_all x1, blocking collectives, body(): gathered = lax.all_to_all(pieces, 'op', 0, 0, tiled=True)  29.2 us
    all_to_all x1, waiting for transfers between devices, send(): lax.all_to_all(outgoing[:, c * chunk:(c + 1) * chunk], 'sec', 0, 0, tiled...  22.9 us
    all_to_all x2, starting transfers between devices, body(): upcoming = lax.all_to_all(piece, 'sec', 0, 0, tiled=True)  17.2 us
    all_to_all x1, starting transfers between devices, send(): lax.all_to_all(outgoing[:, c * chunk:(c + 1) * chunk], 'sec', 0, 0, tiled...  13.9 us
    reshape x4, local copies, waits for them, and re-layouts, process(): incoming = received.reshape(sec_count, chunk, physical, rows)  9.33 us
  transfers between devices with their start and end apart: 3, of which 3 were waited for; matrix products, arithmetic and copies ran while one was open for 8% of the time, Pallas kernels for 0%

profile of v2, /device:TPU:1, one launch (start us, length us, event | category | flops | bytes accessed | tf_op | source)
XLA Modules:
  0.0 207.6 jit_solution(12181141129141646006)
XLA Ops:
  0.0 0.0 copy-start
  0.0 0.8 add_select_fusion.3
  0.8 0.1 copy.35
  0.9 1.9 convert_bitcast_fusion
  2.8 0.0 copy-done
  2.8 1.7 bitcast_convert_fusion
  4.5 2.3 %fusion.77 = (bf16[32,16,1024]{2,1,0:T(8,128)(2,1)}, bf16[32,16,1024]{2,1,0:T(8,128)(2,1)}, bf16[32,16,1024]{2,1,0:T(8,128)(2,1)}, bf16[32,16,1024]{2,1,0:T(8,128)(2,1)}) fusion(bf16[32,64,1024]{2,1,0:T(8,128)(2,1)S(1)} %bitcast_convert_fusion), kind=kLoop, calls=%fused_computation.124 | loop fusion | bytes 8388608 | tf_op jit(solution)/shard_map/slice | solution.py:66
  6.8 0.0 copy-start.7
  6.8 0.0 copy-start.4
  6.8 13.9 %all-to-all-start = ((bf16[32,16,1024]{2,1,0:T(8,128)(2,1)}), bf16[32,16,1024]{2,1,0:T(8,128)(2,1)S(1)}, u32[]{:S(2)}, u32[]{:S(2)}) async-start(bf16[32,16,1024]{2,1,0:T(8,128)(2,1)} %get-tuple-element.33), calls=%async_computation | async-start | bytes 2097152 | tf_op jit(solution)/shard_map/all_to_all | solution.py:66
  20.7 0.0 copy-done.7
  20.7 0.0 copy-start.8
  20.7 0.1 copy.38
  20.8 0.1 reduce_sum.182
  21.0 0.1 reduce_sum.183
  21.1 0.1 convert_reduce_fusion
  21.2 0.0 copy-done.4
  21.2 0.3 fusion.50
  21.5 0.9 copy.55
  22.4 0.0 copy-start.2
  22.4 22.9 %all-to-all-done = bf16[32,16,1024]{2,1,0:T(8,128)(2,1)S(1)} async-done(((bf16[32,16,1024]{2,1,0:T(8,128)(2,1)}), bf16[32,16,1024]{2,1,0:T(8,128)(2,1)S(1)}, u32[]{:S(2)}, u32[]{:S(2)}) %all-to-all-start) | async-done | bytes 1048608 | tf_op jit(solution)/shard_map/all_to_all | solution.py:66
  45.3 8.6 %all-to-all-start.1 = ((bf16[32,16,1024]{2,1,0:T(8,128)(2,1)}), bf16[32,16,1024]{2,1,0:T(8,128)(2,1)S(1)}, u32[]{:S(2)}, u32[]{:S(2)}) async-start(bf16[32,16,1024]{2,1,0:T(8,128)(2,1)} %get-tuple-element.34), calls=%async_computation.1 | async-start | bytes 2097152 | tf_op jit(solution)/shard_map/all_to_all | solution.py:76
  53.9 0.0 copy-done.8
  54.0 0.1 convolution_convert_fusion.1
  54.1 3.1 %fusion.45 = bf16[32,4,64,64,1]{3,0,2,1,4:T(8,128)(2,1)} fusion(bf16[4,4,64,64]{3,2,1,0:T(8,128)(2,1)} %param.8, pred[32,4]{0,1:T(4,128)(4,1)S(1)} %iota_compare_fusion.2, pred[32,4,4]{0,2,1:T(4,128)(4,1)S(1)} %iota_compare_fusion.1), kind=kOutput, calls=%fused_computation.56 | convolution fusion | flops 17303552 | bytes 1180288 | tf_op jit(solution)/shard_map/itbd,bdmr->itmr/dot_general | solution.py:47
  57.2 2.4 %reshape.57 = bf16[32,16,16,64,1]{3,2,1,0,4:T(8,128)(2,1)} reshape(bf16[32,16,1024]{2,1,0:T(8,128)(2,1)S(1)} %all-to-all-done) | data formatting | bytes 2097152 | tf_op jit(solution)/shard_map/reshape | solution.py:53
  59.6 7.2 %fusion.32 = (bf16[16,16,64]{2,1,0:T(8,128)(2,1)S(1)}, bf16[16,16,64]{2,1,0:T(8,128)(2,1)S(1)}, bf16[16,16,64]{2,1,0:T(8,128)(2,1)S(1)}, bf16[16,16,64]{2,1,0:T(8,128)(2,1)S(1)}) fusion(pred[32]{0:T(512)(128)(4,1)S(1)} %get-tuple-element.40, pred[32]{0:T(512)(128)(4,1)S(1)} %get-tuple-element.39, pred[32]{0:T(512)(128)(4,1)S(1)} %get-tuple-element.38, ...), kind=kOutput, calls=%fused_computation.45 | convolution fusion | flops 341770240 | bytes 2293888 | tf_op jit(solution)/shard_map/itlpr,itmr->ilpm/dot_general | solution.py:57
  66.8 0.1 pad_maximum_fusion
  66.9 11.8 %all-to-all-done.1 = bf16[32,16,1024]{2,1,0:T(8,128)(2,1)S(1)} async-done(((bf16[32,16,1024]{2,1,0:T(8,128)(2,1)}), bf16[32,16,1024]{2,1,0:T(8,128)(2,1)S(1)}, u32[]{:S(2)}, u32[]{:S(2)}) %all-to-all-start.1) | async-done | bytes 1048608 | tf_op jit(solution)/shard_map/all_to_all | solution.py:76
  78.7 8.6 %all-to-all-start.2 = ((bf16[32,16,1024]{2,1,0:T(8,128)(2,1)}), bf16[32,16,1024]{2,1,0:T(8,128)(2,1)S(1)}, u32[]{:S(2)}, u32[]{:S(2)}) async-start(bf16[32,16,1024]{2,1,0:T(8,128)(2,1)} %get-tuple-element.11), calls=%async_computation.2 | async-start | bytes 2097152 | tf_op jit(solution)/shard_map/all_to_all | solution.py:76
  87.3 2.3 %reshape.64 = bf16[32,16,16,64,1]{3,2,1,0,4:T(8,128)(2,1)} reshape(bf16[32,16,1024]{2,1,0:T(8,128)(2,1)S(1)} %all-to-all-done.1) | data formatting | bytes 2097152 | tf_op jit(solution)/shard_map/reshape | solution.py:53
  89.6 22.3 %all-to-all-done.2 = bf16[32,16,1024]{2,1,0:T(8,128)(2,1)S(1)} async-done(((bf16[32,16,1024]{2,1,0:T(8,128)(2,1)}), bf16[32,16,1024]{2,1,0:T(8,128)(2,1)S(1)}, u32[]{:S(2)}, u32[]{:S(2)}) %all-to-all-start.2) | async-done | bytes 1048608 | tf_op jit(solution)/shard_map/all_to_all | solution.py:76
  111.9 2.3 %reshape.68 = bf16[32,16,16,64,1]{3,2,1,0,4:T(8,128)(2,1)} reshape(bf16[32,16,1024]{2,1,0:T(8,128)(2,1)S(1)} %all-to-all-done.2) | data formatting | bytes 2097152 | tf_op jit(solution)/shard_map/reshape | solution.py:53
  114.2 8.8 %fusion.2 = f32[32,16,16,64,1]{3,2,4,1,0:T(8,128)} fusion(bf16[32,4,16,16,1]{3,2,1,4,0:T(8,128)(2,1)S(1)} %copy.55, bf16[32,16,16,64,1]{3,2,1,0,4:T(8,128)(2,1)} %reshape.68, bf16[32,4,64,64,1]{3,0,2,1,4:T(8,128)(2,1)} %fusion.45), kind=kOutput, calls=%fused_computation.2 | convolution fusion | flops 337641472 | bytes 4259840 | tf_op jit(solution)/shard_map/itlpr,itmr->ilpm/dot_general | solution.py:57
  123.0 0.0 copy-done.2
  123.0 0.0 copy-start.1
  123.0 10.6 %fusion.28 = (bf16[16,16,64]{2,1,0:T(8,128)(2,1)S(1)}, bf16[16,16,64]{2,1,0:T(8,128)(2,1)S(1)}, bf16[16,16,64]{2,1,0:T(8,128)(2,1)S(1)}, bf16[16,16,64]{2,1,0:T(...) fusion(pred[32]{0:T(512)(128)(4,1)S(1)} %get-tuple-element.40, ...), kind=kOutput, calls=%fused_computation.37 | convolution fusion | flops 345899008 | bytes 4522112 | tf_op jit(solution)/shard_map/itlpr,itmr->ilpm/dot_general | solution.py:57
  133.6 0.1 pad_maximum_fusion.1
  133.7 0.0 copy-done.1
  133.7 33.0 %all_to_all.25 = bf16[32,16,1024]{2,1,0:T(8,128)(2,1)S(1)} all-to-all(bf16[32,16,1024]{2,1,0:T(8,128)(2,1)S(1)} %copy-done.1), channel_id=1, replica_groups=mesh['op'=16,'sec'=32] {'sec'}, dimensions={0} | all-to-all | bytes 2097152 | tf_op jit(solution)/shard_map/all_to_all | solution.py:76
  166.7 0.0 copy-start.3
  166.7 2.4 %reshape.72 = bf16[32,16,16,64,1]{3,2,1,0,4:T(8,128)(2,1)} reshape(bf16[32,16,1024]{2,1,0:T(8,128)(2,1)S(1)} %all_to_all.25) | data formatting | bytes 2097152 | tf_op jit(solution)/shard_map/reshape | solution.py:53
  169.1 0.0 copy-done.3
  169.1 0.0 copy-start.5
  169.1 0.0 copy-start.6
  169.1 7.3 %fusion.20 = (bf16[16,16,64]{2,1,0:T(8,128)(2,1)S(1)}, bf16[16,16,64]{2,1,0:T(8,128)(2,1)S(1)}, bf16[16,16,64]{2,1,0:T(8,128)(2,1)S(1)}, bf16[16,16,64]{2,1,0:T(8,128)(2,1)S(1)}) fusion(pred[32]{0:T(512)(128)(4,1)S(1)} %get-tuple-element.40, pred[32]{0:T(512)(128)(4,1)S(1)} %get-tuple-element.39, pred[32]{0:T(512)(128)(4,1)S(1)} %get-tuple-element.38, ...), kind=kOutput, calls=%fused_computation.21 | convolution fusion | flops 341770240 | bytes 2293888 | tf_op jit(solution)/shard_map/itlpr,itmr->ilpm/dot_general | solution.py:57
  176.3 0.0 copy-done.5
  176.3 0.0 copy-done.6
  176.4 0.3 maximum_maximum_fusion
  176.7 0.6 convert_element_type.79
  177.3 0.2 copy.50
  177.5 29.2 %all_to_all.26 = bf16[16,4,4,1024]{3,2,1,0:T(4,128)(2,1)S(1)} all-to-all(bf16[16,4,4,1024]{3,2,1,0:T(4,128)(2,1)S(1)} %copy.50), channel_id=1, replica_groups=mesh['op'=16,'sec'=32] {'op'}, dimensions={0} | all-to-all | bytes 1048576 | tf_op jit(solution)/shard_map/all_to_all | solution.py:83
  206.8 0.8 reduce_sum.201
  (4 shorter events, 0.1 us)
Async XLA Ops:
  0.0 2.8 %copy-start = (bf16[4,64,1024]{2,1,0:T(8,128)(2,1)S(1)}, bf16[4,64,1024]{2,1,0:T(8,128)(2,1)}, u32[]{:S(2)}) copy-start(bf16[4,64,1024]{2,1,0:T(8,128)(2,1)} %param.6) | copy-start | bytes 1572868
  6.8 13.9 %copy-start.7 = (s32[8,128]{1,0:T(8,128)S(1)}, s32[8,128]{1,0:T(8,128)}, u32[]{:S(2)}) copy-start(s32[8,128]{1,0:T(8,128)} %param.10) | copy-start | bytes 12292
  6.8 14.4 %copy-start.4 = (bf16[8,4,16,16]{3,2,1,0:T(8,128)(2,1)S(1)}, bf16[8,4,16,16]{3,2,1,0:T(8,128)(2,1)}, u32[]{:S(2)}) copy-start(bf16[8,4,16,16]{3,2,1,0:T(8,128)(2,1)} %param.9) | copy-start | bytes 49156
  6.8 38.5 %all-to-all-start = ((bf16[32,16,1024]{2,1,0:T(8,128)(2,1)}), bf16[32,16,1024]{2,1,0:T(8,128)(2,1)S(1)}, u32[]{:S(2)}, u32[]{:S(2)}) async-start(bf16[32,16,1024]{2,1,0:T(8,128)(2,1)} %get-tuple-element.33), calls=%async_computation | async-start | bytes 2097152 | tf_op jit(solution)/shard_map/all_to_all | solution.py:66
  20.7 33.2 %copy-start.8 = (s32[8,4]{0,1:T(4,128)S(1)}, s32[8,4]{0,1:T(4,128)}, u32[]{:S(2)}) copy-start(s32[8,4]{0,1:T(4,128)} %param.11) | copy-start | bytes 388
  22.4 100.6 %copy-start.2 = (bf16[32,4,16,16,1]{3,2,1,4,0:T(8,128)(2,1)}, bf16[32,4,16,16,1]{3,2,1,4,0:T(8,128)(2,1)S(1)}, u32[]{:S(2)}) copy-start(bf16[32,4,16,16,1]{3,2,1,4,0:T(8,128)(2,1)S(1)} %copy.55) | copy-start | bytes 196612
  45.3 33.4 %all-to-all-start.1 = ((bf16[32,16,1024]{2,1,0:T(8,128)(2,1)}), bf16[32,16,1024]{2,1,0:T(8,128)(2,1)S(1)}, u32[]{:S(2)}, u32[]{:S(2)}) async-start(bf16[32,16,1024]{2,1,0:T(8,128)(2,1)} %get-tuple-element.34), calls=%async_computation.1 | async-start | bytes 2097152 | tf_op jit(solution)/shard_map/all_to_all | solution.py:76
  78.7 33.2 %all-to-all-start.2 = ((bf16[32,16,1024]{2,1,0:T(8,128)(2,1)}), bf16[32,16,1024]{2,1,0:T(8,128)(2,1)S(1)}, u32[]{:S(2)}, u32[]{:S(2)}) async-start(bf16[32,16,1024]{2,1,0:T(8,128)(2,1)} %get-tuple-element.11), calls=%async_computation.2 | async-start | bytes 2097152 | tf_op jit(solution)/shard_map/all_to_all | solution.py:76
  123.0 10.6 %copy-start.1 = (bf16[32,16,1024]{2,1,0:T(8,128)(2,1)S(1)}, bf16[32,16,1024]{2,1,0:T(8,128)(2,1)}, u32[]{:S(2)}) copy-start(bf16[32,16,1024]{2,1,0:T(8,128)(2,1)} %get-tuple-element.12) | copy-start | bytes 3145732
  166.7 2.4 %copy-start.3 = (bf16[32,4,16,16,1]{3,2,1,4,0:T(8,128)(2,1)S(1)}, bf16[32,4,16,16,1]{3,2,1,4,0:T(8,128)(2,1)}, u32[]{:S(2)}) copy-start(bf16[32,4,16,16,1]{3,2,1,4,0:T(8,128)(2,1)} %copy-done.2) | copy-start | bytes 196612
  169.1 7.3 %copy-start.5 = (bf16[16,16,64]{2,1,0:T(8,128)(2,1)S(1)}, bf16[16,16,64]{2,1,0:T(8,128)(2,1)}, u32[]{:S(2)}) copy-start(bf16[16,16,64]{2,1,0:T(8,128)(2,1)} %get-tuple-element.31) | copy-start | bytes 98308
  169.1 7.3 %copy-start.6 = (bf16[16,16,64]{2,1,0:T(8,128)(2,1)S(1)}, bf16[16,16,64]{2,1,0:T(8,128)(2,1)}, u32[]{:S(2)}) copy-start(bf16[16,16,64]{2,1,0:T(8,128)(2,1)} %get-tuple-element.32) | copy-start | bytes 98308

commit v3 on v2

--- a/solution.py
+++ b/solution.py
@@ -4,7 +4,7 @@
 from jax.sharding import PartitionSpec as P
 
 
-CHUNKS = 4
+CHUNKS = 2
 
 
 def body(wavefunction, left_env, right_env, local_ops, dest_sector, right_bond):

time: 208 us -> 214 us (1.029)
  matrix products: 41 us -> 72.5 us
  waiting for transfers between devices: 57 us -> 27.7 us
  blocking collectives: 62.2 us -> 87.5 us
  starting transfers between devices: 31.1 us -> 8.76 us
    all_to_all x1, blocking collectives: 33 us -> 60.9 us  [send(): lax.all_to_all(outgoing[:, c * chunk:(c + 1) * chunk], 'sec', 0, 0, tiled...]
    all_to_all x1 -> x0, waiting for transfers between devices: 22.9 us -> none  [send(): lax.all_to_all(outgoing[:, c * chunk:(c + 1) * chunk], 'sec', 0, 0, tiled...]
    dot_general x0 -> x2, matrix products: none -> 20.9 us  [process(): jnp.einsum('itpq,ilqr->itlpr', item_ops, incoming, preferred_element_type...]
    all_to_all x1 -> x0, starting transfers between devices: 13.9 us -> none  [send(): lax.all_to_all(outgoing[:, c * chunk:(c + 1) * chunk], 'sec', 0, 0, tiled...]
    dot_general x4 -> x2, matrix products: 33.9 us -> 45.5 us  [process(): jnp.einsum('itlpr,itmr->ilpm', mixed, item_env, preferred_element_type=f32)]
    all_to_all x2 -> x1, starting transfers between devices: 17.2 us -> 8.76 us  [body(): upcoming = lax.all_to_all(piece, 'sec', 0, 0, tiled=True)]
    all_to_all x2 -> x1, waiting for transfers between devices: 34.1 us -> 27.7 us  [body(): upcoming = lax.all_to_all(piece, 'sec', 0, 0, tiled=True)]
    all_to_all x1, blocking collectives: 29.2 us -> 26.6 us  [body(): gathered = lax.all_to_all(pieces, 'op', 0, 0, tiled=True)]
  transfers between devices with their start and end apart: 3 -> 1, of which waited for: 3 -> 1; matrix products, arithmetic and copies ran while one was open for 8% -> 10% of each run, Pallas kernels for 0% -> 0%
where the time goes in v3:
time: 214 us
  blocking collectives  87.5 us (41%)
  matrix products  72.5 us (34%)
  waiting for transfers between devices  27.7 us (13%)
  local copies, waits for them, and re-layouts  15.1 us (7%)
  starting transfers between devices  8.76 us (4%)
  other arithmetic  2.23 us (1%)
    all_to_all x1, blocking collectives, send(): lax.all_to_all(outgoing[:, c * chunk:(c + 1) * chunk], 'sec', 0, 0, tiled...  60.9 us
    dot_general x2, matrix products, process(): jnp.einsum('itlpr,itmr->ilpm', mixed, item_env, preferred_element_type=f32)  45.5 us
    all_to_all x1, waiting for transfers between devices, body(): upcoming = lax.all_to_all(piece, 'sec', 0, 0, tiled=True)  27.7 us
    all_to_all x1, blocking collectives, body(): gathered = lax.all_to_all(pieces, 'op', 0, 0, tiled=True)  26.6 us
    dot_general x2, matrix products, process(): jnp.einsum('itpq,ilqr->itlpr', item_ops, incoming, preferred_element_type...  20.9 us
    reshape x2, local copies, waits for them, and re-layouts, process(): incoming = received.reshape(sec_count, chunk, physical, rows)  10.4 us
    all_to_all x1, starting transfers between devices, body(): upcoming = lax.all_to_all(piece, 'sec', 0, 0, tiled=True)  8.76 us
  transfers between devices with their start and end apart: 1, of which 1 were waited for; matrix products, arithmetic and copies ran while one was open for 10% of the time, Pallas kernels for 0%

profile of v3, /device:TPU:1, one launch (start us, length us, event | category | flops | bytes accessed | tf_op | source)
XLA Modules:
  0.0 214.0 jit_solution(6010908444750796109)
XLA Ops:
  0.0 0.0 copy-start
  0.0 0.8 add_select_fusion.1
  0.8 0.1 copy.29
  0.9 1.9 convert_bitcast_fusion.2
  2.8 0.0 copy-done
  2.8 1.7 bitcast_convert_fusion
  4.5 1.9 fusion.45
  6.4 0.0 copy-start.3
  6.4 0.0 copy-start.2
  6.4 0.0 copy-start.4
  6.5 0.0 copy-start.5
  6.5 60.9 %all_to_all.15 = bf16[32,32,1024]{2,1,0:T(8,128)(2,1)} all-to-all(bf16[32,32,1024]{2,1,0:T(8,128)(2,1)S(1)} %get-tuple-element.17), channel_id=1, replica_groups=mesh['op'=16,'sec'=32] {'sec'}, dimensions={0} | all-to-all | bytes 4194304 | tf_op jit(solution)/shard_map/all_to_all | solution.py:66
  67.3 8.8 %all-to-all-start.1 = ((bf16[32,32,1024]{2,1,0:T(8,128)(2,1)}), bf16[32,32,1024]{2,1,0:T(8,128)(2,1)S(1)}, u32[]{:S(2)}, u32[]{:S(2)}) async-start(bf16[32,32,1024]{2,1,0:T(8,128)(2,1)} %get-tuple-element.18), calls=%async_computation.1 | async-start | bytes 4194304 | tf_op jit(solution)/shard_map/all_to_all | solution.py:76
  76.1 0.0 copy-done.3
  76.1 0.1 copy.32
  76.2 0.1 convert_reduce_fusion
  76.3 0.0 copy-done.2
  76.3 0.3 fusion.18
  76.6 0.9 copy.48
  77.6 0.1 reduce_sum.110
  77.7 0.1 reduce_sum.111
  77.8 0.0 copy-done.4
  77.8 0.1 convolution_convert_fusion.1
  78.0 0.0 copy-done.5
  78.0 2.2 %fusion.17 = bf16[32,4,64,64,1]{3,0,2,1,4:T(8,128)(2,1)} fusion(bf16[4,4,64,64]{3,2,1,0:T(8,128)(2,1)S(1)} %copy-done.5, pred[32,4]{0,1:T(4,128)(4,1)S(1)} %iota_compare_fusion.2, pred[32,4,4]{0,2,1:T(4,128)(4,1)S(1)} %iota_compare_fusion.1), kind=kOutput, calls=%fused_computation.30 | convolution fusion | flops 17303552 | bytes 1180288 | tf_op jit(solution)/shard_map/itbd,bdmr->itmr/dot_general | solution.py:47
  80.2 6.4 %reshape.49 = bf16[32,32,16,64,1]{3,2,1,0,4:T(8,128)(2,1)} reshape(bf16[32,32,1024]{2,1,0:T(8,128)(2,1)} %all_to_all.15) | data formatting | bytes 4194304 | tf_op jit(solution)/shard_map/reshape | solution.py:53
  86.6 10.3 %convert_bitcast_fusion.1 = bf16[32,4,32,16,64]{4,3,1,2,0:T(8,128)(2,1)} fusion(bf16[32,4,16,16,1]{3,2,1,4,0:T(8,128)(2,1)S(1)} %copy.48, bf16[32,32,16,64,1]{3,2,1,0,4:T(8,128)(2,1)} %reshape.49), kind=kOutput, calls=%fused_computation.5 | convolution fusion | flops 138412032 | bytes 10551296 | tf_op jit(solution)/shard_map/itpq,ilqr->itlpr/dot_general | solution.py:54
  96.9 27.7 %all-to-all-done.1 = bf16[32,32,1024]{2,1,0:T(8,128)(2,1)S(1)} async-done(((bf16[32,32,1024]{2,1,0:T(8,128)(2,1)}), bf16[32,32,1024]{2,1,0:T(8,128)(2,1)S(1)}, u32[]{:S(2)}, u32[]{:S(2)}) %all-to-all-start.1) | async-done | bytes 2097184 | tf_op jit(solution)/shard_map/all_to_all | solution.py:76
  124.6 4.0 %reshape.56 = bf16[32,32,16,64,1]{3,2,1,0,4:T(8,128)(2,1)} reshape(bf16[32,32,1024]{2,1,0:T(8,128)(2,1)S(1)} %all-to-all-done.1) | data formatting | bytes 4194304 | tf_op jit(solution)/shard_map/reshape | solution.py:53
  128.6 0.0 copy-start.6
  128.6 10.5 %convert_bitcast_fusion = bf16[32,4,32,16,64]{4,3,1,2,0:T(8,128)(2,1)} fusion(bf16[32,4,16,16,1]{3,2,1,4,0:T(8,128)(2,1)S(1)} %copy.48, bf16[32,32,16,64,1]{3,2,1,0,4:T(8,128)(2,1)} %reshape.56), kind=kOutput, calls=%fused_computation.4 | convolution fusion | flops 138412032 | bytes 10551296 | tf_op jit(solution)/shard_map/itpq,ilqr->itlpr/dot_general | solution.py:54
  139.2 0.0 copy-done.6
  139.2 19.8 %fusion.2 = f32[32,32,16,64,1]{3,1,4,2,0:T(8,128)} fusion(bf16[32,4,32,16,64]{4,3,1,2,0:T(8,128)(2,1)} %convert_bitcast_fusion.1, bf16[32,4,64,64,1]{3,0,2,1,4:T(8,128)(2,1)S(1)} %copy-done.6), kind=kOutput, calls=%fused_computation.2 | convolution fusion | flops 536870912 | bytes 13631488 | tf_op jit(solution)/shard_map/itlpr,itmr->ilpm/dot_general | solution.py:57
  158.9 25.7 %fusion.4 = (bf16[32,16,64]{2,0,1:T(8,128)(2,1)S(1)}, bf16[32,16,64]{2,0,1:T(8,128)(2,1)S(1)}, bf16[32,16,64]{2,0,1:T(8,128)(2,1)S(1)}, bf16[32,16,64]{2,0,1:T(8...) fusion(pred[32]{0:T(512)(128)(4,1)S(1)} %get-tuple-element.22, ...), kind=kOutput, calls=%fused_computation.10 | convolution fusion | flops 553385984 | bytes 14155904 | tf_op jit(solution)/shard_map/itlpr,itmr->ilpm/dot_general | solution.py:57
  184.6 0.0 copy-start.1
  184.6 0.3 maximum_maximum_fusion
  184.9 0.7 copy.42
  185.6 0.6 convert_element_type.63
  186.3 0.2 copy.43
  186.5 26.6 %all_to_all.16 = bf16[16,4,4,1024]{3,2,1,0:T(4,128)(2,1)S(1)} all-to-all(bf16[16,4,4,1024]{3,2,1,0:T(4,128)(2,1)S(1)} %copy.43), channel_id=1, replica_groups=mesh['op'=16,'sec'=32] {'op'}, dimensions={0} | all-to-all | bytes 1048576 | tf_op jit(solution)/shard_map/all_to_all | solution.py:83
  213.1 0.8 reduce_sum.121
  214.0 0.0 copy-done.1
  (4 shorter events, 0.1 us)
Async XLA Ops:
  0.0 2.8 %copy-start = (bf16[4,64,1024]{2,1,0:T(8,128)(2,1)S(1)}, bf16[4,64,1024]{2,1,0:T(8,128)(2,1)}, u32[]{:S(2)}) copy-start(bf16[4,64,1024]{2,1,0:T(8,128)(2,1)} %param.6) | copy-start | bytes 1572868
  6.4 69.7 %copy-start.3 = (s32[8,128]{1,0:T(8,128)S(1)}, s32[8,128]{1,0:T(8,128)}, u32[]{:S(2)}) copy-start(s32[8,128]{1,0:T(8,128)} %param.10) | copy-start | bytes 12292
  6.4 69.9 %copy-start.2 = (bf16[8,4,16,16]{3,2,1,0:T(8,128)(2,1)S(1)}, bf16[8,4,16,16]{3,2,1,0:T(8,128)(2,1)}, u32[]{:S(2)}) copy-start(bf16[8,4,16,16]{3,2,1,0:T(8,128)(2,1)} %param.9) | copy-start | bytes 49156
  6.4 71.4 %copy-start.4 = (s32[8,4]{0,1:T(4,128)S(1)}, s32[8,4]{0,1:T(4,128)}, u32[]{:S(2)}) copy-start(s32[8,4]{0,1:T(4,128)} %param.11) | copy-start | bytes 388
  6.5 71.5 %copy-start.5 = (bf16[4,4,64,64]{3,2,1,0:T(8,128)(2,1)S(1)}, bf16[4,4,64,64]{3,2,1,0:T(8,128)(2,1)}, u32[]{:S(2)}) copy-start(bf16[4,4,64,64]{3,2,1,0:T(8,128)(2,1)} %param.8) | copy-start | bytes 393220
  67.3 57.3 %all-to-all-start.1 = ((bf16[32,32,1024]{2,1,0:T(8,128)(2,1)}), bf16[32,32,1024]{2,1,0:T(8,128)(2,1)S(1)}, u32[]{:S(2)}, u32[]{:S(2)}) async-start(bf16[32,32,1024]{2,1,0:T(8,128)(2,1)} %get-tuple-element.18), calls=%async_computation.1 | async-start | bytes 4194304 | tf_op jit(solution)/shard_map/all_to_all | solution.py:76
  128.6 10.6 %copy-start.6 = (bf16[32,4,64,64,1]{3,0,2,1,4:T(8,128)(2,1)S(1)}, bf16[32,4,64,64,1]{3,0,2,1,4:T(8,128)(2,1)}, u32[]{:S(2)}) copy-start(bf16[32,4,64,64,1]{3,0,2,1,4:T(8,128)(2,1)} %fusion.17) | copy-start | bytes 3145732
  184.6 29.3 %copy-start.1 = (bf16[4,64,1024]{2,1,0:T(8,128)(2,1)S(1)}, bf16[4,64,1024]{2,1,0:T(8,128)(2,1)}, u32[]{:S(2)}) copy-start(bf16[4,64,1024]{2,1,0:T(8,128)(2,1)} %param.6) | copy-start | bytes 1572868

commit v4 on v3

--- a/solution.py
+++ b/solution.py
@@ -48,19 +48,17 @@
         "itbd,bdmr->itmr", env_hot, right_env, preferred_element_type=f32
     ).astype(bf16)
 
+    sector_env = jnp.einsum(
+        "itmr,id->itdmr", item_env, dest_hot.astype(bf16), preferred_element_type=f32
+    ).astype(bf16)
+
     chunk = rows // CHUNKS
     def process(received):
         incoming = received.reshape(sec_count, chunk, physical, rows)
         mixed = jnp.einsum(
             "itpq,ilqr->itlpr", item_ops, incoming, preferred_element_type=f32
         ).astype(bf16)
-        accum = jnp.einsum("itlpr,itmr->ilpm", mixed, item_env, preferred_element_type=f32)
-        return jnp.stack(
-            [
-                jnp.sum(jnp.where(dest_hot[:, d, None, None, None], accum, 0.0), axis=0)
-                for d in range(sec_blocks)
-            ]
-        )
+        return jnp.einsum("itlpr,itdmr->dlpm", mixed, sector_env, preferred_element_type=f32)
 
     def send(c):
         return lax.all_to_all(outgoing[:, c * chunk:(c + 1) * chunk], "sec", 0, 0, tiled=True)

time: 214 us -> 200 us (0.935)
  matrix products: 72.5 us -> 56.7 us
  local copies, waits for them, and re-layouts: 15.1 us -> 19.4 us
  waiting for transfers between devices: 27.7 us -> 24.6 us
    dot_general x2, matrix products: 45.5 us -> 31 us  [process(): jnp.einsum('itlpr,itdmr->dlpm', mixed, sector_env, preferred_element_type...]
    another operation x0 -> x1, local copies, waits for them, and re-layouts: none -> 4.47 us
    all_to_all x1, waiting for transfers between devices: 27.7 us -> 24.6 us  [body(): upcoming = lax.all_to_all(piece, 'sec', 0, 0, tiled=True)]
  transfers between devices with their start and end apart: 1 -> 1, of which waited for: 1 -> 1; matrix products, arithmetic and copies ran while one was open for 10% -> 12% of each run, Pallas kernels for 0% -> 0%
where the time goes in v4:
time: 200 us; the launch traced here: 199 us
  blocking collectives  87.5 us (44%)
  matrix products  56.7 us (28%)
  waiting for transfers between devices  24.6 us (12%)
  local copies, waits for them, and re-layouts  19.4 us (10%)
  starting transfers between devices  8.76 us (4%)
  other arithmetic  2.25 us (1%)
    all_to_all x1, blocking collectives, send(): lax.all_to_all(outgoing[:, c * chunk:(c + 1) * chunk], 'sec', 0, 0, tiled...  60.9 us
    dot_general x2, matrix products, process(): jnp.einsum('itlpr,itdmr->dlpm', mixed, sector_env, preferred_element_type...  31 us
    all_to_all x1, blocking collectives, body(): gathered = lax.all_to_all(pieces, 'op', 0, 0, tiled=True)  26.6 us
    all_to_all x1, waiting for transfers between devices, body(): upcoming = lax.all_to_all(piece, 'sec', 0, 0, tiled=True)  24.6 us
    dot_general x2, matrix products, process(): jnp.einsum('itpq,ilqr->itlpr', item_ops, incoming, preferred_element_type...  20.9 us
    reshape x2, local copies, waits for them, and re-layouts, process(): incoming = received.reshape(sec_count, chunk, physical, rows)  10.3 us
    all_to_all x1, starting transfers between devices, body(): upcoming = lax.all_to_all(piece, 'sec', 0, 0, tiled=True)  8.76 us
    another operation x1, local copies, waits for them, and re-layouts  4.47 us
  transfers between devices with their start and end apart: 1, of which 1 were waited for; matrix products, arithmetic and copies ran while one was open for 12% of the time, Pallas kernels for 0%

profile of v4, /device:TPU:1, one launch (start us, length us, event | category | flops | bytes accessed | tf_op | source)
XLA Modules:
  0.0 199.5 jit_solution(6223533918795626176)
XLA Ops:
  0.0 0.0 copy-start
  0.0 0.8 add_select_fusion.1
  0.8 0.1 copy.18
  0.9 1.9 convert_bitcast_fusion.2
  2.8 0.0 copy-done
  2.8 1.7 bitcast_convert_fusion
  4.5 1.9 fusion.75
  6.4 0.0 copy-start.5
  6.4 0.0 copy-start.4
  6.4 0.0 copy-start.6
  6.4 0.0 copy-start.7
  6.5 60.9 %all_to_all.15 = bf16[32,32,1024]{2,1,0:T(8,128)(2,1)} all-to-all(bf16[32,32,1024]{2,1,0:T(8,128)(2,1)S(1)} %get-tuple-element.5), channel_id=1, replica_groups=mesh['op'=16,'sec'=32] {'sec'}, dimensions={0} | all-to-all | bytes 4194304 | tf_op jit(solution)/shard_map/all_to_all | solution.py:64
  67.3 8.8 %all-to-all-start.1 = ((bf16[32,32,1024]{2,1,0:T(8,128)(2,1)}), bf16[32,32,1024]{2,1,0:T(8,128)(2,1)S(1)}, u32[]{:S(2)}, u32[]{:S(2)}) async-start(bf16[32,32,1024]{2,1,0:T(8,128)(2,1)} %get-tuple-element.6), calls=%async_computation.1 | async-start | bytes 4194304 | tf_op jit(solution)/shard_map/all_to_all | solution.py:74
  76.1 0.0 copy-done.5
  76.1 0.1 copy.15
  76.2 0.1 convert_reduce_fusion
  76.3 0.0 copy-done.4
  76.3 0.3 fusion.47
  76.6 0.9 copy.35
  77.6 0.1 reduce_sum.38
  77.7 0.1 reduce_sum.39
  77.8 0.0 copy-done.6
  77.8 0.1 convolution_convert_fusion.1
  77.9 0.0 copy-done.7
  77.9 0.8 fusion.16
  78.8 4.5 %copy.17 = f32[32,4,64,64]{3,2,1,0:T(8,128)} copy(f32[32,4,64,64]{3,0,2,1:T(8,128)S(1)} %fusion.16) | data formatting | bytes 4194304 | tf_op jit(solution)/shard_map/convert.2
  83.3 6.4 %reshape.48 = bf16[32,32,16,64,1]{3,2,1,0,4:T(8,128)(2,1)} reshape(bf16[32,32,1024]{2,1,0:T(8,128)(2,1)} %all_to_all.15) | data formatting | bytes 4194304 | tf_op jit(solution)/shard_map/reshape | solution.py:57
  89.6 10.3 %convert_bitcast_fusion.1 = bf16[32,4,32,16,64]{4,3,1,2,0:T(8,128)(2,1)} fusion(bf16[32,4,16,16,1]{3,2,1,4,0:T(8,128)(2,1)S(1)} %copy.35, bf16[32,32,16,64,1]{3,2,1,0,4:T(8,128)(2,1)} %reshape.48), kind=kOutput, calls=%fused_computation.7 | convolution fusion | flops 138412032 | bytes 10551296 | tf_op jit(solution)/shard_map/itpq,ilqr->itlpr/dot_general | solution.py:58
  100.0 24.6 %all-to-all-done.1 = bf16[32,32,1024]{2,1,0:T(8,128)(2,1)S(1)} async-done(((bf16[32,32,1024]{2,1,0:T(8,128)(2,1)}), bf16[32,32,1024]{2,1,0:T(8,128)(2,1)S(1)}, u32[]{:S(2)}, u32[]{:S(2)}) %all-to-all-start.1) | async-done | bytes 2097184 | tf_op jit(solution)/shard_map/all_to_all | solution.py:74
  124.6 3.9 %reshape.53 = bf16[32,32,16,64,1]{3,2,1,0,4:T(8,128)(2,1)} reshape(bf16[32,32,1024]{2,1,0:T(8,128)(2,1)S(1)} %all-to-all-done.1) | data formatting | bytes 4194304 | tf_op jit(solution)/shard_map/reshape | solution.py:57
  128.5 0.0 copy-start.3
  128.5 10.5 %convert_bitcast_fusion = bf16[32,4,32,16,64]{4,3,1,2,0:T(8,128)(2,1)} fusion(bf16[32,4,16,16,1]{3,2,1,4,0:T(8,128)(2,1)S(1)} %copy.35, bf16[32,32,16,64,1]{3,2,1,0,4:T(8,128)(2,1)} %reshape.53), kind=kOutput, calls=%fused_computation.6 | convolution fusion | flops 138412032 | bytes 10551296 | tf_op jit(solution)/shard_map/itpq,ilqr->itlpr/dot_general | solution.py:58
  139.1 0.0 copy-done.3
  139.1 0.0 copy-start.2
  139.1 21.7 %fusion.37 = bf16[4,32,16,64]{3,1,2,0:T(8,128)(2,1)S(1)} fusion(bf16[32,4,32,16,64]{4,3,1,2,0:T(8,128)(2,1)} %convert_bitcast_fusion.1, f32[32,4,64,64]{3,2,1,0:T(8,128)S(1)} %copy-done.3, f32[32,4]{0,1:T(4,128)S(1)} %get-tuple-element.7), kind=kOutput, calls=%fused_computation.25 | convolution fusion | flops 2151809024 | bytes 10748416 | tf_op jit(solution)/shard_map/itlpr,itdmr->dlpm/dot_general | solution.py:61
  160.8 0.0 copy-done.2
  160.8 0.0 copy-start.1
  160.8 9.3 %fusion.42 = bf16[4,32,16,64]{3,1,2,0:T(8,128)(2,1)S(1)} fusion(bf16[32,4,32,16,64]{4,3,1,2,0:T(8,128)(2,1)S(1)} %copy-done.2, f32[32,4,64,64]{3,2,1,0:T(8,128)S(1)} %copy-done.3, f32[32,4]{0,1:T(4,128)S(1)} %get-tuple-element.7), kind=kOutput, calls=%fused_computation.26 | convolution fusion | flops 2151809024 | bytes 10748416 | tf_op jit(solution)/shard_map/itlpr,itdmr->dlpm/dot_general | solution.py:61
  170.1 0.3 pad_maximum_fusion
  170.4 0.7 copy.27
  171.1 0.6 convert_element_type.72
  171.7 0.2 copy.28
  172.0 26.6 %all_to_all.16 = bf16[16,4,4,1024]{3,2,1,0:T(4,128)(2,1)S(1)} all-to-all(bf16[16,4,4,1024]{3,2,1,0:T(4,128)(2,1)S(1)} %copy.28), channel_id=1, replica_groups=mesh['op'=16,'sec'=32] {'op'}, dimensions={0} | all-to-all | bytes 1048576 | tf_op jit(solution)/shard_map/all_to_all | solution.py:81
  198.6 0.8 reduce_sum.41
  199.4 0.0 copy-done.1
  (3 shorter events, 0.0 us)
Async XLA Ops:
  0.0 2.8 %copy-start = (bf16[4,64,1024]{2,1,0:T(8,128)(2,1)S(1)}, bf16[4,64,1024]{2,1,0:T(8,128)(2,1)}, u32[]{:S(2)}) copy-start(bf16[4,64,1024]{2,1,0:T(8,128)(2,1)} %param.6) | copy-start | bytes 1572868
  6.4 69.7 %copy-start.5 = (s32[8,128]{1,0:T(8,128)S(1)}, s32[8,128]{1,0:T(8,128)}, u32[]{:S(2)}) copy-start(s32[8,128]{1,0:T(8,128)} %param.10) | copy-start | bytes 12292
  6.4 69.9 %copy-start.4 = (bf16[8,4,16,16]{3,2,1,0:T(8,128)(2,1)S(1)}, bf16[8,4,16,16]{3,2,1,0:T(8,128)(2,1)}, u32[]{:S(2)}) copy-start(bf16[8,4,16,16]{3,2,1,0:T(8,128)(2,1)} %param.9) | copy-start | bytes 49156
  6.4 71.4 %copy-start.6 = (s32[8,4]{0,1:T(4,128)S(1)}, s32[8,4]{0,1:T(4,128)}, u32[]{:S(2)}) copy-start(s32[8,4]{0,1:T(4,128)} %param.11) | copy-start | bytes 388
  6.4 71.5 %copy-start.7 = (bf16[4,4,64,64]{3,2,1,0:T(8,128)(2,1)S(1)}, bf16[4,4,64,64]{3,2,1,0:T(8,128)(2,1)}, u32[]{:S(2)}) copy-start(bf16[4,4,64,64]{3,2,1,0:T(8,128)(2,1)} %param.8) | copy-start | bytes 393220
  67.3 57.3 %all-to-all-start.1 = ((bf16[32,32,1024]{2,1,0:T(8,128)(2,1)}), bf16[32,32,1024]{2,1,0:T(8,128)(2,1)S(1)}, u32[]{:S(2)}, u32[]{:S(2)}) async-start(bf16[32,32,1024]{2,1,0:T(8,128)(2,1)} %get-tuple-element.6), calls=%async_computation.1 | async-start | bytes 4194304 | tf_op jit(solution)/shard_map/all_to_all | solution.py:74
  128.5 10.6 %copy-start.3 = (f32[32,4,64,64]{3,2,1,0:T(8,128)S(1)}, f32[32,4,64,64]{3,2,1,0:T(8,128)}, u32[]{:S(2)}) copy-start(f32[32,4,64,64]{3,2,1,0:T(8,128)} %copy.17) | copy-start | bytes 6291460
  139.1 21.7 %copy-start.2 = (bf16[32,4,32,16,64]{4,3,1,2,0:T(8,128)(2,1)S(1)}, bf16[32,4,32,16,64]{4,3,1,2,0:T(8,128)(2,1)}, u32[]{:S(2)}) copy-start(bf16[32,4,32,16,64]{4,3,1,2,0:T(8,128)(2,1)} %convert_bitcast_fusion) | copy-start | bytes 25165828
  160.8 38.7 %copy-start.1 = (bf16[4,64,1024]{2,1,0:T(8,128)(2,1)S(1)}, bf16[4,64,1024]{2,1,0:T(8,128)(2,1)}, u32[]{:S(2)}) copy-start(bf16[4,64,1024]{2,1,0:T(8,128)(2,1)} %param.6) | copy-start | bytes 1572868

commit v5 on v4

--- a/solution.py
+++ b/solution.py
@@ -4,7 +4,7 @@
 from jax.sharding import PartitionSpec as P
 
 
-CHUNKS = 2
+CHUNKS = 4
 
 
 def body(wavefunction, left_env, right_env, local_ops, dest_sector, right_bond):

time: 200 us -> 189 us (0.945)
  blocking collectives: 87.5 us -> 29.2 us
  starting transfers between devices: 8.76 us -> 39.9 us
  waiting for transfers between devices: 24.6 us -> 54.1 us
  matrix products: 56.7 us -> 44.4 us
    all_to_all x1 -> x0, blocking collectives: 60.9 us -> none  [send(): lax.all_to_all(outgoing[:, c * chunk:(c + 1) * chunk], 'sec', 0, 0, tiled...]
    all_to_all x1 -> x3, starting transfers between devices: 8.76 us -> 31.1 us  [body(): upcoming = lax.all_to_all(piece, 'sec', 0, 0, tiled=True)]
    dot_general x2 -> x0, matrix products: 20.9 us -> none  [process(): jnp.einsum('itpq,ilqr->itlpr', item_ops, incoming, preferred_element_type...]
    all_to_all x1 -> x3, waiting for transfers between devices: 24.6 us -> 41.4 us  [body(): upcoming = lax.all_to_all(piece, 'sec', 0, 0, tiled=True)]
    all_to_all x0 -> x1, waiting for transfers between devices: none -> 12.7 us  [send(): lax.all_to_all(outgoing[:, c * chunk:(c + 1) * chunk], 'sec', 0, 0, tiled...]
    all_to_all x0 -> x1, starting transfers between devices: none -> 8.76 us  [send(): lax.all_to_all(outgoing[:, c * chunk:(c + 1) * chunk], 'sec', 0, 0, tiled...]
    dot_general x2 -> x4, matrix products: 31 us -> 39.6 us  [process(): jnp.einsum('itlpr,itdmr->dlpm', mixed, sector_env, preferred_element_type...]
    all_to_all x1, blocking collectives: 26.6 us -> 29.2 us  [body(): gathered = lax.all_to_all(pieces, 'op', 0, 0, tiled=True)]
  transfers between devices with their start and end apart: 1 -> 4, of which waited for: 1 -> 4; matrix products, arithmetic and copies ran while one was open for 12% -> 23% of each run, Pallas kernels for 0% -> 0%
where the time goes in v5:
time: 189 us; the launch traced here: 188 us
  waiting for transfers between devices  54.1 us (29%)
  matrix products  44.4 us (23%)
  starting transfers between devices  39.9 us (21%)
  blocking collectives  29.2 us (15%)
  local copies, waits for them, and re-layouts  18.1 us (10%)
  other arithmetic  2.2 us (1%)
    all_to_all x3, waiting for transfers between devices, body(): upcoming = lax.all_to_all(piece, 'sec', 0, 0, tiled=True)  41.4 us
    dot_general x4, matrix products, process(): jnp.einsum('itlpr,itdmr->dlpm', mixed, sector_env, preferred_element_type...  39.6 us
    all_to_all x3, starting transfers between devices, body(): upcoming = lax.all_to_all(piece, 'sec', 0, 0, tiled=True)  31.1 us
    all_to_all x1, blocking collectives, body(): gathered = lax.all_to_all(pieces, 'op', 0, 0, tiled=True)  29.2 us
    all_to_all x1, waiting for transfers between devices, send(): lax.all_to_all(outgoing[:, c * chunk:(c + 1) * chunk], 'sec', 0, 0, tiled...  12.7 us
    reshape x4, local copies, waits for them, and re-layouts, process(): incoming = received.reshape(sec_count, chunk, physical, rows)  9.37 us
    all_to_all x1, starting transfers between devices, send(): lax.all_to_all(outgoing[:, c * chunk:(c + 1) * chunk], 'sec', 0, 0, tiled...  8.76 us
    another operation x1, local copies, waits for them, and re-layouts  4.36 us
  transfers between devices with their start and end apart: 4, of which 4 were waited for; matrix products, arithmetic and copies ran while one was open for 23% of the time, Pallas kernels for 0%

profile of v5, /device:TPU:1, one launch (start us, length us, event | category | flops | bytes accessed | tf_op | source)
XLA Modules:
  0.0 188.1 jit_solution(8415781260679055529)
XLA Ops:
  0.0 0.0 copy-start
  0.0 0.8 add_select_fusion.3
  0.8 0.1 copy.14
  0.9 1.9 convert_bitcast_fusion
  2.8 0.0 copy-done
  2.8 1.7 bitcast_convert_fusion
  4.5 0.0 copy-start.4
  4.5 0.0 copy-start.5
  4.5 0.0 copy-start.6
  4.5 2.3 %fusion.134 = (bf16[32,16,1024]{2,1,0:T(8,128)(2,1)}, bf16[32,16,1024]{2,1,0:T(8,128)(2,1)}, bf16[32,16,1024]{2,1,0:T(8,128)(2,1)}, bf16[32,16,1024]{2,1,0:T(8,128)(2,1)}) fusion(bf16[32,64,1024]{2,1,0:T(8,128)(2,1)S(1)} %bitcast_convert_fusion), kind=kLoop, calls=%fused_computation.97 | loop fusion | bytes 8388608 | tf_op jit(solution)/shard_map/slice | solution.py:64
  6.9 13.7 %all-to-all-start.1 = ((bf16[32,16,1024]{2,1,0:T(8,128)(2,1)}), bf16[32,16,1024]{2,1,0:T(8,128)(2,1)S(1)}, u32[]{:S(2)}, u32[]{:S(2)}) async-start(bf16[32,16,1024]{2,1,0:T(8,128)(2,1)} %get-tuple-element.14), calls=%async_computation.1 | async-start | bytes 2097152 | tf_op jit(solution)/shard_map/all_to_all | solution.py:74
  20.6 0.0 copy-done.4
  20.6 0.1 copy.17
  20.8 0.1 reduce_sum.38
  20.9 0.1 reduce_sum.39
  21.0 0.1 convert_reduce_fusion
  21.1 0.0 copy-done.5
  21.1 0.1 convolution_convert_fusion.1
  21.3 0.0 copy-done.6
  21.3 0.8 fusion.42
  22.1 0.0 copy-start.3
  22.1 4.4 %copy.19 = f32[32,4,64,64]{3,2,1,0:T(8,128)} copy(f32[32,4,64,64]{3,0,2,1:T(8,128)S(1)} %fusion.42) | data formatting | bytes 4194304 | tf_op jit(solution)/shard_map/convert.2
  26.5 0.0 copy-done.3
  26.5 0.3 convolution_convert_fusion
  26.8 0.9 copy.23
  27.7 17.6 %all-to-all-done.1 = bf16[32,16,1024]{2,1,0:T(8,128)(2,1)S(1)} async-done(((bf16[32,16,1024]{2,1,0:T(8,128)(2,1)}), bf16[32,16,1024]{2,1,0:T(8,128)(2,1)S(1)}, u32[]{:S(2)}, u32[]{:S(2)}) %all-to-all-start.1) | async-done | bytes 1048608 | tf_op jit(solution)/shard_map/all_to_all | solution.py:74
  45.2 8.8 %all-to-all-start = ((bf16[32,16,1024]{2,1,0:T(8,128)(2,1)}), bf16[32,16,1024]{2,1,0:T(8,128)(2,1)S(1)}, u32[]{:S(2)}, u32[]{:S(2)}) async-start(bf16[32,16,1024]{2,1,0:T(8,128)(2,1)} %get-tuple-element.13), calls=%async_computation | async-start | bytes 2097152 | tf_op jit(solution)/shard_map/all_to_all | solution.py:64
  54.0 2.3 %reshape.46 = bf16[32,16,16,64]{3,2,1,0:T(8,128)(2,1)} reshape(bf16[32,16,1024]{2,1,0:T(8,128)(2,1)S(1)} %all-to-all-done.1) | data formatting | bytes 2097152 | tf_op jit(solution)/shard_map/reshape | solution.py:57
  56.4 9.5 %fusion.50 = bf16[4,16,16,64]{3,2,1,0:T(8,128)(2,1)S(1)} fusion(f32[32,4,64,64]{3,2,1,0:T(8,128)} %copy.19, f32[32,4]{0,1:T(4,128)S(1)} %get-tuple-element.17, bf16[32,4,16,16]{3,2,1,0:T(8,128)(2,1)S(1)} %copy.23, bf16[32,16,16,64]{3,2,1,0:T(8,128)(2,1)} %reshape.46), kind=kOutput, calls=%fused_computation.36 | convolution fusion | flops 1147142144 | bytes 3342848 | tf_op jit(solution)/shard_map/itlpr,itdmr->dlpm/dot_general | solution.py:61
  65.9 12.7 %all-to-all-done = bf16[32,16,1024]{2,1,0:T(8,128)(2,1)S(1)} async-done(((bf16[32,16,1024]{2,1,0:T(8,128)(2,1)}), bf16[32,16,1024]{2,1,0:T(8,128)(2,1)S(1)}, u32[]{:S(2)}, u32[]{:S(2)}) %all-to-all-start) | async-done | bytes 1048608 | tf_op jit(solution)/shard_map/all_to_all | solution.py:64
  78.6 8.7 %all-to-all-start.3 = ((bf16[32,16,1024]{2,1,0:T(8,128)(2,1)}), bf16[32,16,1024]{2,1,0:T(8,128)(2,1)S(1)}, u32[]{:S(2)}, u32[]{:S(2)}) async-start(bf16[32,16,1024]{2,1,0:T(8,128)(2,1)} %get-tuple-element.12), calls=%async_computation.3 | async-start | bytes 2097152 | tf_op jit(solution)/shard_map/all_to_all | solution.py:74
  87.3 2.3 %reshape.45 = bf16[32,16,16,64]{3,2,1,0:T(8,128)(2,1)} reshape(bf16[32,16,1024]{2,1,0:T(8,128)(2,1)S(1)} %all-to-all-done) | data formatting | bytes 2097152 | tf_op jit(solution)/shard_map/reshape | solution.py:57
  89.6 10.3 %fusion.43 = bf16[4,16,16,64]{3,2,1,0:T(8,128)(2,1)} fusion(f32[32,4,64,64]{3,2,1,0:T(8,128)} %copy.19, f32[32,4]{0,1:T(4,128)S(1)} %get-tuple-element.17, bf16[32,4,16,16]{3,2,1,0:T(8,128)(2,1)S(1)} %copy.23, bf16[32,16,16,64]{3,2,1,0:T(8,128)(2,1)} %reshape.45), kind=kOutput, calls=%fused_computation.35 | convolution fusion | flops 1147142144 | bytes 3342848 | tf_op jit(solution)/shard_map/itlpr,itdmr->dlpm/dot_general | solution.py:61
  99.9 11.9 %all-to-all-done.3 = bf16[32,16,1024]{2,1,0:T(8,128)(2,1)S(1)} async-done(((bf16[32,16,1024]{2,1,0:T(8,128)(2,1)}), bf16[32,16,1024]{2,1,0:T(8,128)(2,1)S(1)}, u32[]{:S(2)}, u32[]{:S(2)}) %all-to-all-start.3) | async-done | bytes 1048608 | tf_op jit(solution)/shard_map/all_to_all | solution.py:74
  111.8 8.7 %all-to-all-start.2 = ((bf16[32,16,1024]{2,1,0:T(8,128)(2,1)}), bf16[32,16,1024]{2,1,0:T(8,128)(2,1)S(1)}, u32[]{:S(2)}, u32[]{:S(2)}) async-start(bf16[32,16,1024]{2,1,0:T(8,128)(2,1)} %get-tuple-element.11), calls=%async_computation.2 | async-start | bytes 2097152 | tf_op jit(solution)/shard_map/all_to_all | solution.py:74
  120.5 2.3 %reshape.48 = bf16[32,16,16,64]{3,2,1,0:T(8,128)(2,1)} reshape(bf16[32,16,1024]{2,1,0:T(8,128)(2,1)S(1)} %all-to-all-done.3) | data formatting | bytes 2097152 | tf_op jit(solution)/shard_map/reshape | solution.py:57
  122.9 10.2 %fusion.92 = bf16[4,16,16,64]{3,2,1,0:T(8,128)(2,1)} fusion(f32[32,4,64,64]{3,2,1,0:T(8,128)} %copy.19, f32[32,4]{0,1:T(4,128)S(1)} %get-tuple-element.17, bf16[32,4,16,16]{3,2,1,0:T(8,128)(2,1)S(1)} %copy.23, bf16[32,16,16,64]{3,2,1,0:T(8,128)(2,1)} %reshape.48), kind=kOutput, calls=%fused_computation.43 | convolution fusion | flops 1147207680 | bytes 3342848 | tf_op jit(solution)/shard_map/itlpr,itdmr->dlpm/dot_general | solution.py:61
  133.1 11.9 %all-to-all-done.2 = bf16[32,16,1024]{2,1,0:T(8,128)(2,1)S(1)} async-done(((bf16[32,16,1024]{2,1,0:T(8,128)(2,1)}), bf16[32,16,1024]{2,1,0:T(8,128)(2,1)S(1)}, u32[]{:S(2)}, u32[]{:S(2)}) %all-to-all-start.2) | async-done | bytes 1048608 | tf_op jit(solution)/shard_map/all_to_all | solution.py:74
  145.0 2.3 %reshape.47 = bf16[32,16,16,64]{3,2,1,0:T(8,128)(2,1)} reshape(bf16[32,16,1024]{2,1,0:T(8,128)(2,1)S(1)} %all-to-all-done.2) | data formatting | bytes 2097152 | tf_op jit(solution)/shard_map/reshape | solution.py:57
  147.4 0.0 copy-start.1
  147.4 0.0 copy-start.2
  147.4 9.6 %fusion.85 = bf16[4,16,16,64]{3,2,1,0:T(8,128)(2,1)S(1)} fusion(f32[32,4,64,64]{3,2,1,0:T(8,128)} %copy.19, f32[32,4]{0,1:T(4,128)S(1)} %get-tuple-element.17, bf16[32,4,16,16]{3,2,1,0:T(8,128)(2,1)S(1)} %copy.23, bf16[32,16,16,64]{3,2,1,0:T(8,128)(2,1)} %reshape.47), kind=kOutput, calls=%fused_computation.42 | convolution fusion | flops 1147207680 | bytes 3342848 | tf_op jit(solution)/shard_map/itlpr,itdmr->dlpm/dot_general | solution.py:61
  156.9 0.0 copy-done.1
  157.0 0.0 copy-done.2
  157.0 0.3 pad_maximum_fusion
  157.2 0.6 convert_element_type.88
  157.9 0.2 copy.93
  158.1 29.2 %all_to_all.25 = bf16[16,4,4,1024]{3,2,1,0:T(4,128)(2,1)S(1)} all-to-all(bf16[16,4,4,1024]{3,2,1,0:T(4,128)(2,1)S(1)} %bitcast.165), channel_id=1, replica_groups=mesh['op'=16,'sec'=32] {'op'}, dimensions={0} | all-to-all | bytes 1048576 | tf_op jit(solution)/shard_map/all_to_all | solution.py:81
  187.3 0.8 reduce_sum.41
  (3 shorter events, 0.0 us)
Async XLA Ops:
  0.0 2.8 %copy-start = (bf16[4,64,1024]{2,1,0:T(8,128)(2,1)S(1)}, bf16[4,64,1024]{2,1,0:T(8,128)(2,1)}, u32[]{:S(2)}) copy-start(bf16[4,64,1024]{2,1,0:T(8,128)(2,1)} %param.6) | copy-start | bytes 1572868
  4.5 16.1 %copy-start.4 = (s32[8,128]{1,0:T(8,128)S(1)}, s32[8,128]{1,0:T(8,128)}, u32[]{:S(2)}) copy-start(s32[8,128]{1,0:T(8,128)} %param.10) | copy-start | bytes 12292
  4.5 16.6 %copy-start.5 = (s32[8,4]{0,1:T(4,128)S(1)}, s32[8,4]{0,1:T(4,128)}, u32[]{:S(2)}) copy-start(s32[8,4]{0,1:T(4,128)} %param.11) | copy-start | bytes 388
  4.5 16.7 %copy-start.6 = (bf16[4,4,64,64]{3,2,1,0:T(8,128)(2,1)S(1)}, bf16[4,4,64,64]{3,2,1,0:T(8,128)(2,1)}, u32[]{:S(2)}) copy-start(bf16[4,4,64,64]{3,2,1,0:T(8,128)(2,1)} %param.8) | copy-start | bytes 393220
  6.9 38.4 %all-to-all-start.1 = ((bf16[32,16,1024]{2,1,0:T(8,128)(2,1)}), bf16[32,16,1024]{2,1,0:T(8,128)(2,1)S(1)}, u32[]{:S(2)}, u32[]{:S(2)}) async-start(bf16[32,16,1024]{2,1,0:T(8,128)(2,1)} %get-tuple-element.14), calls=%async_computation.1 | async-start | bytes 2097152 | tf_op jit(solution)/shard_map/all_to_all | solution.py:74
  22.1 4.4 %copy-start.3 = (bf16[8,4,16,16]{3,2,1,0:T(8,128)(2,1)S(1)}, bf16[8,4,16,16]{3,2,1,0:T(8,128)(2,1)}, u32[]{:S(2)}) copy-start(bf16[8,4,16,16]{3,2,1,0:T(8,128)(2,1)} %param.9) | copy-start | bytes 49156
  45.2 33.4 %all-to-all-start = ((bf16[32,16,1024]{2,1,0:T(8,128)(2,1)}), bf16[32,16,1024]{2,1,0:T(8,128)(2,1)S(1)}, u32[]{:S(2)}, u32[]{:S(2)}) async-start(bf16[32,16,1024]{2,1,0:T(8,128)(2,1)} %get-tuple-element.13), calls=%async_computation | async-start | bytes 2097152 | tf_op jit(solution)/shard_map/all_to_all | solution.py:64
  78.6 33.2 %all-to-all-start.3 = ((bf16[32,16,1024]{2,1,0:T(8,128)(2,1)}), bf16[32,16,1024]{2,1,0:T(8,128)(2,1)S(1)}, u32[]{:S(2)}, u32[]{:S(2)}) async-start(bf16[32,16,1024]{2,1,0:T(8,128)(2,1)} %get-tuple-element.12), calls=%async_computation.3 | async-start | bytes 2097152 | tf_op jit(solution)/shard_map/all_to_all | solution.py:74
  111.8 33.2 %all-to-all-start.2 = ((bf16[32,16,1024]{2,1,0:T(8,128)(2,1)}), bf16[32,16,1024]{2,1,0:T(8,128)(2,1)S(1)}, u32[]{:S(2)}, u32[]{:S(2)}) async-start(bf16[32,16,1024]{2,1,0:T(8,128)(2,1)} %get-tuple-element.11), calls=%async_computation.2 | async-start | bytes 2097152 | tf_op jit(solution)/shard_map/all_to_all | solution.py:74
  147.4 9.6 %copy-start.1 = (bf16[4,16,16,64]{3,2,1,0:T(8,128)(2,1)S(1)}, bf16[4,16,16,64]{3,2,1,0:T(8,128)(2,1)}, u32[]{:S(2)}) copy-start(bf16[4,16,16,64]{3,2,1,0:T(8,128)(2,1)} %fusion.43) | copy-start | bytes 393220
  147.4 9.6 %copy-start.2 = (bf16[4,16,16,64]{3,2,1,0:T(8,128)(2,1)S(1)}, bf16[4,16,16,64]{3,2,1,0:T(8,128)(2,1)}, u32[]{:S(2)}) copy-start(bf16[4,16,16,64]{3,2,1,0:T(8,128)(2,1)} %fusion.92) | copy-start | bytes 393220

commit v6 on v5

--- a/solution.py
+++ b/solution.py
@@ -4,7 +4,7 @@
 from jax.sharding import PartitionSpec as P
 
 
-CHUNKS = 4
+CHUNK_ROWS = (32, 16, 16)
 
 
 def body(wavefunction, left_env, right_env, local_ops, dest_sector, right_bond):
@@ -52,25 +52,30 @@
         "itmr,id->itdmr", item_env, dest_hot.astype(bf16), preferred_element_type=f32
     ).astype(bf16)
 
-    chunk = rows // CHUNKS
+    bounds = [0]
+    for size in CHUNK_ROWS:
+        bounds.append(bounds[-1] + size * rows // 64)
+
     def process(received):
-        incoming = received.reshape(sec_count, chunk, physical, rows)
+        incoming = received.reshape(sec_count, -1, physical, rows)
         mixed = jnp.einsum(
             "itpq,ilqr->itlpr", item_ops, incoming, preferred_element_type=f32
         ).astype(bf16)
         return jnp.einsum("itlpr,itdmr->dlpm", mixed, sector_env, preferred_element_type=f32)
 
-    def send(c):
-        return lax.all_to_all(outgoing[:, c * chunk:(c + 1) * chunk], "sec", 0, 0, tiled=True)
-
-    received = send(0)
+    count = len(CHUNK_ROWS)
+    received = lax.all_to_all(outgoing[:, bounds[0]:bounds[1]], "sec", 0, 0, tiled=True)
     parts = []
-    for c in range(CHUNKS):
+    for c in range(count):
         upcoming = None
-        if c + 1 < CHUNKS:
-            piece = outgoing[:, (c + 1) * chunk:(c + 2) * chunk]
+        if c + 1 < count:
+            piece = outgoing[:, bounds[c + 1]:bounds[c + 2]]
             if parts:
-                piece, parts[-1] = lax.optimization_barrier((piece, parts[-1]))
+                piece, received, parts[-1] = lax.optimization_barrier(
+                    (piece, received, parts[-1])
+                )
+            else:
+                piece, received = lax.optimization_barrier((piece, received))
             upcoming = lax.all_to_all(piece, "sec", 0, 0, tiled=True)
         parts.append(process(received))
         received = upcoming

time: 189 us -> 193 us (1.021)
  starting transfers between devices: 39.9 us -> 30.5 us
  local copies, waits for them, and re-layouts: 18.1 us -> 24.1 us
  matrix products: 44.4 us -> 50 us
    all_to_all x1, waiting for transfers between devices: 12.7 us -> 38.4 us  [body(): lax.all_to_all(outgoing[:, bounds[0]:bounds[1]], 'sec', 0, 0, tiled=True)]
    all_to_all x3 -> x2, waiting for transfers between devices: 41.4 us -> 16.9 us  [body(): upcoming = lax.all_to_all(piece, 'sec', 0, 0, tiled=True)]
    dot_general x0 -> x3, matrix products: none -> 15 us  [process(): jnp.einsum('itpq,ilqr->itlpr', item_ops, incoming, preferred_element_type...]
    all_to_all x3 -> x2, starting transfers between devices: 31.1 us -> 16.6 us  [body(): upcoming = lax.all_to_all(piece, 'sec', 0, 0, tiled=True)]
    dot_general x4 -> x3, matrix products: 39.6 us -> 29.2 us  [process(): jnp.einsum('itlpr,itdmr->dlpm', mixed, sector_env, preferred_element_type...]
    all_to_all x1, starting transfers between devices: 8.76 us -> 13.9 us  [body(): lax.all_to_all(outgoing[:, bounds[0]:bounds[1]], 'sec', 0, 0, tiled=True)]
    unnamed x15 -> x23, local copies, waits for them, and re-layouts: 0.14 us -> 3.03 us
    reshape x4 -> x3, local copies, waits for them, and re-layouts: 9.37 us -> 10.1 us  [process(): incoming = received.reshape(sec_count, -1, physical, rows)]
  transfers between devices with their start and end apart: 4 -> 3, of which waited for: 4 -> 2; matrix products, arithmetic and copies ran while one was open for 23% -> 25% of each run, Pallas kernels for 0% -> 0%
where the time goes in v6:
time: 193 us; the launch traced here: 192 us
  waiting for transfers between devices  55.3 us (29%)
  matrix products  50 us (26%)
  starting transfers between devices  30.5 us (16%)
  blocking collectives  29.7 us (15%)
  local copies, waits for them, and re-layouts  24.1 us (12%)
  other arithmetic  2.23 us (1%)
    all_to_all x1, waiting for transfers between devices, body(): lax.all_to_all(outgoing[:, bounds[0]:bounds[1]], 'sec', 0, 0, tiled=True)  38.4 us
    all_to_all x1, blocking collectives, body(): gathered = lax.all_to_all(pieces, 'op', 0, 0, tiled=True)  29.7 us
    dot_general x3, matrix products, process(): jnp.einsum('itlpr,itdmr->dlpm', mixed, sector_env, preferred_element_type...  29.2 us
    all_to_all x2, waiting for transfers between devices, body(): upcoming = lax.all_to_all(piece, 'sec', 0, 0, tiled=True)  16.9 us
    all_to_all x2, starting transfers between devices, body(): upcoming = lax.all_to_all(piece, 'sec', 0, 0, tiled=True)  16.6 us
    dot_general x3, matrix products, process(): jnp.einsum('itpq,ilqr->itlpr', item_ops, incoming, preferred_element_type...  15 us
    all_to_all x1, starting transfers between devices, body(): lax.all_to_all(outgoing[:, bounds[0]:bounds[1]], 'sec', 0, 0, tiled=True)  13.9 us
    reshape x3, local copies, waits for them, and re-layouts, process(): incoming = received.reshape(sec_count, -1, physical, rows)  10.1 us
  transfers between devices with their start and end apart: 3, of which 2 were waited for; matrix products, arithmetic and copies ran while one was open for 25% of the time, Pallas kernels for 0%

profile of v6, /device:TPU:1, one launch (start us, length us, event | category | flops | bytes accessed | tf_op | source)
XLA Modules:
  0.0 192.2 jit_solution(13291123469697748804)
XLA Ops:
  0.0 0.0 copy-start
  0.0 0.8 add_select_fusion.3
  0.8 0.1 copy.19
  0.9 1.9 convert_bitcast_fusion.3
  2.8 0.0 copy-done
  2.8 1.7 bitcast_convert_fusion
  4.5 0.0 copy-start.6
  4.5 1.9 %copy-done.6 = bf16[32,64,1024]{2,1,0:T(8,128)(2,1)} copy-done((bf16[32,64,1024]{2,1,0:T(8,128)(2,1)}, bf16[32,64,1024]{2,1,0:T(8,128)(2,1)S(1)}, u32[]{:S(2)}) %copy-start.6) | copy-done | bytes 4194328
  6.4 0.0 copy-start.9
  6.4 0.0 copy-start.8
  6.4 1.5 slice.14
  8.0 0.0 copy-start.10
  8.0 13.9 %all-to-all-start = ((bf16[32,32,1024]{2,1,0:T(8,128)(2,1)}), bf16[32,32,1024]{2,1,0:T(8,128)(2,1)S(1)}, u32[]{:S(2)}, u32[]{:S(2)}) async-start(bf16[32,32,1024]{2,1,0:T(8,128)(2,1)} %slice.14), calls=%async_computation | async-start | bytes 4194304 | tf_op jit(solution)/shard_map/all_to_all | solution.py:67
  21.9 0.0 copy-done.9
  21.9 0.1 copy.22
  22.0 0.1 convert_reduce_fusion
  22.1 0.0 copy-done.8
  22.1 0.3 convolution_convert_fusion
  22.4 0.9 copy.30
  23.3 0.9 copy.43
  24.2 0.1 reduce_sum.38
  24.3 0.1 reduce_sum.39
  24.5 0.0 copy-done.10
  24.5 0.1 convolution_convert_fusion.1
  24.6 1.8 fusion.21
  26.4 0.0 copy-start.7
  26.4 4.4 %copy.24 = f32[32,4,64,64]{3,2,1,0:T(8,128)} copy(f32[32,4,64,64]{3,0,2,1:T(8,128)S(1)} %fusion.21) | data formatting | bytes 4194304 | tf_op jit(solution)/shard_map/convert.2
  30.8 0.0 copy-done.7
  30.8 1.5 fusion.86
  32.3 38.4 %all-to-all-done = bf16[32,32,1024]{2,1,0:T(8,128)(2,1)S(1)} async-done(((bf16[32,32,1024]{2,1,0:T(8,128)(2,1)}), bf16[32,32,1024]{2,1,0:T(8,128)(2,1)S(1)}, u32[]{:S(2)}, u32[]{:S(2)}) %all-to-all-start) | async-done | bytes 2097184 | tf_op jit(solution)/shard_map/all_to_all | solution.py:67
  70.7 4.0 %reshape.52 = bf16[32,32,16,64,1]{3,2,1,0,4:T(8,128)(2,1)} reshape(bf16[32,32,1024]{2,1,0:T(8,128)(2,1)S(1)} %all-to-all-done) | data formatting | bytes 4194304 | tf_op jit(solution)/shard_map/reshape | solution.py:60
  74.7 7.2 %all-to-all-start.1 = ((bf16[32,16,1024]{2,1,0:T(8,128)(2,1)}), bf16[32,16,1024]{2,1,0:T(8,128)(2,1)S(1)}, u32[]{:S(2)}, u32[]{:S(2)}) async-start(bf16[32,16,1024]{2,1,0:T(8,128)(2,1)} %get-tuple-element.10), calls=%async_computation.1 | async-start | bytes 2097152 | tf_op jit(solution)/shard_map/all_to_all | solution.py:79
  81.9 0.0 copy-start.3
  82.0 10.5 %convert_bitcast_fusion = bf16[32,4,32,16,64]{4,3,1,2,0:T(8,128)(2,1)} fusion(bf16[32,4,16,16,1]{3,2,1,4,0:T(8,128)(2,1)S(1)} %copy.43, bf16[32,32,16,64,1]{3,2,1,0,4:T(8,128)(2,1)} %reshape.52), kind=kOutput, calls=%fused_computation.3 | convolution fusion | flops 138412032 | bytes 10551296 | tf_op jit(solution)/shard_map/itpq,ilqr->itlpr/dot_general | solution.py:61
  92.4 0.0 copy-done.3
  92.4 19.1 %fusion.22 = bf16[4,32,16,64]{3,1,2,0:T(8,128)(2,1)S(1)} fusion(bf16[32,4,32,16,64]{4,3,1,2,0:T(8,128)(2,1)} %convert_bitcast_fusion, f32[32,4,64,64]{3,2,1,0:T(8,128)S(1)} %copy-done.3, f32[32,4]{0,1:T(4,128)S(1)} %get-tuple-element.17), kind=kOutput, calls=%fused_computation.26 | convolution fusion | flops 2151677952 | bytes 10748416 | tf_op jit(solution)/shard_map/itlpr,itdmr->dlpm/dot_general | solution.py:64
  111.6 0.0 all-to-all-done.1
  111.6 0.0 copy-start.2
  111.6 1.0 copy-done.2
  112.5 2.9 %reshape.43 = bf16[32,16,16,64]{3,2,1,0:T(8,128)(2,1)S(1)} reshape(bf16[32,16,1024]{2,1,0:T(8,128)(2,1)} %copy-done.2) | data formatting | bytes 2097152 | tf_op jit(solution)/shard_map/reshape | solution.py:60
  115.5 9.4 %all-to-all-start.2 = ((bf16[32,16,1024]{2,1,0:T(8,128)(2,1)}), bf16[32,16,1024]{2,1,0:T(8,128)(2,1)}, u32[]{:S(2)}, u32[]{:S(2)}) async-start(bf16[32,16,1024]{2,1,0:T(8,128)(2,1)} %get-tuple-element.14), calls=%async_computation.2 | async-start | bytes 2097152 | tf_op jit(solution)/shard_map/all_to_all | solution.py:79
  124.9 0.0 copy-start.4
  124.9 2.3 %convert_bitcast_fusion.2 = bf16[32,4,16,16,64,1]{4,3,1,0,2,5:T(8,128)(2,1)S(1)} fusion(bf16[32,4,16,16]{3,2,1,0:T(8,128)(2,1)S(1)} %copy.30, bf16[32,16,16,64]{3,2,1,0:T(8,128)(2,1)S(1)} %reshape.43), kind=kOutput, calls=%fused_computation.12 | convolution fusion | flops 69206016 | bytes 5308416 | tf_op jit(solution)/shard_map/itpq,ilqr->itlpr/dot_general | solution.py:61
  127.2 0.0 copy-done.4
  127.3 5.0 %fusion.47 = bf16[4,16,16,64]{3,1,2,0:T(8,128)(2,1)S(1)} fusion(bf16[32,4,16,16,64,1]{4,3,1,0,2,5:T(8,128)(2,1)S(1)} %convert_bitcast_fusion.2, f32[32,4,64,64]{3,2,1,0:T(8,128)S(1)} %copy-done.4, f32[32,4]{0,1:T(4,128)S(1)} %get-tuple-element.17), kind=kOutput, calls=%fused_computation.32 | convolution fusion | flops 1078001664 | bytes 6423040 | tf_op jit(solution)/shard_map/itlpr,itdmr->dlpm/dot_general | solution.py:64
  132.3 16.9 %all-to-all-done.2 = bf16[32,16,1024]{2,1,0:T(8,128)(2,1)} async-done(((bf16[32,16,1024]{2,1,0:T(8,128)(2,1)}), bf16[32,16,1024]{2,1,0:T(8,128)(2,1)}, u32[]{:S(2)}, u32[]{:S(2)}) %all-to-all-start.2) | async-done | bytes 1048608 | tf_op jit(solution)/shard_map/all_to_all | solution.py:79
  149.2 3.2 %reshape.44 = bf16[32,16,16,64]{3,2,1,0:T(8,128)(2,1)S(1)} reshape(bf16[32,16,1024]{2,1,0:T(8,128)(2,1)} %all-to-all-done.2) | data formatting | bytes 2097152 | tf_op jit(solution)/shard_map/reshape | solution.py:60
  152.4 0.0 copy-start.5
  152.4 2.3 %convert_bitcast_fusion.1 = bf16[32,4,16,16,64,1]{4,3,1,0,2,5:T(8,128)(2,1)S(1)} fusion(bf16[32,4,16,16]{3,2,1,0:T(8,128)(2,1)S(1)} %copy.30, bf16[32,16,16,64]{3,2,1,0:T(8,128)(2,1)S(1)} %reshape.44), kind=kOutput, calls=%fused_computation.11 | convolution fusion | flops 69206016 | bytes 5308416 | tf_op jit(solution)/shard_map/itpq,ilqr->itlpr/dot_general | solution.py:61
  154.7 0.0 copy-done.5
  154.7 0.0 copy-start.1
  154.7 5.0 %fusion.52 = bf16[4,16,16,64]{3,1,2,0:T(8,128)(2,1)S(1)} fusion(bf16[32,4,16,16,64,1]{4,3,1,0,2,5:T(8,128)(2,1)S(1)} %convert_bitcast_fusion.1, f32[32,4,64,64]{3,2,1,0:T(8,128)S(1)} %copy-done.5, f32[32,4]{0,1:T(4,128)S(1)} %get-tuple-element.17), kind=kOutput, calls=%fused_computation.33 | convolution fusion | flops 1078001664 | bytes 6423040 | tf_op jit(solution)/shard_map/itlpr,itdmr->dlpm/dot_general | solution.py:64
  159.8 0.3 pad_maximum_fusion
  160.1 0.7 copy.35
  160.7 0.6 convert_element_type.80
  161.4 0.2 copy.36
  161.6 29.7 %all_to_all.20 = bf16[16,4,4,1024]{3,2,1,0:T(4,128)(2,1)S(1)} all-to-all(bf16[16,4,4,1024]{3,2,1,0:T(4,128)(2,1)S(1)} %copy.36), channel_id=1, replica_groups=mesh['op'=16,'sec'=32] {'op'}, dimensions={0} | all-to-all | bytes 1048576 | tf_op jit(solution)/shard_map/all_to_all | solution.py:86
  191.3 0.8 reduce_sum.41
  192.1 0.0 copy-done.1
  (3 shorter events, 0.0 us)
Async XLA Ops:
  0.0 2.8 %copy-start = (bf16[4,64,1024]{2,1,0:T(8,128)(2,1)S(1)}, bf16[4,64,1024]{2,1,0:T(8,128)(2,1)}, u32[]{:S(2)}) copy-start(bf16[4,64,1024]{2,1,0:T(8,128)(2,1)} %param.6) | copy-start | bytes 1572868
  4.5 1.9 %copy-start.6 = (bf16[32,64,1024]{2,1,0:T(8,128)(2,1)}, bf16[32,64,1024]{2,1,0:T(8,128)(2,1)S(1)}, u32[]{:S(2)}) copy-start(bf16[32,64,1024]{2,1,0:T(8,128)(2,1)S(1)} %bitcast_convert_fusion) | copy-start | bytes 12582916
  6.4 15.4 %copy-start.9 = (s32[8,128]{1,0:T(8,128)S(1)}, s32[8,128]{1,0:T(8,128)}, u32[]{:S(2)}) copy-start(s32[8,128]{1,0:T(8,128)} %param.10) | copy-start | bytes 12292
  6.4 15.7 %copy-start.8 = (bf16[8,4,16,16]{3,2,1,0:T(8,128)(2,1)S(1)}, bf16[8,4,16,16]{3,2,1,0:T(8,128)(2,1)}, u32[]{:S(2)}) copy-start(bf16[8,4,16,16]{3,2,1,0:T(8,128)(2,1)} %param.9) | copy-start | bytes 49156
  8.0 16.5 %copy-start.10 = (s32[8,4]{0,1:T(4,128)S(1)}, s32[8,4]{0,1:T(4,128)}, u32[]{:S(2)}) copy-start(s32[8,4]{0,1:T(4,128)} %param.11) | copy-start | bytes 388
  8.0 62.7 %all-to-all-start = ((bf16[32,32,1024]{2,1,0:T(8,128)(2,1)}), bf16[32,32,1024]{2,1,0:T(8,128)(2,1)S(1)}, u32[]{:S(2)}, u32[]{:S(2)}) async-start(bf16[32,32,1024]{2,1,0:T(8,128)(2,1)} %slice.14), calls=%async_computation | async-start | bytes 4194304 | tf_op jit(solution)/shard_map/all_to_all | solution.py:67
  26.4 4.4 %copy-start.7 = (bf16[32,64,1024]{2,1,0:T(8,128)(2,1)S(1)}, bf16[32,64,1024]{2,1,0:T(8,128)(2,1)}, u32[]{:S(2)}) copy-start(bf16[32,64,1024]{2,1,0:T(8,128)(2,1)} %copy-done.6) | copy-start | bytes 12582916
  74.7 36.9 %all-to-all-start.1 = ((bf16[32,16,1024]{2,1,0:T(8,128)(2,1)}), bf16[32,16,1024]{2,1,0:T(8,128)(2,1)S(1)}, u32[]{:S(2)}, u32[]{:S(2)}) async-start(bf16[32,16,1024]{2,1,0:T(8,128)(2,1)} %get-tuple-element.10), calls=%async_computation.1 | async-start | bytes 2097152 | tf_op jit(solution)/shard_map/all_to_all | solution.py:79
  81.9 10.5 %copy-start.3 = (f32[32,4,64,64]{3,2,1,0:T(8,128)S(1)}, f32[32,4,64,64]{3,2,1,0:T(8,128)}, u32[]{:S(2)}) copy-start(f32[32,4,64,64]{3,2,1,0:T(8,128)} %copy.24) | copy-start | bytes 6291460
  111.6 1.0 copy-start.2
  115.5 33.7 %all-to-all-start.2 = ((bf16[32,16,1024]{2,1,0:T(8,128)(2,1)}), bf16[32,16,1024]{2,1,0:T(8,128)(2,1)}, u32[]{:S(2)}, u32[]{:S(2)}) async-start(bf16[32,16,1024]{2,1,0:T(8,128)(2,1)} %get-tuple-element.14), calls=%async_computation.2 | async-start | bytes 2097152 | tf_op jit(solution)/shard_map/all_to_all | solution.py:79
  124.9 2.3 %copy-start.4 = (f32[32,4,64,64]{3,2,1,0:T(8,128)S(1)}, f32[32,4,64,64]{3,2,1,0:T(8,128)}, u32[]{:S(2)}) copy-start(f32[32,4,64,64]{3,2,1,0:T(8,128)} %copy.24) | copy-start | bytes 6291460
  152.4 2.3 %copy-start.5 = (f32[32,4,64,64]{3,2,1,0:T(8,128)S(1)}, f32[32,4,64,64]{3,2,1,0:T(8,128)}, u32[]{:S(2)}) copy-start(f32[32,4,64,64]{3,2,1,0:T(8,128)} %copy.24) | copy-start | bytes 6291460
  154.7 37.4 %copy-start.1 = (bf16[4,64,1024]{2,1,0:T(8,128)(2,1)S(1)}, bf16[4,64,1024]{2,1,0:T(8,128)(2,1)}, u32[]{:S(2)}) copy-start(bf16[4,64,1024]{2,1,0:T(8,128)(2,1)} %param.6) | copy-start | bytes 1572868

commit v7 on v6

--- a/solution.py
+++ b/solution.py
@@ -4,7 +4,8 @@
 from jax.sharding import PartitionSpec as P
 
 
-CHUNK_ROWS = (32, 16, 16)
+CHUNK_ROWS = (48, 16)
+PIECE_ROWS = 16
 
 
 def body(wavefunction, left_env, right_env, local_ops, dest_sector, right_bond):
@@ -56,12 +57,22 @@
     for size in CHUNK_ROWS:
         bounds.append(bounds[-1] + size * rows // 64)
 
-    def process(received):
+    def process_piece(received):
         incoming = received.reshape(sec_count, -1, physical, rows)
         mixed = jnp.einsum(
             "itpq,ilqr->itlpr", item_ops, incoming, preferred_element_type=f32
         ).astype(bf16)
         return jnp.einsum("itlpr,itdmr->dlpm", mixed, sector_env, preferred_element_type=f32)
+
+    def process(received):
+        step = PIECE_ROWS * rows // 64
+        return jnp.concatenate(
+            [
+                process_piece(received[:, start:start + step])
+                for start in range(0, received.shape[1], step)
+            ],
+            axis=1,
+        )
 
     count = len(CHUNK_ROWS)
     received = lax.all_to_all(outgoing[:, bounds[0]:bounds[1]], "sec", 0, 0, tiled=True)

time: 193 us -> 186 us (0.964)
  starting transfers between devices: 30.5 us -> 22.9 us
  waiting for transfers between devices: 55.3 us -> 62.1 us
  matrix products: 50 us -> 43.7 us
  local copies, waits for them, and re-layouts: 24.1 us -> 29.3 us
  blocking collectives: 29.7 us -> 25.1 us
    all_to_all x1, waiting for transfers between devices: 38.4 us -> 62.1 us  [body(): lax.all_to_all(outgoing[:, bounds[0]:bounds[1]], 'sec', 0, 0, tiled=True)]
    all_to_all x2 -> x1, waiting for transfers between devices: 16.9 us -> 0.01 us  [body(): upcoming = lax.all_to_all(piece, 'sec', 0, 0, tiled=True)]
    all_to_all x2 -> x1, starting transfers between devices: 16.6 us -> 8.93 us  [body(): upcoming = lax.all_to_all(piece, 'sec', 0, 0, tiled=True)]
    dot_general x6 -> x4, matrix products: 44.2 us -> 38.9 us  [process_piece(): jnp.einsum('itlpr,itdmr->dlpm', mixed, sector_env, preferred_element_type...]
    all_to_all x1, blocking collectives: 29.7 us -> 25.1 us  [body(): gathered = lax.all_to_all(pieces, 'op', 0, 0, tiled=True)]
    slice x0 -> x1, local copies, waits for them, and re-layouts: none -> 3.74 us  [process(): received[:, start:start + step]]
    reshape x3 -> x4, local copies, waits for them, and re-layouts: 10.1 us -> 12.7 us  [process_piece(): incoming = received.reshape(sec_count, -1, physical, rows)]
  transfers between devices with their start and end apart: 3 -> 2, of which waited for: 2 -> 1; matrix products, arithmetic and copies ran while one was open for 25% -> 28% of each run, Pallas kernels for 0% -> 0%
where the time goes in v7:
time: 186 us
  waiting for transfers between devices  62.1 us (33%)
  matrix products  43.7 us (23%)
  local copies, waits for them, and re-layouts  29.3 us (16%)
  blocking collectives  25.1 us (13%)
  starting transfers between devices  22.9 us (12%)
  other arithmetic  2.2 us (1%)
    all_to_all x1, waiting for transfers between devices, body(): lax.all_to_all(outgoing[:, bounds[0]:bounds[1]], 'sec', 0, 0, tiled=True)  62.1 us
    dot_general x4, matrix products, process_piece(): jnp.einsum('itlpr,itdmr->dlpm', mixed, sector_env, preferred_element_type...  38.9 us
    all_to_all x1, blocking collectives, body(): gathered = lax.all_to_all(pieces, 'op', 0, 0, tiled=True)  25.1 us
    all_to_all x1, starting transfers between devices, body(): lax.all_to_all(outgoing[:, bounds[0]:bounds[1]], 'sec', 0, 0, tiled=True)  14 us
    reshape x4, local copies, waits for them, and re-layouts, process_piece(): incoming = received.reshape(sec_count, -1, physical, rows)  12.7 us
    all_to_all x1, starting transfers between devices, body(): upcoming = lax.all_to_all(piece, 'sec', 0, 0, tiled=True)  8.93 us
    another operation x1, local copies, waits for them, and re-layouts  4.36 us
    slice x1, local copies, waits for them, and re-layouts, process(): received[:, start:start + step]  3.74 us
  transfers between devices with their start and end apart: 2, of which 1 were waited for; matrix products, arithmetic and copies ran while one was open for 28% of the time, Pallas kernels for 0%

profile of v7, /device:TPU:1, one launch (start us, length us, event | category | flops | bytes accessed | tf_op | source)
XLA Modules:
  0.0 185.6 jit_solution(16279852904888967715)
XLA Ops:
  0.0 0.0 copy-start
  0.0 0.8 add_select_fusion.1
  0.8 0.1 copy.17
  0.9 1.9 %convert_bitcast_fusion = bf16[32,64,4,64]{3,0,1,2:T(8,128)(2,1)S(1)} fusion(bf16[8,4,64,64]{3,2,1,0:T(8,128)(2,1)} %param.7, s32[8,4]{0,1:T(4,128)S(1)} %copy.17), kind=kOutput, calls=%fused_computation.33 | convolution fusion | flops 8913920 | bytes 1310848 | tf_op jit(solution)/shard_map/ask,asij->kisj/dot_general | solution.py:27
  2.8 0.0 copy-done
  2.8 1.7 bitcast_convert_fusion
  4.5 0.0 copy-start.1
  4.5 1.9 %copy-done.1 = bf16[32,64,1024]{2,1,0:T(8,128)(2,1)} copy-done((bf16[32,64,1024]{2,1,0:T(8,128)(2,1)}, bf16[32,64,1024]{2,1,0:T(8,128)(2,1)S(1)}, u32[]{:S(2)}) %copy-start.1) | copy-done | bytes 4194328
  6.4 2.2 %slice.21 = bf16[32,48,1024]{2,1,0:T(8,128)(2,1)} slice(bf16[32,64,1024]{2,1,0:T(8,128)(2,1)S(1)} %bitcast_convert_fusion), slice={[0:32], [0:48], [0:1024]} | slice | bytes 6291456 | tf_op jit(solution)/shard_map/slice | solution.py:78
  8.6 0.0 copy-start.4
  8.6 0.0 copy-start.5
  8.6 0.0 copy-start.6
  8.6 14.0 %all-to-all-start = ((bf16[32,48,1024]{2,1,0:T(8,128)(2,1)}), bf16[32,48,1024]{2,1,0:T(8,128)(2,1)}, u32[]{:S(2)}, u32[]{:S(2)}) async-start(bf16[32,48,1024]{2,1,0:T(8,128)(2,1)} %slice.21), calls=%async_computation | async-start | bytes 6291456 | tf_op jit(solution)/shard_map/all_to_all | solution.py:78
  22.6 0.0 copy-done.4
  22.6 0.1 copy.14
  22.7 2.3 %slice.20 = bf16[32,16,1024]{2,1,0:T(8,128)(2,1)} slice(bf16[32,64,1024]{2,1,0:T(8,128)(2,1)} %copy-done.1), slice={[0:32], [48:64], [0:1024]} | slice | bytes 2097152 | tf_op jit(solution)/shard_map/slice | solution.py:83
  25.1 0.1 reduce_sum.38
  25.2 0.1 reduce_sum.39
  25.3 0.1 convert_reduce_fusion
  25.5 0.0 copy-done.5
  25.5 0.1 convolution_convert_fusion.1
  25.6 0.0 copy-done.6
  25.6 0.8 fusion.42
  26.5 0.0 copy-start.3
  26.5 4.4 %copy.16 = f32[32,4,64,64]{3,2,1,0:T(8,128)} copy(f32[32,4,64,64]{3,0,2,1:T(8,128)S(1)} %fusion.42) | data formatting | bytes 4194304 | tf_op jit(solution)/shard_map/convert.2
  30.8 0.0 copy-done.3
  30.8 0.3 convolution_convert_fusion
  31.1 0.9 copy.23
  32.0 62.1 %all-to-all-done = bf16[32,48,1024]{2,1,0:T(8,128)(2,1)} async-done(((bf16[32,48,1024]{2,1,0:T(8,128)(2,1)}), bf16[32,48,1024]{2,1,0:T(8,128)(2,1)}, u32[]{:S(2)}, u32[]{:S(2)}) %all-to-all-start) | async-done | bytes 3145760 | tf_op jit(solution)/shard_map/all_to_all | solution.py:78
  94.2 8.9 %all-to-all-start.1 = ((bf16[32,16,1024]{2,1,0:T(8,128)(2,1)}), bf16[32,16,1024]{2,1,0:T(8,128)(2,1)S(1)}, u32[]{:S(2)}, u32[]{:S(2)}) async-start(bf16[32,16,1024]{2,1,0:T(8,128)(2,1)} %slice.20), calls=%async_computation.1 | async-start | bytes 2097152 | tf_op jit(solution)/shard_map/all_to_all | solution.py:90
  103.1 3.7 %fusion.162 = (bf16[32,16,1024]{2,1,0:T(8,128)(2,1)S(1)}, bf16[32,16,1024]{2,1,0:T(8,128)(2,1)}, bf16[32,16,1024]{2,1,0:T(8,128)(2,1)}) fusion(bf16[32,48,1024]{2,1,0:T(8,128)(2,1)} %all-to-all-done), kind=kLoop, calls=%fused_computation.101 | loop fusion | bytes 6291456 | tf_op jit(solution)/shard_map/slice | solution.py:71
  106.8 4.0 %reshape.47 = bf16[32,16,16,64]{3,2,1,0:T(8,128)(2,1)} reshape(bf16[32,16,1024]{2,1,0:T(8,128)(2,1)} %get-tuple-element.10) | data formatting | bytes 2097152 | tf_op jit(solution)/shard_map/reshape | solution.py:61
  110.9 4.0 %reshape.46 = bf16[32,16,16,64]{3,2,1,0:T(8,128)(2,1)} reshape(bf16[32,16,1024]{2,1,0:T(8,128)(2,1)} %get-tuple-element.11) | data formatting | bytes 2097152 | tf_op jit(solution)/shard_map/reshape | solution.py:61
  114.9 9.5 %fusion.113 = bf16[4,16,16,64]{3,2,1,0:T(8,128)(2,1)S(1)} fusion(f32[32,4,64,64]{3,2,1,0:T(8,128)} %copy.16, f32[32,4]{0,1:T(4,128)S(1)} %get-tuple-element.12, bf16[32,4,16,16]{3,2,1,0:T(8,128)(2,1)S(1)} %copy.23, bf16[32,16,16,64]{3,2,1,0:T(8,128)(2,1)} %reshape.47), kind=kOutput, calls=%fused_computation.46 | convolution fusion | flops 1147207680 | bytes 3342848 | tf_op jit(solution)/shard_map/itlpr,itdmr->dlpm/dot_general | solution.py:65
  124.4 10.3 %fusion.106 = bf16[4,16,16,64]{3,2,1,0:T(8,128)(2,1)} fusion(f32[32,4,64,64]{3,2,1,0:T(8,128)} %copy.16, f32[32,4]{0,1:T(4,128)S(1)} %get-tuple-element.12, bf16[32,4,16,16]{3,2,1,0:T(8,128)(2,1)S(1)} %copy.23, bf16[32,16,16,64]{3,2,1,0:T(8,128)(2,1)} %reshape.46), kind=kOutput, calls=%fused_computation.45 | convolution fusion | flops 1147207680 | bytes 3342848 | tf_op jit(solution)/shard_map/itlpr,itdmr->dlpm/dot_general | solution.py:65
  134.7 2.3 %reshape.45 = bf16[32,16,16,64]{3,2,1,0:T(8,128)(2,1)} reshape(bf16[32,16,1024]{2,1,0:T(8,128)(2,1)S(1)} %get-tuple-element.9) | data formatting | bytes 2097152 | tf_op jit(solution)/shard_map/reshape | solution.py:61
  137.0 9.5 %fusion.99 = bf16[4,16,16,64]{3,2,1,0:T(8,128)(2,1)S(1)} fusion(f32[32,4,64,64]{3,2,1,0:T(8,128)} %copy.16, f32[32,4]{0,1:T(4,128)S(1)} %get-tuple-element.12, bf16[32,4,16,16]{3,2,1,0:T(8,128)(2,1)S(1)} %copy.23, bf16[32,16,16,64]{3,2,1,0:T(8,128)(2,1)} %reshape.45), kind=kOutput, calls=%fused_computation.44 | convolution fusion | flops 1147207680 | bytes 3342848 | tf_op jit(solution)/shard_map/itlpr,itdmr->dlpm/dot_general | solution.py:65
  146.6 0.0 all-to-all-done.1
  146.6 2.3 %reshape.48 = bf16[32,16,16,64]{3,2,1,0:T(8,128)(2,1)} reshape(bf16[32,16,1024]{2,1,0:T(8,128)(2,1)S(1)} %all-to-all-done.1) | data formatting | bytes 2097152 | tf_op jit(solution)/shard_map/reshape | solution.py:61
  148.9 0.0 copy-start.2
  148.9 9.6 %fusion.120 = bf16[4,16,16,64]{3,2,1,0:T(8,128)(2,1)S(1)} fusion(f32[32,4,64,64]{3,2,1,0:T(8,128)} %copy.16, f32[32,4]{0,1:T(4,128)S(1)} %get-tuple-element.12, bf16[32,4,16,16]{3,2,1,0:T(8,128)(2,1)S(1)} %copy.23, bf16[32,16,16,64]{3,2,1,0:T(8,128)(2,1)} %reshape.48), kind=kOutput, calls=%fused_computation.47 | convolution fusion | flops 1147207680 | bytes 3342848 | tf_op jit(solution)/shard_map/itlpr,itdmr->dlpm/dot_general | solution.py:65
  158.5 0.0 copy-done.2
  158.5 0.3 pad_maximum_fusion
  158.8 0.6 convert_element_type.88
  159.4 0.2 copy.101
  159.6 25.1 %all_to_all.15 = bf16[16,4,4,1024]{3,2,1,0:T(4,128)(2,1)S(1)} all-to-all(bf16[16,4,4,1024]{3,2,1,0:T(4,128)(2,1)S(1)} %bitcast.189), channel_id=1, replica_groups=mesh['op'=16,'sec'=32] {'op'}, dimensions={0} | all-to-all | bytes 1048576 | tf_op jit(solution)/shard_map/all_to_all | solution.py:97
  184.7 0.8 reduce_sum.41
  (3 shorter events, 0.0 us)
Async XLA Ops:
  0.0 2.8 %copy-start = (bf16[4,64,1024]{2,1,0:T(8,128)(2,1)S(1)}, bf16[4,64,1024]{2,1,0:T(8,128)(2,1)}, u32[]{:S(2)}) copy-start(bf16[4,64,1024]{2,1,0:T(8,128)(2,1)} %param.6) | copy-start | bytes 1572868
  4.5 1.9 %copy-start.1 = (bf16[32,64,1024]{2,1,0:T(8,128)(2,1)}, bf16[32,64,1024]{2,1,0:T(8,128)(2,1)S(1)}, u32[]{:S(2)}) copy-start(bf16[32,64,1024]{2,1,0:T(8,128)(2,1)S(1)} %bitcast_convert_fusion) | copy-start | bytes 12582916
  8.6 14.0 %copy-start.4 = (s32[8,128]{1,0:T(8,128)S(1)}, s32[8,128]{1,0:T(8,128)}, u32[]{:S(2)}) copy-start(s32[8,128]{1,0:T(8,128)} %param.10) | copy-start | bytes 12292
  8.6 16.8 %copy-start.5 = (s32[8,4]{0,1:T(4,128)S(1)}, s32[8,4]{0,1:T(4,128)}, u32[]{:S(2)}) copy-start(s32[8,4]{0,1:T(4,128)} %param.11) | copy-start | bytes 388
  8.6 17.0 %copy-start.6 = (bf16[4,4,64,64]{3,2,1,0:T(8,128)(2,1)S(1)}, bf16[4,4,64,64]{3,2,1,0:T(8,128)(2,1)}, u32[]{:S(2)}) copy-start(bf16[4,4,64,64]{3,2,1,0:T(8,128)(2,1)} %param.8) | copy-start | bytes 393220
  8.6 85.5 %all-to-all-start = ((bf16[32,48,1024]{2,1,0:T(8,128)(2,1)}), bf16[32,48,1024]{2,1,0:T(8,128)(2,1)}, u32[]{:S(2)}, u32[]{:S(2)}) async-start(bf16[32,48,1024]{2,1,0:T(8,128)(2,1)} %slice.21), calls=%async_computation | async-start | bytes 6291456 | tf_op jit(solution)/shard_map/all_to_all | solution.py:78
  26.5 4.4 %copy-start.3 = (bf16[8,4,16,16]{3,2,1,0:T(8,128)(2,1)S(1)}, bf16[8,4,16,16]{3,2,1,0:T(8,128)(2,1)}, u32[]{:S(2)}) copy-start(bf16[8,4,16,16]{3,2,1,0:T(8,128)(2,1)} %param.9) | copy-start | bytes 49156
  94.2 52.4 %all-to-all-start.1 = ((bf16[32,16,1024]{2,1,0:T(8,128)(2,1)}), bf16[32,16,1024]{2,1,0:T(8,128)(2,1)S(1)}, u32[]{:S(2)}, u32[]{:S(2)}) async-start(bf16[32,16,1024]{2,1,0:T(8,128)(2,1)} %slice.20), calls=%async_computation.1 | async-start | bytes 2097152 | tf_op jit(solution)/shard_map/all_to_all | solution.py:90
  148.9 9.6 %copy-start.2 = (bf16[4,16,16,64]{3,2,1,0:T(8,128)(2,1)S(1)}, bf16[4,16,16,64]{3,2,1,0:T(8,128)(2,1)}, u32[]{:S(2)}) copy-start(bf16[4,16,16,64]{3,2,1,0:T(8,128)(2,1)} %fusion.106) | copy-start | bytes 393220

commit v8 on v7

--- a/solution.py
+++ b/solution.py
@@ -27,9 +27,15 @@
     chosen_left = jnp.einsum(
         "ask,asij->kisj", send_hot, left_env, preferred_element_type=f32
     ).astype(bf16)
-    outgoing = jnp.einsum(
-        "kisj,sjx->kix", chosen_left, wavefunction, preferred_element_type=f32
-    ).astype(bf16)
+
+    def outgoing(start, stop):
+        return jnp.einsum(
+            "kisj,sjx->kix",
+            chosen_left[:, start:stop],
+            wavefunction,
+            preferred_element_type=f32,
+        ).astype(bf16)
+
     grid = dest_sector.reshape(left_count, sec_count, sec_blocks)
     mine = (grid // sec_blocks) == own_sec
     bond_hot = jnp.sum(mine, axis=2).T.astype(bf16)
@@ -75,12 +81,12 @@
         )
 
     count = len(CHUNK_ROWS)
-    received = lax.all_to_all(outgoing[:, bounds[0]:bounds[1]], "sec", 0, 0, tiled=True)
+    received = lax.all_to_all(outgoing(bounds[0], bounds[1]), "sec", 0, 0, tiled=True)
     parts = []
     for c in range(count):
         upcoming = None
         if c + 1 < count:
-            piece = outgoing[:, bounds[c + 1]:bounds[c + 2]]
+            piece = outgoing(bounds[c + 1], bounds[c + 2])
             if parts:
                 piece, received, parts[-1] = lax.optimization_barrier(
                     (piece, received, parts[-1])

time: 186 us -> 184 us (0.989)
  local copies, waits for them, and re-layouts: 29.3 us -> 23.2 us
  matrix products: 43.7 us -> 46.6 us
    slice x2 -> x3, local copies, waits for them, and re-layouts: 4.52 us -> 0.28 us  [outgoing(): chosen_left[:, start:stop]]
    dot_general x1 -> x2, matrix products: 1.71 us -> 4.66 us  [outgoing(): jnp.einsum('kisj,sjx->kix', chosen_left[:, start:stop], wavefunction, pre...]
    unnamed x15, local copies, waits for them, and re-layouts: 2.05 us -> 0.13 us
where the time goes in v8:
time: 184 us; the launch traced here: 183 us
  waiting for transfers between devices  62.9 us (34%)
  matrix products  46.6 us (25%)
  blocking collectives  25.5 us (14%)
  local copies, waits for them, and re-layouts  23.2 us (13%)
  starting transfers between devices  22.7 us (12%)
  other arithmetic  2.2 us (1%)
    all_to_all x1, waiting for transfers between devices, body(): lax.all_to_all(outgoing(bounds[0], bounds[1]), 'sec', 0, 0, tiled=True)  62.9 us
    dot_general x4, matrix products, process_piece(): jnp.einsum('itlpr,itdmr->dlpm', mixed, sector_env, preferred_element_type...  38.9 us
    all_to_all x1, blocking collectives, body(): gathered = lax.all_to_all(pieces, 'op', 0, 0, tiled=True)  25.5 us
    all_to_all x1, starting transfers between devices, body(): lax.all_to_all(outgoing(bounds[0], bounds[1]), 'sec', 0, 0, tiled=True)  14 us
    reshape x4, local copies, waits for them, and re-layouts, process_piece(): incoming = received.reshape(sec_count, -1, physical, rows)  12.7 us
    all_to_all x1, starting transfers between devices, body(): upcoming = lax.all_to_all(piece, 'sec', 0, 0, tiled=True)  8.74 us
    dot_general x2, matrix products, outgoing(): jnp.einsum('kisj,sjx->kix', chosen_left[:, start:stop], wavefunction, pre...  4.66 us
    another operation x1, local copies, waits for them, and re-layouts  4.37 us
  transfers between devices with their start and end apart: 2, of which 1 were waited for; matrix products, arithmetic and copies ran while one was open for 28% of the time, Pallas kernels for 0%

profile of v8, /device:TPU:1, one launch (start us, length us, event | category | flops | bytes accessed | tf_op | source)
XLA Modules:
  0.0 183.3 jit_solution(17566398415736763797)
XLA Ops:
  0.0 0.0 copy-start
  0.0 0.8 add_select_fusion.1
  0.8 0.1 copy.25
  0.9 1.9 %convert_bitcast_fusion = bf16[32,64,4,64]{3,0,1,2:T(8,128)(2,1)S(1)} fusion(bf16[8,4,64,64]{3,2,1,0:T(8,128)(2,1)} %param.7, s32[8,4]{0,1:T(4,128)S(1)} %copy.25), kind=kOutput, calls=%fused_computation.33 | convolution fusion | flops 8913920 | bytes 1310848 | tf_op jit(solution)/shard_map/ask,asij->kisj/dot_general | solution.py:27
  2.8 0.0 copy-start.1
  2.8 0.3 slice.21
  3.1 0.0 copy-done
  3.1 3.1 %bitcast_convert_fusion = bf16[32,48,1024]{2,1,0:T(8,128)(2,1)} fusion(bf16[32,48,4,64]{3,0,1,2:T(8,128)(2,1)S(1)} %slice.21, bf16[4,64,1024]{2,1,0:T(8,128)(2,1)S(1)} %copy-done), kind=kOutput, calls=%fused_computation.22 | convolution fusion | flops 806879232 | bytes 4456448 | tf_op jit(solution)/shard_map/kisj,sjx->kix/dot_general | solution.py:32
  6.2 0.0 copy-start.4
  6.2 0.0 copy-start.5
  6.2 0.0 copy-start.6
  6.2 14.0 %all-to-all-start = ((bf16[32,48,1024]{2,1,0:T(8,128)(2,1)}), bf16[32,48,1024]{2,1,0:T(8,128)(2,1)}, u32[]{:S(2)}, u32[]{:S(2)}) async-start(bf16[32,48,1024]{2,1,0:T(8,128)(2,1)} %bitcast_convert_fusion), calls=%async_computation | async-start | bytes 6291456 | tf_op jit(solution)/shard_map/all_to_all | solution.py:84
  20.2 0.0 copy-done.4
  20.2 0.1 copy.22
  20.3 0.0 copy-done.1
  20.3 0.1 reduce_sum.38
  20.4 0.1 reduce_sum.39
  20.5 0.1 convert_reduce_fusion
  20.7 0.0 copy-done.5
  20.7 0.1 convolution_convert_fusion.1
  20.8 0.0 copy-done.6
  20.8 0.8 fusion.41
  21.7 0.0 copy-start.3
  21.7 0.0 slice-start
  21.7 4.4 %copy.24 = f32[32,4,64,64]{3,2,1,0:T(8,128)} copy(f32[32,4,64,64]{3,0,2,1:T(8,128)S(1)} %fusion.41) | data formatting | bytes 4194304 | tf_op jit(solution)/shard_map/convert.2
  26.1 0.0 copy-done.3
  26.1 0.3 convolution_convert_fusion
  26.4 0.9 copy.32
  27.3 0.0 slice-done
  27.3 1.5 bitcast_convert_fusion.2
  28.8 62.9 %all-to-all-done = bf16[32,48,1024]{2,1,0:T(8,128)(2,1)} async-done(((bf16[32,48,1024]{2,1,0:T(8,128)(2,1)}), bf16[32,48,1024]{2,1,0:T(8,128)(2,1)}, u32[]{:S(2)}, u32[]{:S(2)}) %all-to-all-start) | async-done | bytes 3145760 | tf_op jit(solution)/shard_map/all_to_all | solution.py:84
  91.7 8.7 %all-to-all-start.1 = ((bf16[32,16,1024]{2,1,0:T(8,128)(2,1)}), bf16[32,16,1024]{2,1,0:T(8,128)(2,1)S(1)}, u32[]{:S(2)}, u32[]{:S(2)}) async-start(bf16[32,16,1024]{2,1,0:T(8,128)(2,1)} %bitcast_convert_fusion.2), calls=%async_computation.1 | async-start | bytes 2097152 | tf_op jit(solution)/shard_map/all_to_all | solution.py:96
  100.4 3.7 %fusion.164 = (bf16[32,16,1024]{2,1,0:T(8,128)(2,1)S(1)}, bf16[32,16,1024]{2,1,0:T(8,128)(2,1)}, bf16[32,16,1024]{2,1,0:T(8,128)(2,1)}) fusion(bf16[32,48,1024]{2,1,0:T(8,128)(2,1)} %all-to-all-done), kind=kLoop, calls=%fused_computation.104 | loop fusion | bytes 6291456 | tf_op jit(solution)/shard_map/slice | solution.py:77
  104.2 4.0 %reshape.47 = bf16[32,16,16,64]{3,2,1,0:T(8,128)(2,1)} reshape(bf16[32,16,1024]{2,1,0:T(8,128)(2,1)} %get-tuple-element.10) | data formatting | bytes 2097152 | tf_op jit(solution)/shard_map/reshape | solution.py:67
  108.2 4.1 %reshape.46 = bf16[32,16,16,64]{3,2,1,0:T(8,128)(2,1)} reshape(bf16[32,16,1024]{2,1,0:T(8,128)(2,1)} %get-tuple-element.11) | data formatting | bytes 2097152 | tf_op jit(solution)/shard_map/reshape | solution.py:67
  112.3 9.5 %fusion.113 = bf16[4,16,16,64]{3,2,1,0:T(8,128)(2,1)S(1)} fusion(f32[32,4,64,64]{3,2,1,0:T(8,128)} %copy.24, f32[32,4]{0,1:T(4,128)S(1)} %get-tuple-element.12, bf16[32,4,16,16]{3,2,1,0:T(8,128)(2,1)S(1)} %copy.32, bf16[32,16,16,64]{3,2,1,0:T(8,128)(2,1)} %reshape.47), kind=kOutput, calls=%fused_computation.47 | convolution fusion | flops 1147207680 | bytes 3342848 | tf_op jit(solution)/shard_map/itlpr,itdmr->dlpm/dot_general | solution.py:71
  121.8 10.3 %fusion.106 = bf16[4,16,16,64]{3,2,1,0:T(8,128)(2,1)} fusion(f32[32,4,64,64]{3,2,1,0:T(8,128)} %copy.24, f32[32,4]{0,1:T(4,128)S(1)} %get-tuple-element.12, bf16[32,4,16,16]{3,2,1,0:T(8,128)(2,1)S(1)} %copy.32, bf16[32,16,16,64]{3,2,1,0:T(8,128)(2,1)} %reshape.46), kind=kOutput, calls=%fused_computation.46 | convolution fusion | flops 1147207680 | bytes 3342848 | tf_op jit(solution)/shard_map/itlpr,itdmr->dlpm/dot_general | solution.py:71
  132.1 2.3 %reshape.45 = bf16[32,16,16,64]{3,2,1,0:T(8,128)(2,1)} reshape(bf16[32,16,1024]{2,1,0:T(8,128)(2,1)S(1)} %get-tuple-element.9) | data formatting | bytes 2097152 | tf_op jit(solution)/shard_map/reshape | solution.py:67
  134.4 9.5 %fusion.99 = bf16[4,16,16,64]{3,2,1,0:T(8,128)(2,1)S(1)} fusion(f32[32,4,64,64]{3,2,1,0:T(8,128)} %copy.24, f32[32,4]{0,1:T(4,128)S(1)} %get-tuple-element.12, bf16[32,4,16,16]{3,2,1,0:T(8,128)(2,1)S(1)} %copy.32, bf16[32,16,16,64]{3,2,1,0:T(8,128)(2,1)} %reshape.45), kind=kOutput, calls=%fused_computation.45 | convolution fusion | flops 1147207680 | bytes 3342848 | tf_op jit(solution)/shard_map/itlpr,itdmr->dlpm/dot_general | solution.py:71
  143.9 0.0 all-to-all-done.1
  143.9 2.3 %reshape.48 = bf16[32,16,16,64]{3,2,1,0:T(8,128)(2,1)} reshape(bf16[32,16,1024]{2,1,0:T(8,128)(2,1)S(1)} %all-to-all-done.1) | data formatting | bytes 2097152 | tf_op jit(solution)/shard_map/reshape | solution.py:67
  146.3 0.0 copy-start.2
  146.3 9.6 %fusion.120 = bf16[4,16,16,64]{3,2,1,0:T(8,128)(2,1)S(1)} fusion(f32[32,4,64,64]{3,2,1,0:T(8,128)} %copy.24, f32[32,4]{0,1:T(4,128)S(1)} %get-tuple-element.12, bf16[32,4,16,16]{3,2,1,0:T(8,128)(2,1)S(1)} %copy.32, bf16[32,16,16,64]{3,2,1,0:T(8,128)(2,1)} %reshape.48), kind=kOutput, calls=%fused_computation.48 | convolution fusion | flops 1147207680 | bytes 3342848 | tf_op jit(solution)/shard_map/itlpr,itdmr->dlpm/dot_general | solution.py:71
  155.8 0.0 copy-done.2
  155.8 0.3 pad_maximum_fusion
  156.1 0.6 convert_element_type.92
  156.7 0.2 copy.113
  157.0 25.5 %all_to_all.15 = bf16[16,4,4,1024]{3,2,1,0:T(4,128)(2,1)S(1)} all-to-all(bf16[16,4,4,1024]{3,2,1,0:T(4,128)(2,1)S(1)} %bitcast.194), channel_id=1, replica_groups=mesh['op'=16,'sec'=32] {'op'}, dimensions={0} | all-to-all | bytes 1048576 | tf_op jit(solution)/shard_map/all_to_all | solution.py:103
  182.4 0.8 reduce_sum.41
  (3 shorter events, 0.0 us)
Async XLA Ops:
  0.0 3.1 %copy-start = (bf16[4,64,1024]{2,1,0:T(8,128)(2,1)S(1)}, bf16[4,64,1024]{2,1,0:T(8,128)(2,1)}, u32[]{:S(2)}) copy-start(bf16[4,64,1024]{2,1,0:T(8,128)(2,1)} %param.6) | copy-start | bytes 1572868
  2.8 17.5 %copy-start.1 = (bf16[32,64,4,64]{3,0,1,2:T(8,128)(2,1)}, bf16[32,64,4,64]{3,0,1,2:T(8,128)(2,1)S(1)}, u32[]{:S(2)}) copy-start(bf16[32,64,4,64]{3,0,1,2:T(8,128)(2,1)S(1)} %convert_bitcast_fusion) | copy-start | bytes 3145732
  6.2 14.0 %copy-start.4 = (s32[8,128]{1,0:T(8,128)S(1)}, s32[8,128]{1,0:T(8,128)}, u32[]{:S(2)}) copy-start(s32[8,128]{1,0:T(8,128)} %param.10) | copy-start | bytes 12292
  6.2 14.5 %copy-start.5 = (s32[8,4]{0,1:T(4,128)S(1)}, s32[8,4]{0,1:T(4,128)}, u32[]{:S(2)}) copy-start(s32[8,4]{0,1:T(4,128)} %param.11) | copy-start | bytes 388
  6.2 14.6 %copy-start.6 = (bf16[4,4,64,64]{3,2,1,0:T(8,128)(2,1)S(1)}, bf16[4,4,64,64]{3,2,1,0:T(8,128)(2,1)}, u32[]{:S(2)}) copy-start(bf16[4,4,64,64]{3,2,1,0:T(8,128)(2,1)} %param.8) | copy-start | bytes 393220
  6.2 85.5 %all-to-all-start = ((bf16[32,48,1024]{2,1,0:T(8,128)(2,1)}), bf16[32,48,1024]{2,1,0:T(8,128)(2,1)}, u32[]{:S(2)}, u32[]{:S(2)}) async-start(bf16[32,48,1024]{2,1,0:T(8,128)(2,1)} %bitcast_convert_fusion), calls=%async_computation | async-start | bytes 6291456 | tf_op jit(solution)/shard_map/all_to_all | solution.py:84
  21.7 4.4 %copy-start.3 = (bf16[8,4,16,16]{3,2,1,0:T(8,128)(2,1)S(1)}, bf16[8,4,16,16]{3,2,1,0:T(8,128)(2,1)}, u32[]{:S(2)}) copy-start(bf16[8,4,16,16]{3,2,1,0:T(8,128)(2,1)} %param.9) | copy-start | bytes 49156
  21.7 5.6 %slice-start = ((bf16[32,64,4,64]{3,0,1,2:T(8,128)(2,1)}), bf16[32,16,4,64]{3,0,1,2:T(8,128)(2,1)S(1)}, s32[]{:S(2)}) async-start(bf16[32,64,4,64]{3,0,1,2:T(8,128)(2,1)} %copy-done.1), calls=%async_computation.3 | async-start | bytes 1048576 | tf_op jit(solution)/shard_map/slice | solution.py:34
  91.7 52.2 %all-to-all-start.1 = ((bf16[32,16,1024]{2,1,0:T(8,128)(2,1)}), bf16[32,16,1024]{2,1,0:T(8,128)(2,1)S(1)}, u32[]{:S(2)}, u32[]{:S(2)}) async-start(bf16[32,16,1024]{2,1,0:T(8,128)(2,1)} %bitcast_convert_fusion.2), calls=%async_computation.1 | async-start | bytes 2097152 | tf_op jit(solution)/shard_map/all_to_all | solution.py:96
  146.3 9.6 %copy-start.2 = (bf16[4,16,16,64]{3,2,1,0:T(8,128)(2,1)S(1)}, bf16[4,16,16,64]{3,2,1,0:T(8,128)(2,1)}, u32[]{:S(2)}) copy-start(bf16[4,16,16,64]{3,2,1,0:T(8,128)(2,1)} %fusion.106) | copy-start | bytes 393220

commit v9 on v8

--- a/solution.py
+++ b/solution.py
@@ -58,6 +58,7 @@
     sector_env = jnp.einsum(
         "itmr,id->itdmr", item_env, dest_hot.astype(bf16), preferred_element_type=f32
     ).astype(bf16)
+    sector_matrix = sector_env.transpose(0, 1, 4, 2, 3).reshape(-1, sec_blocks * rows)
 
     bounds = [0]
     for size in CHUNK_ROWS:
@@ -68,7 +69,11 @@
         mixed = jnp.einsum(
             "itpq,ilqr->itlpr", item_ops, incoming, preferred_element_type=f32
         ).astype(bf16)
-        return jnp.einsum("itlpr,itdmr->dlpm", mixed, sector_env, preferred_element_type=f32)
+        piece_rows = mixed.shape[2]
+        lhs = mixed.transpose(2, 3, 0, 1, 4).reshape(piece_rows * physical, -1)
+        flat = jnp.dot(lhs, sector_matrix, preferred_element_type=f32)
+        flat = flat.reshape(piece_rows, physical, sec_blocks, rows)
+        return flat.transpose(2, 0, 1, 3)
 
     def process(received):
         step = PIECE_ROWS * rows // 64

time: 184 us -> 273 us (1.48); the launches traced: 183 us -> 268 us
  local copies, waits for them, and re-layouts: 23.2 us -> 116 us
  matrix products: 46.6 us -> 34.9 us
  waiting for transfers between devices: 62.9 us -> 57.2 us
  other arithmetic: 2.2 us -> 6.45 us
  blocking collectives: 25.5 us -> 29.1 us
    dot_general x0 -> x4, local copies, waits for them, and re-layouts: none -> 54.7 us  [process_piece(): flat = jnp.dot(lhs, sector_matrix, preferred_element_type=f32)]
    convert_element_type x0 -> x4, local copies, waits for them, and re-layouts: none -> 25.4 us  [process_piece(): mixed = jnp.einsum('itpq,ilqr->itlpr', item_ops, incoming, preferred_elem...]
    all_to_all x1, waiting for transfers between devices: 62.9 us -> 44.7 us  [body(): lax.all_to_all(outgoing(bounds[0], bounds[1]), 'sec', 0, 0, tiled=True)]
    reshape x0 -> x1, local copies, waits for them, and re-layouts: none -> 13.7 us  [body(): sector_env.transpose(0, 1, 4, 2, 3).reshape(-1, sec_blocks * rows)]
    all_to_all x1, waiting for transfers between devices: 0.01 us -> 12.5 us  [body(): upcoming = lax.all_to_all(piece, 'sec', 0, 0, tiled=True)]
    dot_general x4 -> x8, matrix products: 38.9 us -> 27.1 us  [the longest x4 17.9 us: process_piece(): flat = jnp.dot(lhs, sector_matrix, preferred_element_type=f32)]
    convert_element_type x0 -> x1, other arithmetic: none -> 4.87 us  [body(): sector_env = jnp.einsum('itmr,id->itdmr', item_env, dest_hot.astype(bf16)...]
    all_to_all x1, blocking collectives: 25.5 us -> 29.1 us  [body(): gathered = lax.all_to_all(pieces, 'op', 0, 0, tiled=True)]
  transfers between devices with their start and end apart: 2 -> 2, of which waited for: 1 -> 2; matrix products, arithmetic and copies ran while one was open for 28% -> 14% of each run, Pallas kernels for 0% -> 0%
where the time goes in v9:
time: 273 us; the launch traced here: 268 us
  local copies, waits for them, and re-layouts  116 us (42%)
  waiting for transfers between devices  57.2 us (21%)
  matrix products  34.9 us (13%)
  blocking collectives  29.1 us (11%)
  starting transfers between devices  23.8 us (9%)
  other arithmetic  6.45 us (2%)
    dot_general x4, local copies, waits for them, and re-layouts, process_piece(): flat = jnp.dot(lhs, sector_matrix, preferred_element_type=f32)  54.7 us
    all_to_all x1, waiting for transfers between devices, body(): lax.all_to_all(outgoing(bounds[0], bounds[1]), 'sec', 0, 0, tiled=True)  44.7 us
    all_to_all x1, blocking collectives, body(): gathered = lax.all_to_all(pieces, 'op', 0, 0, tiled=True)  29.1 us
    convert_element_type x4, local copies, waits for them, and re-layouts, process_piece(): mixed = jnp.einsum('itpq,ilqr->itlpr', item_ops, incoming, preferred_elem...  25.4 us
    dot_general x4, matrix products, process_piece(): flat = jnp.dot(lhs, sector_matrix, preferred_element_type=f32)  17.9 us
    all_to_all x1, starting transfers between devices, body(): lax.all_to_all(outgoing(bounds[0], bounds[1]), 'sec', 0, 0, tiled=True)  14.5 us
    reshape x1, local copies, waits for them, and re-layouts, body(): sector_env.transpose(0, 1, 4, 2, 3).reshape(-1, sec_blocks * rows)  13.7 us
    all_to_all x1, waiting for transfers between devices, body(): upcoming = lax.all_to_all(piece, 'sec', 0, 0, tiled=True)  12.5 us
  transfers between devices with their start and end apart: 2, of which 2 were waited for; matrix products, arithmetic and copies ran while one was open for 14% of the time, Pallas kernels for 0%

profile of v9, /device:TPU:1, one launch (start us, length us, event | category | flops | bytes accessed | tf_op | source)
XLA Modules:
  0.0 268.0 jit_solution(18360982041950412481)
XLA Ops:
  0.0 0.0 copy-start
  0.0 0.8 add_select_fusion.3
  0.8 0.1 copy.34
  0.9 1.9 convert_bitcast_fusion.4
  2.8 0.0 copy-start.2
  2.8 0.3 slice.21
  3.1 0.0 copy-done
  3.1 3.1 %bitcast_convert_fusion = bf16[32,48,1024]{2,1,0:T(8,128)(2,1)} fusion(bf16[32,48,4,64]{3,0,1,2:T(8,128)(2,1)S(1)} %slice.21, bf16[4,64,1024]{2,1,0:T(8,128)(2,1)S(1)} %copy-done), kind=kOutput, calls=%fused_computation.6 | convolution fusion | flops 806879232 | bytes 4456448 | tf_op jit(solution)/shard_map/kisj,sjx->kix/dot_general | solution.py:32
  6.2 14.5 %all-to-all-start = ((bf16[32,48,1024]{2,1,0:T(8,128)(2,1)}), bf16[32,48,1024]{2,1,0:T(8,128)(2,1)}, u32[]{:S(2)}, u32[]{:S(2)}) async-start(bf16[32,48,1024]{2,1,0:T(8,128)(2,1)} %bitcast_convert_fusion), calls=%async_computation | async-start | bytes 6291456 | tf_op jit(solution)/shard_map/all_to_all | solution.py:89
  20.7 0.0 copy-done.2
  20.7 0.0 copy-done.9
  20.7 0.1 copy.38
  20.8 0.1 convert_reduce_fusion
  20.9 0.0 copy-done.8
  21.0 0.3 fusion.27
  21.2 0.9 copy.57
  22.2 0.1 reduce_sum.39
  22.3 0.1 reduce_sum.40
  22.4 0.0 copy-done.10
  22.4 0.1 convolution_convert_fusion.1
  22.5 0.0 copy-done.11
  22.5 0.9 fusion.13
  23.4 3.9 %copy.44 = f32[32,4,64,64]{3,1,0,2:T(4,128)S(1)} copy(f32[32,4,64,64]{3,0,2,1:T(8,128)S(1)} %fusion.13) | data formatting | bytes 4194304 | tf_op jit(solution)/shard_map/convert.2
  27.4 4.9 %fusion = bf16[32,4,64,4,64]{2,1,0,4,3:T(4,128)(2,1)} fusion(f32[32,4,64,64]{3,1,0,2:T(4,128)S(1)} %copy.44, f32[32,4]{0,1:T(4,128)S(1)} %get-tuple-element.12), kind=kLoop, calls=%fused_computation.1 | loop fusion | flops 4194304 | bytes 6291968 | tf_op jit(solution)/shard_map/convert_element_type | solution.py:60
  32.2 13.7 %reshape.69 = bf16[8192,256]{0,1:T(8,128)(2,1)} reshape(bf16[32,4,64,4,64]{2,1,0,4,3:T(4,128)(2,1)} %fusion) | data formatting | bytes 8388608 | tf_op jit(solution)/shard_map/reshape | solution.py:61
  45.9 0.0 slice-done
  45.9 1.6 bitcast_convert_fusion.2
  47.5 44.7 %all-to-all-done = bf16[32,48,1024]{2,1,0:T(8,128)(2,1)} async-done(((bf16[32,48,1024]{2,1,0:T(8,128)(2,1)}), bf16[32,48,1024]{2,1,0:T(8,128)(2,1)}, u32[]{:S(2)}, u32[]{:S(2)}) %all-to-all-start) | async-done | bytes 3145760 | tf_op jit(solution)/shard_map/all_to_all | solution.py:89
  92.2 3.6 %fusion.69 = (bf16[32,16,1024]{2,1,0:T(8,128)(2,1)}, bf16[32,16,1024]{2,1,0:T(8,128)(2,1)}, bf16[32,16,1024]{2,1,0:T(8,128)(2,1)}) fusion(bf16[32,48,1024]{2,1,0:T(8,128)(2,1)} %all-to-all-done), kind=kLoop, calls=%fused_computation.84 | loop fusion | bytes 6291456 | tf_op jit(solution)/shard_map/slice | solution.py:82
  95.8 3.1 %reshape.88 = bf16[32,16,16,64,1]{3,2,1,0,4:T(8,128)(2,1)S(1)} reshape(bf16[32,16,1024]{2,1,0:T(8,128)(2,1)} %get-tuple-element.10) | data formatting | bytes 2097152 | tf_op jit(solution)/shard_map/reshape | solution.py:68
  98.9 2.3 convert_bitcast_fusion.1
  101.2 6.3 %copy.48 = bf16[16,16,32,4,64]{4,3,2,1,0:T(4,128)(2,1)} copy(bf16[16,16,32,4,64]{4,1,3,0,2:T(8,128)(2,1)S(1)} %convert_bitcast_fusion.1) | data formatting | bytes 8388608 | tf_op jit(solution)/shard_map/convert_element_type | solution.py:71
  107.6 13.6 %reshape.90 = bf16[16,16,8192,1]{2,1,0,3:T(8,128)(2,1)} reshape(bf16[16,16,32,4,64]{4,3,2,1,0:T(4,128)(2,1)} %copy.48) | data formatting | bytes 8388608 | tf_op jit(solution)/shard_map/dot_general | solution.py:74
  121.2 2.9 %reshape.85 = bf16[32,16,16,64,1]{3,2,1,0,4:T(8,128)(2,1)S(1)} reshape(bf16[32,16,1024]{2,1,0:T(8,128)(2,1)} %get-tuple-element.11) | data formatting | bytes 2097152 | tf_op jit(solution)/shard_map/reshape | solution.py:68
  124.1 2.3 convert_bitcast_fusion.2
  126.4 6.3 %copy.46 = bf16[16,16,32,4,64]{4,3,2,1,0:T(4,128)(2,1)} copy(bf16[16,16,32,4,64]{4,1,3,0,2:T(8,128)(2,1)S(1)} %convert_bitcast_fusion.2) | data formatting | bytes 8388608 | tf_op jit(solution)/shard_map/convert_element_type | solution.py:71
  132.8 13.6 %reshape.87 = bf16[16,16,8192,1]{2,1,0,3:T(8,128)(2,1)} reshape(bf16[16,16,32,4,64]{4,3,2,1,0:T(4,128)(2,1)} %copy.46) | data formatting | bytes 8388608 | tf_op jit(solution)/shard_map/dot_general | solution.py:74
  146.4 2.9 %reshape.78 = bf16[32,16,16,64,1]{3,2,1,0,4:T(8,128)(2,1)S(1)} reshape(bf16[32,16,1024]{2,1,0:T(8,128)(2,1)} %get-tuple-element.9) | data formatting | bytes 2097152 | tf_op jit(solution)/shard_map/reshape | solution.py:68
  149.3 2.3 convert_bitcast_fusion.3
  151.6 6.3 %copy.42 = bf16[16,16,32,4,64]{4,3,2,1,0:T(4,128)(2,1)} copy(bf16[16,16,32,4,64]{4,1,3,0,2:T(8,128)(2,1)S(1)} %convert_bitcast_fusion.3) | data formatting | bytes 8388608 | tf_op jit(solution)/shard_map/convert_element_type | solution.py:71
  158.0 13.7 %reshape.83 = bf16[16,16,8192,1]{2,1,0,3:T(8,128)(2,1)} reshape(bf16[16,16,32,4,64]{4,3,2,1,0:T(4,128)(2,1)} %copy.42) | data formatting | bytes 8388608 | tf_op jit(solution)/shard_map/dot_general | solution.py:74
  171.6 9.3 %all-to-all-start.1 = ((bf16[32,16,1024]{2,1,0:T(8,128)(2,1)}), bf16[32,16,1024]{2,1,0:T(8,128)(2,1)}, u32[]{:S(2)}, u32[]{:S(2)}) async-start(bf16[32,16,1024]{2,1,0:T(8,128)(2,1)} %bitcast_convert_fusion.2), calls=%async_computation.1 | async-start | bytes 2097152 | tf_op jit(solution)/shard_map/all_to_all | solution.py:101
  180.9 5.9 %fusion.31 = bf16[4,16,16,64]{3,2,0,1:T(8,128)(2,1)S(1)} fusion(bf16[4,64,8192,1]{2,1,0,3:T(8,128)(2,1)} %bitcast.118, bf16[16,16,8192,1]{2,1,0,3:T(8,128)(2,1)} %reshape.90), kind=kOutput, calls=%fused_computation.31 | convolution fusion | flops 1073807360 | bytes 8519680 | tf_op jit(solution)/shard_map/dot_general | solution.py:74
  186.9 0.0 copy-done.3
  186.9 0.0 copy-done.4
  186.9 0.0 copy-start.5
  186.9 3.0 %fusion.34 = bf16[4,16,16,64]{3,2,0,1:T(8,128)(2,1)} fusion(bf16[4,64,8192,1]{2,1,0,3:T(8,128)(2,1)S(1)} %bitcast.120, bf16[16,16,8192,1]{2,1,0,3:T(8,128)(2,1)S(1)} %copy-done.4), kind=kOutput, calls=%fused_computation.32 | convolution fusion | flops 1073807360 | bytes 8519680 | tf_op jit(solution)/shard_map/dot_general | solution.py:74
  190.0 3.1 %fusion.37 = bf16[4,16,16,64]{3,2,0,1:T(8,128)(2,1)} fusion(bf16[4,64,8192,1]{2,1,0,3:T(8,128)(2,1)S(1)} %bitcast.121, bf16[16,16,8192,1]{2,1,0,3:T(8,128)(2,1)S(1)} %copy-done.5), kind=kOutput, calls=%fused_computation.33 | convolution fusion | flops 1073807360 | bytes 8519680 | tf_op jit(solution)/shard_map/dot_general | solution.py:74
  193.0 12.5 %all-to-all-done.1 = bf16[32,16,1024]{2,1,0:T(8,128)(2,1)} async-done(((bf16[32,16,1024]{2,1,0:T(8,128)(2,1)}), bf16[32,16,1024]{2,1,0:T(8,128)(2,1)}, u32[]{:S(2)}, u32[]{:S(2)}) %all-to-all-start.1) | async-done | bytes 1048608 | tf_op jit(solution)/shard_map/all_to_all | solution.py:101
  205.5 2.9 %reshape.91 = bf16[32,16,16,64,1]{3,2,1,0,4:T(8,128)(2,1)S(1)} reshape(bf16[32,16,1024]{2,1,0:T(8,128)(2,1)} %all-to-all-done.1) | data formatting | bytes 2097152 | tf_op jit(solution)/shard_map/reshape | solution.py:68
  208.5 2.3 convert_bitcast_fusion
  210.8 6.3 %copy.50 = bf16[16,16,32,4,64]{4,3,2,1,0:T(4,128)(2,1)} copy(bf16[16,16,32,4,64]{4,1,3,0,2:T(8,128)(2,1)S(1)} %convert_bitcast_fusion) | data formatting | bytes 8388608 | tf_op jit(solution)/shard_map/convert_element_type | solution.py:71
  217.1 13.8 %reshape.93 = bf16[16,16,8192,1]{2,1,0,3:T(8,128)(2,1)} reshape(bf16[16,16,32,4,64]{4,3,2,1,0:T(4,128)(2,1)} %copy.50) | data formatting | bytes 8388608 | tf_op jit(solution)/shard_map/dot_general | solution.py:74
  230.9 0.0 copy-start.6
  230.9 0.0 copy-start.7
  231.0 0.0 copy-start.1
  231.0 5.9 %fusion.28 = bf16[4,16,16,64]{3,2,0,1:T(8,128)(2,1)S(1)} fusion(bf16[4,64,8192,1]{2,1,0,3:T(8,128)(2,1)} %bitcast.119, bf16[16,16,8192,1]{2,1,0,3:T(8,128)(2,1)} %reshape.93), kind=kOutput, calls=%fused_computation.30 | convolution fusion | flops 1073807360 | bytes 8519680 | tf_op jit(solution)/shard_map/dot_general | solution.py:74
  236.8 0.0 copy-done.6
  236.9 0.0 copy-done.7
  236.9 0.3 pad_maximum_fusion
  237.1 0.6 convert_element_type.97
  237.8 29.1 %all_to_all.15 = bf16[16,4,4,1024]{3,1,2,0:T(4,128)(2,1)S(1)} all-to-all(bf16[16,4,4,1024]{3,1,2,0:T(4,128)(2,1)S(1)} %bitcast.122), channel_id=1, replica_groups=mesh['op'=16,'sec'=32] {'op'}, dimensions={0} | all-to-all | bytes 1048576 | tf_op jit(solution)/shard_map/all_to_all | solution.py:108
  266.8 0.2 reduce_sum.41
  267.0 0.6 copy.51
  (12 shorter events, 0.1 us)
Async XLA Ops:
  0.0 3.1 %copy-start = (bf16[4,64,1024]{2,1,0:T(8,128)(2,1)S(1)}, bf16[4,64,1024]{2,1,0:T(8,128)(2,1)}, u32[]{:S(2)}) copy-start(bf16[4,64,1024]{2,1,0:T(8,128)(2,1)} %param.6) | copy-start | bytes 1572868
  2.8 17.9 %copy-start.2 = (bf16[32,64,4,64]{3,0,1,2:T(8,128)(2,1)}, bf16[32,64,4,64]{3,0,1,2:T(8,128)(2,1)S(1)}, u32[]{:S(2)}) copy-start(bf16[32,64,4,64]{3,0,1,2:T(8,128)(2,1)S(1)} %convert_bitcast_fusion.4) | copy-start | bytes 3145732
  6.2 14.5 %copy-start.9 = (s32[8,128]{1,0:T(8,128)S(1)}, s32[8,128]{1,0:T(8,128)}, u32[]{:S(2)}) copy-start(s32[8,128]{1,0:T(8,128)} %param.10) | copy-start | bytes 12292
  6.2 14.8 %copy-start.8 = (bf16[8,4,16,16]{3,2,1,0:T(8,128)(2,1)S(1)}, bf16[8,4,16,16]{3,2,1,0:T(8,128)(2,1)}, u32[]{:S(2)}) copy-start(bf16[8,4,16,16]{3,2,1,0:T(8,128)(2,1)} %param.9) | copy-start | bytes 49156
  6.2 16.2 %copy-start.10 = (s32[8,4]{0,1:T(4,128)S(1)}, s32[8,4]{0,1:T(4,128)}, u32[]{:S(2)}) copy-start(s32[8,4]{0,1:T(4,128)} %param.11) | copy-start | bytes 388
  6.2 16.4 %copy-start.11 = (bf16[4,4,64,64]{3,2,1,0:T(8,128)(2,1)S(1)}, bf16[4,4,64,64]{3,2,1,0:T(8,128)(2,1)}, u32[]{:S(2)}) copy-start(bf16[4,4,64,64]{3,2,1,0:T(8,128)(2,1)} %param.8) | copy-start | bytes 393220
  6.2 86.0 %all-to-all-start = ((bf16[32,48,1024]{2,1,0:T(8,128)(2,1)}), bf16[32,48,1024]{2,1,0:T(8,128)(2,1)}, u32[]{:S(2)}, u32[]{:S(2)}) async-start(bf16[32,48,1024]{2,1,0:T(8,128)(2,1)} %bitcast_convert_fusion), calls=%async_computation | async-start | bytes 6291456 | tf_op jit(solution)/shard_map/all_to_all | solution.py:89
  32.2 13.7 %slice-start = ((bf16[32,64,4,64]{3,0,1,2:T(8,128)(2,1)}), bf16[32,16,4,64]{3,0,1,2:T(8,128)(2,1)S(1)}, s32[]{:S(2)}) async-start(bf16[32,64,4,64]{3,0,1,2:T(8,128)(2,1)} %copy-done.2), calls=%async_computation.3 | async-start | bytes 1048576 | tf_op jit(solution)/shard_map/slice | solution.py:34
  171.6 33.9 %all-to-all-start.1 = ((bf16[32,16,1024]{2,1,0:T(8,128)(2,1)}), bf16[32,16,1024]{2,1,0:T(8,128)(2,1)}, u32[]{:S(2)}, u32[]{:S(2)}) async-start(bf16[32,16,1024]{2,1,0:T(8,128)(2,1)} %bitcast_convert_fusion.2), calls=%async_computation.1 | async-start | bytes 2097152 | tf_op jit(solution)/shard_map/all_to_all | solution.py:101
  180.9 6.0 %copy-start.3 = (bf16[8192,256]{0,1:T(8,128)(2,1)S(1)}, bf16[8192,256]{0,1:T(8,128)(2,1)}, u32[]{:S(2)}) copy-start(bf16[8192,256]{0,1:T(8,128)(2,1)} %reshape.69) | copy-start | bytes 12582916
  180.9 6.0 %copy-start.4 = (bf16[16,16,8192,1]{2,1,0,3:T(8,128)(2,1)S(1)}, bf16[16,16,8192,1]{2,1,0,3:T(8,128)(2,1)}, u32[]{:S(2)}) copy-start(bf16[16,16,8192,1]{2,1,0,3:T(8,128)(2,1)} %reshape.87) | copy-start | bytes 12582916
  186.9 3.0 %copy-start.5 = (bf16[16,16,8192,1]{2,1,0,3:T(8,128)(2,1)S(1)}, bf16[16,16,8192,1]{2,1,0,3:T(8,128)(2,1)}, u32[]{:S(2)}) copy-start(bf16[16,16,8192,1]{2,1,0,3:T(8,128)(2,1)} %reshape.83) | copy-start | bytes 12582916
  230.9 5.9 %copy-start.6 = (bf16[4,16,16,64]{3,2,0,1:T(8,128)(2,1)S(1)}, bf16[4,16,16,64]{3,2,0,1:T(8,128)(2,1)}, u32[]{:S(2)}) copy-start(bf16[4,16,16,64]{3,2,0,1:T(8,128)(2,1)} %fusion.34) | copy-start | bytes 393220
  230.9 5.9 %copy-start.7 = (bf16[4,16,16,64]{3,2,0,1:T(8,128)(2,1)S(1)}, bf16[4,16,16,64]{3,2,0,1:T(8,128)(2,1)}, u32[]{:S(2)}) copy-start(bf16[4,16,16,64]{3,2,0,1:T(8,128)(2,1)} %fusion.37) | copy-start | bytes 393220
  231.0 36.7 %copy-start.1 = (bf16[4,64,1024]{2,1,0:T(8,128)(2,1)S(1)}, bf16[4,64,1024]{2,1,0:T(8,128)(2,1)}, u32[]{:S(2)}) copy-start(bf16[4,64,1024]{2,1,0:T(8,128)(2,1)} %param.6) | copy-start | bytes 1572868

commit v10 on v8

--- a/solution.py
+++ b/solution.py
@@ -68,7 +68,8 @@
         mixed = jnp.einsum(
             "itpq,ilqr->itlpr", item_ops, incoming, preferred_element_type=f32
         ).astype(bf16)
-        return jnp.einsum("itlpr,itdmr->dlpm", mixed, sector_env, preferred_element_type=f32)
+        flat = jnp.einsum("itlpr,itdmr->lpdm", mixed, sector_env, preferred_element_type=f32)
+        return flat.transpose(2, 0, 1, 3)
 
     def process(received):
         step = PIECE_ROWS * rows // 64

time: 184 us -> 197 us (1.071)
  matrix products: 46.6 us -> 60.1 us
    dot_general x4, matrix products: 38.9 us -> 52.3 us  [process_piece(): jnp.einsum('itlpr,itdmr->lpdm', mixed, sector_env, preferred_element_type...]
  transfers between devices with their start and end apart: 2 -> 2, of which waited for: 1 -> 1; matrix products, arithmetic and copies ran while one was open for 28% -> 32% of each run, Pallas kernels for 0% -> 0%
where the time goes in v10:
time: 197 us
  waiting for transfers between devices  62.9 us (32%)
  matrix products  60.1 us (31%)
  blocking collectives  25.4 us (13%)
  local copies, waits for them, and re-layouts  23.6 us (12%)
  starting transfers between devices  22.9 us (12%)
    all_to_all x1, waiting for transfers between devices, body(): lax.all_to_all(outgoing(bounds[0], bounds[1]), 'sec', 0, 0, tiled=True)  62.9 us
    dot_general x4, matrix products, process_piece(): jnp.einsum('itlpr,itdmr->lpdm', mixed, sector_env, preferred_element_type...  52.3 us
    all_to_all x1, blocking collectives, body(): gathered = lax.all_to_all(pieces, 'op', 0, 0, tiled=True)  25.4 us
    all_to_all x1, starting transfers between devices, body(): lax.all_to_all(outgoing(bounds[0], bounds[1]), 'sec', 0, 0, tiled=True)  14 us
    reshape x4, local copies, waits for them, and re-layouts, process_piece(): incoming = received.reshape(sec_count, -1, physical, rows)  12.7 us
    all_to_all x1, starting transfers between devices, body(): upcoming = lax.all_to_all(piece, 'sec', 0, 0, tiled=True)  8.92 us
    dot_general x2, matrix products, outgoing(): jnp.einsum('kisj,sjx->kix', chosen_left[:, start:stop], wavefunction, pre...  4.66 us
    another operation x1, local copies, waits for them, and re-layouts  4.37 us
  transfers between devices with their start and end apart: 2, of which 1 were waited for; matrix products, arithmetic and copies ran while one was open for 32% of the time, Pallas kernels for 0%

profile of v10, /device:TPU:1, one launch (start us, length us, event | category | flops | bytes accessed | tf_op | source)
XLA Modules:
  0.0 196.7 jit_solution(8696687873590902192)
XLA Ops:
  0.0 0.0 copy-start
  0.0 0.8 add_select_fusion.3
  0.8 0.1 copy.22
  0.9 1.9 convert_bitcast_fusion
  2.8 0.0 copy-start.1
  2.8 0.3 slice.21
  3.1 0.0 copy-done
  3.1 3.1 %bitcast_convert_fusion = bf16[32,48,1024]{2,1,0:T(8,128)(2,1)} fusion(bf16[32,48,4,64]{3,0,1,2:T(8,128)(2,1)S(1)} %slice.21, bf16[4,64,1024]{2,1,0:T(8,128)(2,1)S(1)} %copy-done), kind=kOutput, calls=%fused_computation.22 | convolution fusion | flops 806879232 | bytes 4456448 | tf_op jit(solution)/shard_map/kisj,sjx->kix/dot_general | solution.py:32
  6.2 0.0 copy-start.4
  6.2 0.0 copy-start.5
  6.2 0.0 copy-start.6
  6.2 14.0 %all-to-all-start = ((bf16[32,48,1024]{2,1,0:T(8,128)(2,1)}), bf16[32,48,1024]{2,1,0:T(8,128)(2,1)}, u32[]{:S(2)}, u32[]{:S(2)}) async-start(bf16[32,48,1024]{2,1,0:T(8,128)(2,1)} %bitcast_convert_fusion), calls=%async_computation | async-start | bytes 6291456 | tf_op jit(solution)/shard_map/all_to_all | solution.py:85
  20.2 0.0 copy-done.4
  20.2 0.1 copy.26
  20.3 0.0 copy-done.1
  20.3 0.1 reduce_sum.39
  20.4 0.1 reduce_sum.40
  20.5 0.1 convert_reduce_fusion
  20.7 0.0 copy-done.5
  20.7 0.1 convolution_convert_fusion.1
  20.8 0.0 copy-done.6
  20.8 0.8 fusion.41
  21.7 0.0 copy-start.3
  21.7 0.0 slice-start
  21.7 4.4 %copy.32 = f32[32,4,64,64]{3,2,1,0:T(8,128)} copy(f32[32,4,64,64]{3,0,2,1:T(8,128)S(1)} %fusion.41) | data formatting | bytes 4194304 | tf_op jit(solution)/shard_map/convert.2
  26.1 0.0 copy-done.3
  26.1 0.3 convolution_convert_fusion
  26.4 0.9 copy.30
  27.3 0.0 slice-done
  27.3 1.5 bitcast_convert_fusion.2
  28.8 62.9 %all-to-all-done = bf16[32,48,1024]{2,1,0:T(8,128)(2,1)} async-done(((bf16[32,48,1024]{2,1,0:T(8,128)(2,1)}), bf16[32,48,1024]{2,1,0:T(8,128)(2,1)}, u32[]{:S(2)}, u32[]{:S(2)}) %all-to-all-start) | async-done | bytes 3145760 | tf_op jit(solution)/shard_map/all_to_all | solution.py:85
  91.7 8.9 %all-to-all-start.1 = ((bf16[32,16,1024]{2,1,0:T(8,128)(2,1)}), bf16[32,16,1024]{2,1,0:T(8,128)(2,1)S(1)}, u32[]{:S(2)}, u32[]{:S(2)}) async-start(bf16[32,16,1024]{2,1,0:T(8,128)(2,1)} %bitcast_convert_fusion.2), calls=%async_computation.1 | async-start | bytes 2097152 | tf_op jit(solution)/shard_map/all_to_all | solution.py:97
  100.6 3.7 %fusion.164 = (bf16[32,16,1024]{2,1,0:T(8,128)(2,1)S(1)}, bf16[32,16,1024]{2,1,0:T(8,128)(2,1)}, bf16[32,16,1024]{2,1,0:T(8,128)(2,1)}) fusion(bf16[32,48,1024]{2,1,0:T(8,128)(2,1)} %all-to-all-done), kind=kLoop, calls=%fused_computation.103 | loop fusion | bytes 6291456 | tf_op jit(solution)/shard_map/slice | solution.py:78
  104.4 4.0 %reshape.47 = bf16[32,16,16,64]{3,2,1,0:T(8,128)(2,1)} reshape(bf16[32,16,1024]{2,1,0:T(8,128)(2,1)} %get-tuple-element.10) | data formatting | bytes 2097152 | tf_op jit(solution)/shard_map/reshape | solution.py:67
  108.4 4.1 %reshape.46 = bf16[32,16,16,64]{3,2,1,0:T(8,128)(2,1)} reshape(bf16[32,16,1024]{2,1,0:T(8,128)(2,1)} %get-tuple-element.11) | data formatting | bytes 2097152 | tf_op jit(solution)/shard_map/reshape | solution.py:67
  112.4 12.9 %fusion.113 = bf16[4,16,16,64]{3,2,0,1:T(8,128)(2,1)S(1)} fusion(f32[32,4,64,64]{3,2,1,0:T(8,128)} %copy.32, f32[32,4]{0,1:T(4,128)S(1)} %get-tuple-element.12, bf16[32,4,16,16]{3,2,1,0:T(8,128)(2,1)S(1)} %copy.30, bf16[32,16,16,64]{3,2,1,0:T(8,128)(2,1)} %reshape.47), kind=kOutput, calls=%fused_computation.47 | convolution fusion | flops 1147207680 | bytes 3342848 | tf_op jit(solution)/shard_map/itlpr,itdmr->lpdm/dot_general | solution.py:71
  125.4 13.6 %fusion.106 = bf16[4,16,16,64]{3,2,0,1:T(8,128)(2,1)} fusion(f32[32,4,64,64]{3,2,1,0:T(8,128)} %copy.32, f32[32,4]{0,1:T(4,128)S(1)} %get-tuple-element.12, bf16[32,4,16,16]{3,2,1,0:T(8,128)(2,1)S(1)} %copy.30, bf16[32,16,16,64]{3,2,1,0:T(8,128)(2,1)} %reshape.46), kind=kOutput, calls=%fused_computation.46 | convolution fusion | flops 1147207680 | bytes 3342848 | tf_op jit(solution)/shard_map/itlpr,itdmr->lpdm/dot_general | solution.py:71
  138.9 2.3 %reshape.44 = bf16[32,16,16,64]{3,2,1,0:T(8,128)(2,1)} reshape(bf16[32,16,1024]{2,1,0:T(8,128)(2,1)S(1)} %get-tuple-element.9) | data formatting | bytes 2097152 | tf_op jit(solution)/shard_map/reshape | solution.py:67
  141.2 12.9 %fusion.99 = bf16[4,16,16,64]{3,2,0,1:T(8,128)(2,1)S(1)} fusion(f32[32,4,64,64]{3,2,1,0:T(8,128)} %copy.32, f32[32,4]{0,1:T(4,128)S(1)} %get-tuple-element.12, bf16[32,4,16,16]{3,2,1,0:T(8,128)(2,1)S(1)} %copy.30, bf16[32,16,16,64]{3,2,1,0:T(8,128)(2,1)} %reshape.44), kind=kOutput, calls=%fused_computation.45 | convolution fusion | flops 1147207680 | bytes 3342848 | tf_op jit(solution)/shard_map/itlpr,itdmr->lpdm/dot_general | solution.py:71
  154.2 0.0 all-to-all-done.1
  154.2 2.3 %reshape.48 = bf16[32,16,16,64]{3,2,1,0:T(8,128)(2,1)} reshape(bf16[32,16,1024]{2,1,0:T(8,128)(2,1)S(1)} %all-to-all-done.1) | data formatting | bytes 2097152 | tf_op jit(solution)/shard_map/reshape | solution.py:67
  156.5 0.0 copy-start.2
  156.5 12.9 %fusion.120 = bf16[4,16,16,64]{3,2,0,1:T(8,128)(2,1)S(1)} fusion(f32[32,4,64,64]{3,2,1,0:T(8,128)} %copy.32, f32[32,4]{0,1:T(4,128)S(1)} %get-tuple-element.12, bf16[32,4,16,16]{3,2,1,0:T(8,128)(2,1)S(1)} %copy.30, bf16[32,16,16,64]{3,2,1,0:T(8,128)(2,1)} %reshape.48), kind=kOutput, calls=%fused_computation.48 | convolution fusion | flops 1147207680 | bytes 3342848 | tf_op jit(solution)/shard_map/itlpr,itdmr->lpdm/dot_general | solution.py:71
  169.5 0.0 copy-done.2
  169.5 0.3 pad_maximum_fusion
  169.7 0.6 convert_element_type.92
  170.4 25.4 %all_to_all.15 = bf16[16,4,4,1024]{3,1,2,0:T(4,128)(2,1)S(1)} all-to-all(bf16[16,4,4,1024]{3,1,2,0:T(4,128)(2,1)S(1)} %bitcast.200), channel_id=1, replica_groups=mesh['op'=16,'sec'=32] {'op'}, dimensions={0} | all-to-all | bytes 1048576 | tf_op jit(solution)/shard_map/all_to_all | solution.py:104
  195.8 0.2 reduce_sum.41
  196.0 0.6 copy.39
  (3 shorter events, 0.0 us)
Async XLA Ops:
  0.0 3.1 %copy-start = (bf16[4,64,1024]{2,1,0:T(8,128)(2,1)S(1)}, bf16[4,64,1024]{2,1,0:T(8,128)(2,1)}, u32[]{:S(2)}) copy-start(bf16[4,64,1024]{2,1,0:T(8,128)(2,1)} %param.6) | copy-start | bytes 1572868
  2.8 17.5 %copy-start.1 = (bf16[32,64,4,64]{3,0,1,2:T(8,128)(2,1)}, bf16[32,64,4,64]{3,0,1,2:T(8,128)(2,1)S(1)}, u32[]{:S(2)}) copy-start(bf16[32,64,4,64]{3,0,1,2:T(8,128)(2,1)S(1)} %convert_bitcast_fusion) | copy-start | bytes 3145732
  6.2 14.0 %copy-start.4 = (s32[8,128]{1,0:T(8,128)S(1)}, s32[8,128]{1,0:T(8,128)}, u32[]{:S(2)}) copy-start(s32[8,128]{1,0:T(8,128)} %param.10) | copy-start | bytes 12292
  6.2 14.5 %copy-start.5 = (s32[8,4]{0,1:T(4,128)S(1)}, s32[8,4]{0,1:T(4,128)}, u32[]{:S(2)}) copy-start(s32[8,4]{0,1:T(4,128)} %param.11) | copy-start | bytes 388
  6.2 14.6 %copy-start.6 = (bf16[4,4,64,64]{3,2,1,0:T(8,128)(2,1)S(1)}, bf16[4,4,64,64]{3,2,1,0:T(8,128)(2,1)}, u32[]{:S(2)}) copy-start(bf16[4,4,64,64]{3,2,1,0:T(8,128)(2,1)} %param.8) | copy-start | bytes 393220
  6.2 85.5 %all-to-all-start = ((bf16[32,48,1024]{2,1,0:T(8,128)(2,1)}), bf16[32,48,1024]{2,1,0:T(8,128)(2,1)}, u32[]{:S(2)}, u32[]{:S(2)}) async-start(bf16[32,48,1024]{2,1,0:T(8,128)(2,1)} %bitcast_convert_fusion), calls=%async_computation | async-start | bytes 6291456 | tf_op jit(solution)/shard_map/all_to_all | solution.py:85
  21.7 4.4 %copy-start.3 = (bf16[8,4,16,16]{3,2,1,0:T(8,128)(2,1)S(1)}, bf16[8,4,16,16]{3,2,1,0:T(8,128)(2,1)}, u32[]{:S(2)}) copy-start(bf16[8,4,16,16]{3,2,1,0:T(8,128)(2,1)} %param.9) | copy-start | bytes 49156
  21.7 5.6 %slice-start = ((bf16[32,64,4,64]{3,0,1,2:T(8,128)(2,1)}), bf16[32,16,4,64]{3,0,1,2:T(8,128)(2,1)S(1)}, s32[]{:S(2)}) async-start(bf16[32,64,4,64]{3,0,1,2:T(8,128)(2,1)} %copy-done.1), calls=%async_computation.3 | async-start | bytes 1048576 | tf_op jit(solution)/shard_map/slice | solution.py:34
  91.7 62.5 %all-to-all-start.1 = ((bf16[32,16,1024]{2,1,0:T(8,128)(2,1)}), bf16[32,16,1024]{2,1,0:T(8,128)(2,1)S(1)}, u32[]{:S(2)}, u32[]{:S(2)}) async-start(bf16[32,16,1024]{2,1,0:T(8,128)(2,1)} %bitcast_convert_fusion.2), calls=%async_computation.1 | async-start | bytes 2097152 | tf_op jit(solution)/shard_map/all_to_all | solution.py:97
  156.5 13.0 %copy-start.2 = (bf16[4,16,16,64]{3,2,0,1:T(8,128)(2,1)S(1)}, bf16[4,16,16,64]{3,2,0,1:T(8,128)(2,1)}, u32[]{:S(2)}) copy-start(bf16[4,16,16,64]{3,2,0,1:T(8,128)(2,1)} %fusion.106) | copy-start | bytes 393220

commit v11 on v8

--- a/solution.py
+++ b/solution.py
@@ -63,8 +63,7 @@
     for size in CHUNK_ROWS:
         bounds.append(bounds[-1] + size * rows // 64)
 
-    def process_piece(received):
-        incoming = received.reshape(sec_count, -1, physical, rows)
+    def process_piece(incoming):
         mixed = jnp.einsum(
             "itpq,ilqr->itlpr", item_ops, incoming, preferred_element_type=f32
         ).astype(bf16)
@@ -72,10 +71,11 @@
 
     def process(received):
         step = PIECE_ROWS * rows // 64
+        incoming = received.reshape(sec_count, -1, physical, rows)
         return jnp.concatenate(
             [
-                process_piece(received[:, start:start + step])
-                for start in range(0, received.shape[1], step)
+                process_piece(incoming[:, start:start + step])
+                for start in range(0, incoming.shape[1], step)
             ],
             axis=1,
         )

time: 184 us -> 204 us (1.11)
  waiting for transfers between devices: 62.9 us -> 77.9 us
  blocking collectives: 25.5 us -> 29.4 us
    all_to_all x1, waiting for transfers between devices: 0.01 us -> 15.1 us  [body(): upcoming = lax.all_to_all(piece, 'sec', 0, 0, tiled=True)]
    all_to_all x1, blocking collectives: 25.5 us -> 29.4 us  [body(): gathered = lax.all_to_all(pieces, 'op', 0, 0, tiled=True)]
    slice x1, local copies, waits for them, and re-layouts: 3.75 us -> 6.61 us  [process(): incoming[:, start:start + step]]
    reshape x4 -> x2, local copies, waits for them, and re-layouts: 12.7 us -> 11.5 us  [process(): incoming = received.reshape(sec_count, -1, physical, rows)]
  transfers between devices with their start and end apart: 2 -> 2, of which waited for: 1 -> 2; matrix products, arithmetic and copies ran while one was open for 28% -> 9% of each run, Pallas kernels for 0% -> 0%
where the time goes in v11:
time: 204 us; the launch traced here: 203 us
  waiting for transfers between devices  77.9 us (38%)
  matrix products  45.9 us (22%)
  blocking collectives  29.4 us (14%)
  local copies, waits for them, and re-layouts  24.9 us (12%)
  starting transfers between devices  22.9 us (11%)
  other arithmetic  2.2 us (1%)
    all_to_all x1, waiting for transfers between devices, body(): lax.all_to_all(outgoing(bounds[0], bounds[1]), 'sec', 0, 0, tiled=True)  62.8 us
    dot_general x4, matrix products, process_piece(): jnp.einsum('itlpr,itdmr->dlpm', mixed, sector_env, preferred_element_type...  38.2 us
    all_to_all x1, blocking collectives, body(): gathered = lax.all_to_all(pieces, 'op', 0, 0, tiled=True)  29.4 us
    all_to_all x1, waiting for transfers between devices, body(): upcoming = lax.all_to_all(piece, 'sec', 0, 0, tiled=True)  15.1 us
    all_to_all x1, starting transfers between devices, body(): lax.all_to_all(outgoing(bounds[0], bounds[1]), 'sec', 0, 0, tiled=True)  14 us
    reshape x2, local copies, waits for them, and re-layouts, process(): incoming = received.reshape(sec_count, -1, physical, rows)  11.5 us
    all_to_all x1, starting transfers between devices, body(): upcoming = lax.all_to_all(piece, 'sec', 0, 0, tiled=True)  8.98 us
    slice x1, local copies, waits for them, and re-layouts, process(): incoming[:, start:start + step]  6.61 us
  transfers between devices with their start and end apart: 2, of which 2 were waited for; matrix products, arithmetic and copies ran while one was open for 9% of the time, Pallas kernels for 0%

profile of v11, /device:TPU:1, one launch (start us, length us, event | category | flops | bytes accessed | tf_op | source)
XLA Modules:
  0.0 203.4 jit_solution(8587082482334329447)
XLA Ops:
  0.0 0.0 copy-start
  0.0 0.8 add_select_fusion.1
  0.8 0.1 copy.25
  0.9 1.9 convert_bitcast_fusion
  2.8 0.0 copy-start.1
  2.8 0.3 slice.21
  3.1 0.0 copy-done
  3.1 3.1 %bitcast_convert_fusion = bf16[32,48,1024]{2,1,0:T(8,128)(2,1)} fusion(bf16[32,48,4,64]{3,0,1,2:T(8,128)(2,1)S(1)} %slice.21, bf16[4,64,1024]{2,1,0:T(8,128)(2,1)S(1)} %copy-done), kind=kOutput, calls=%fused_computation.22 | convolution fusion | flops 806879232 | bytes 4456448 | tf_op jit(solution)/shard_map/kisj,sjx->kix/dot_general | solution.py:32
  6.1 0.0 copy-start.4
  6.2 0.0 copy-start.5
  6.2 0.0 copy-start.6
  6.2 14.0 %all-to-all-start = ((bf16[32,48,1024]{2,1,0:T(8,128)(2,1)}), bf16[32,48,1024]{2,1,0:T(8,128)(2,1)}, u32[]{:S(2)}, u32[]{:S(2)}) async-start(bf16[32,48,1024]{2,1,0:T(8,128)(2,1)} %bitcast_convert_fusion), calls=%async_computation | async-start | bytes 6291456 | tf_op jit(solution)/shard_map/all_to_all | solution.py:84
  20.1 0.0 copy-done.1
  20.1 0.0 copy-done.4
  20.1 0.1 copy.22
  20.3 0.1 reduce_sum.38
  20.4 0.1 reduce_sum.39
  20.5 0.1 convert_reduce_fusion
  20.6 0.0 copy-done.5
  20.7 0.1 convolution_convert_fusion.1
  20.8 0.0 copy-done.6
  20.8 0.8 fusion.35
  21.6 0.0 copy-start.3
  21.6 0.0 slice-start
  21.7 4.4 %copy.24 = f32[32,4,64,64]{3,2,1,0:T(8,128)} copy(f32[32,4,64,64]{3,0,2,1:T(8,128)S(1)} %fusion.35) | data formatting | bytes 4194304 | tf_op jit(solution)/shard_map/convert.2
  26.1 0.0 copy-done.3
  26.1 0.3 convolution_convert_fusion
  26.4 0.9 copy.32
  27.3 0.0 slice-done
  27.3 1.5 bitcast_convert_fusion.2
  28.8 62.8 %all-to-all-done = bf16[32,48,1024]{2,1,0:T(8,128)(2,1)} async-done(((bf16[32,48,1024]{2,1,0:T(8,128)(2,1)}), bf16[32,48,1024]{2,1,0:T(8,128)(2,1)}, u32[]{:S(2)}, u32[]{:S(2)}) %all-to-all-start) | async-done | bytes 3145760 | tf_op jit(solution)/shard_map/all_to_all | solution.py:84
  91.6 9.2 %reshape.39 = bf16[32,48,16,64]{3,2,1,0:T(8,128)(2,1)} reshape(bf16[32,48,1024]{2,1,0:T(8,128)(2,1)} %all-to-all-done) | data formatting | bytes 6291456 | tf_op jit(solution)/shard_map/reshape | solution.py:74
  100.8 6.6 %fusion.140 = (bf16[32,16,16,64]{3,2,1,0:T(8,128)(2,1)}, bf16[32,16,16,64]{3,2,1,0:T(8,128)(2,1)S(1)}, bf16[32,16,16,64]{3,2,1,0:T(8,128)(2,1)}) fusion(bf16[32,48,16,64]{3,2,1,0:T(8,128)(2,1)} %reshape.39), kind=kLoop, calls=%fused_computation.104 | loop fusion | bytes 6291456 | tf_op jit(solution)/shard_map/slice | solution.py:77
  107.4 9.5 %fusion.81 = bf16[4,16,16,64]{3,2,1,0:T(8,128)(2,1)S(1)} fusion(bf16[32,16,16,64]{3,2,1,0:T(8,128)(2,1)} %get-tuple-element.9, f32[32,4,64,64]{3,2,1,0:T(8,128)} %copy.24, f32[32,4]{0,1:T(4,128)S(1)} %get-tuple-element.12, bf16[32,4,16,16]{3,2,1,0:T(8,128)(2,1)S(1)} %copy.32), kind=kOutput, calls=%fused_computation.45 | convolution fusion | flops 1147207680 | bytes 3342848 | tf_op jit(solution)/shard_map/itlpr,itdmr->dlpm/dot_general | solution.py:70
  116.9 9.6 %fusion.86 = bf16[4,16,16,64]{3,2,1,0:T(8,128)(2,1)} fusion(bf16[32,16,16,64]{3,2,1,0:T(8,128)(2,1)S(1)} %get-tuple-element.10, f32[32,4,64,64]{3,2,1,0:T(8,128)} %copy.24, f32[32,4]{0,1:T(4,128)S(1)} %get-tuple-element.12, bf16[32,4,16,16]{3,2,1,0:T(8,128)(2,1)S(1)} %copy.32), kind=kOutput, calls=%fused_computation.46 | convolution fusion | flops 1147207680 | bytes 3342848 | tf_op jit(solution)/shard_map/itlpr,itdmr->dlpm/dot_general | solution.py:70
  126.5 9.0 %all-to-all-start.1 = ((bf16[32,16,1024]{2,1,0:T(8,128)(2,1)}), bf16[32,16,1024]{2,1,0:T(8,128)(2,1)S(1)}, u32[]{:S(2)}, u32[]{:S(2)}) async-start(bf16[32,16,1024]{2,1,0:T(8,128)(2,1)} %bitcast_convert_fusion.2), calls=%async_computation.1 | async-start | bytes 2097152 | tf_op jit(solution)/shard_map/all_to_all | solution.py:96
  135.5 9.5 %fusion.91 = bf16[4,16,16,64]{3,2,1,0:T(8,128)(2,1)S(1)} fusion(bf16[32,16,16,64]{3,2,1,0:T(8,128)(2,1)} %get-tuple-element.11, f32[32,4,64,64]{3,2,1,0:T(8,128)} %copy.24, f32[32,4]{0,1:T(4,128)S(1)} %get-tuple-element.12, bf16[32,4,16,16]{3,2,1,0:T(8,128)(2,1)S(1)} %copy.32), kind=kOutput, calls=%fused_computation.47 | convolution fusion | flops 1147207680 | bytes 3342848 | tf_op jit(solution)/shard_map/itlpr,itdmr->dlpm/dot_general | solution.py:70
  145.0 15.1 %all-to-all-done.1 = bf16[32,16,1024]{2,1,0:T(8,128)(2,1)S(1)} async-done(((bf16[32,16,1024]{2,1,0:T(8,128)(2,1)}), bf16[32,16,1024]{2,1,0:T(8,128)(2,1)S(1)}, u32[]{:S(2)}, u32[]{:S(2)}) %all-to-all-start.1) | async-done | bytes 1048608 | tf_op jit(solution)/shard_map/all_to_all | solution.py:96
  160.1 2.3 %reshape.40 = bf16[32,16,16,64]{3,2,1,0:T(8,128)(2,1)} reshape(bf16[32,16,1024]{2,1,0:T(8,128)(2,1)S(1)} %all-to-all-done.1) | data formatting | bytes 2097152 | tf_op jit(solution)/shard_map/reshape | solution.py:74
  162.5 0.0 copy-start.2
  162.5 9.6 %fusion.96 = bf16[4,16,16,64]{3,2,1,0:T(8,128)(2,1)S(1)} fusion(f32[32,4,64,64]{3,2,1,0:T(8,128)} %copy.24, f32[32,4]{0,1:T(4,128)S(1)} %get-tuple-element.12, bf16[32,4,16,16]{3,2,1,0:T(8,128)(2,1)S(1)} %copy.32, bf16[32,16,16,64]{3,2,1,0:T(8,128)(2,1)} %reshape.40), kind=kOutput, calls=%fused_computation.48 | convolution fusion | flops 1147207680 | bytes 3342848 | tf_op jit(solution)/shard_map/itlpr,itdmr->dlpm/dot_general | solution.py:70
  172.0 0.0 copy-done.2
  172.1 0.3 pad_maximum_fusion
  172.3 0.6 convert_element_type.92
  172.9 0.2 copy.110
  173.2 29.4 %all_to_all.15 = bf16[16,4,4,1024]{3,2,1,0:T(4,128)(2,1)S(1)} all-to-all(bf16[16,4,4,1024]{3,2,1,0:T(4,128)(2,1)S(1)} %bitcast.215), channel_id=1, replica_groups=mesh['op'=16,'sec'=32] {'op'}, dimensions={0} | all-to-all | bytes 1048576 | tf_op jit(solution)/shard_map/all_to_all | solution.py:103
  202.5 0.8 reduce_sum.41
  (3 shorter events, 0.0 us)
Async XLA Ops:
  0.0 3.1 %copy-start = (bf16[4,64,1024]{2,1,0:T(8,128)(2,1)S(1)}, bf16[4,64,1024]{2,1,0:T(8,128)(2,1)}, u32[]{:S(2)}) copy-start(bf16[4,64,1024]{2,1,0:T(8,128)(2,1)} %param.6) | copy-start | bytes 1572868
  2.8 17.4 %copy-start.1 = (bf16[32,64,4,64]{3,0,1,2:T(8,128)(2,1)}, bf16[32,64,4,64]{3,0,1,2:T(8,128)(2,1)S(1)}, u32[]{:S(2)}) copy-start(bf16[32,64,4,64]{3,0,1,2:T(8,128)(2,1)S(1)} %convert_bitcast_fusion) | copy-start | bytes 3145732
  6.1 14.0 %copy-start.4 = (s32[8,128]{1,0:T(8,128)S(1)}, s32[8,128]{1,0:T(8,128)}, u32[]{:S(2)}) copy-start(s32[8,128]{1,0:T(8,128)} %param.10) | copy-start | bytes 12292
  6.2 14.5 %copy-start.5 = (s32[8,4]{0,1:T(4,128)S(1)}, s32[8,4]{0,1:T(4,128)}, u32[]{:S(2)}) copy-start(s32[8,4]{0,1:T(4,128)} %param.11) | copy-start | bytes 388
  6.2 14.6 %copy-start.6 = (bf16[4,4,64,64]{3,2,1,0:T(8,128)(2,1)S(1)}, bf16[4,4,64,64]{3,2,1,0:T(8,128)(2,1)}, u32[]{:S(2)}) copy-start(bf16[4,4,64,64]{3,2,1,0:T(8,128)(2,1)} %param.8) | copy-start | bytes 393220
  6.2 85.5 %all-to-all-start = ((bf16[32,48,1024]{2,1,0:T(8,128)(2,1)}), bf16[32,48,1024]{2,1,0:T(8,128)(2,1)}, u32[]{:S(2)}, u32[]{:S(2)}) async-start(bf16[32,48,1024]{2,1,0:T(8,128)(2,1)} %bitcast_convert_fusion), calls=%async_computation | async-start | bytes 6291456 | tf_op jit(solution)/shard_map/all_to_all | solution.py:84
  21.6 4.5 %copy-start.3 = (bf16[8,4,16,16]{3,2,1,0:T(8,128)(2,1)S(1)}, bf16[8,4,16,16]{3,2,1,0:T(8,128)(2,1)}, u32[]{:S(2)}) copy-start(bf16[8,4,16,16]{3,2,1,0:T(8,128)(2,1)} %param.9) | copy-start | bytes 49156
  21.6 5.7 %slice-start = ((bf16[32,64,4,64]{3,0,1,2:T(8,128)(2,1)}), bf16[32,16,4,64]{3,0,1,2:T(8,128)(2,1)S(1)}, s32[]{:S(2)}) async-start(bf16[32,64,4,64]{3,0,1,2:T(8,128)(2,1)} %copy-done.1), calls=%async_computation.3 | async-start | bytes 1048576 | tf_op jit(solution)/shard_map/slice | solution.py:34
  126.5 33.6 %all-to-all-start.1 = ((bf16[32,16,1024]{2,1,0:T(8,128)(2,1)}), bf16[32,16,1024]{2,1,0:T(8,128)(2,1)S(1)}, u32[]{:S(2)}, u32[]{:S(2)}) async-start(bf16[32,16,1024]{2,1,0:T(8,128)(2,1)} %bitcast_convert_fusion.2), calls=%async_computation.1 | async-start | bytes 2097152 | tf_op jit(solution)/shard_map/all_to_all | solution.py:96
  162.5 9.6 %copy-start.2 = (bf16[4,16,16,64]{3,2,1,0:T(8,128)(2,1)S(1)}, bf16[4,16,16,64]{3,2,1,0:T(8,128)(2,1)}, u32[]{:S(2)}) copy-start(bf16[4,16,16,64]{3,2,1,0:T(8,128)(2,1)} %fusion.86) | copy-start | bytes 393220

commit v12 on v8

--- a/solution.py
+++ b/solution.py
@@ -5,7 +5,7 @@
 
 
 CHUNK_ROWS = (48, 16)
-PIECE_ROWS = 16
+PIECE_ROWS = 48
 
 
 def body(wavefunction, left_env, right_env, local_ops, dest_sector, right_bond):

time: 184 us -> 183 us (level)
  local copies, waits for them, and re-layouts: 23.2 us -> 20.7 us
  matrix products: 46.6 us -> 48.6 us
    dot_general x0 -> x2, matrix products: none -> 16.1 us  [process_piece(): jnp.einsum('itpq,ilqr->itlpr', item_ops, incoming, preferred_element_type...]
    dot_general x4 -> x2, matrix products: 38.9 us -> 24.8 us  [process_piece(): jnp.einsum('itlpr,itdmr->dlpm', mixed, sector_env, preferred_element_type...]
    slice x1 -> x0, local copies, waits for them, and re-layouts: 3.75 us -> none  [process(): received[:, start:start + step]]
    reshape x4 -> x2, local copies, waits for them, and re-layouts: 12.7 us -> 12.4 us  [process_piece(): incoming = received.reshape(sec_count, -1, physical, rows)]
  transfers between devices with their start and end apart: 2 -> 2, of which waited for: 1 -> 1; matrix products, arithmetic and copies ran while one was open for 28% -> 24% of each run, Pallas kernels for 0% -> 0%
where the time goes in v12:
time: 183 us; the launch traced here: 182 us
  waiting for transfers between devices  62 us (34%)
  matrix products  48.6 us (27%)
  blocking collectives  25.5 us (14%)
  starting transfers between devices  23 us (13%)
  local copies, waits for them, and re-layouts  20.7 us (11%)
  other arithmetic  2.23 us (1%)
    all_to_all x1, waiting for transfers between devices, body(): lax.all_to_all(outgoing(bounds[0], bounds[1]), 'sec', 0, 0, tiled=True)  62 us
    all_to_all x1, blocking collectives, body(): gathered = lax.all_to_all(pieces, 'op', 0, 0, tiled=True)  25.5 us
    dot_general x2, matrix products, process_piece(): jnp.einsum('itlpr,itdmr->dlpm', mixed, sector_env, preferred_element_type...  24.8 us
    dot_general x2, matrix products, process_piece(): jnp.einsum('itpq,ilqr->itlpr', item_ops, incoming, preferred_element_type...  16.1 us
    all_to_all x1, starting transfers between devices, body(): lax.all_to_all(outgoing(bounds[0], bounds[1]), 'sec', 0, 0, tiled=True)  14 us
    reshape x2, local copies, waits for them, and re-layouts, process_piece(): incoming = received.reshape(sec_count, -1, physical, rows)  12.4 us
    all_to_all x1, starting transfers between devices, body(): upcoming = lax.all_to_all(piece, 'sec', 0, 0, tiled=True)  9.05 us
    dot_general x2, matrix products, outgoing(): jnp.einsum('kisj,sjx->kix', chosen_left[:, start:stop], wavefunction, pre...  4.61 us
  transfers between devices with their start and end apart: 2, of which 1 were waited for; matrix products, arithmetic and copies ran while one was open for 24% of the time, Pallas kernels for 0%

profile of v12, /device:TPU:1, one launch (start us, length us, event | category | flops | bytes accessed | tf_op | source)
XLA Modules:
  0.0 182.2 jit_solution(1000023371029830953)
XLA Ops:
  0.0 0.0 copy-start
  0.0 0.8 add_select_fusion.1
  0.8 0.1 copy.28
  0.9 1.9 %convert_bitcast_fusion.2 = bf16[32,64,4,64]{3,0,1,2:T(8,128)(2,1)S(1)} fusion(bf16[8,4,64,64]{3,2,1,0:T(8,128)(2,1)} %param.7, s32[8,4]{0,1:T(4,128)S(1)} %copy.28), kind=kOutput, calls=%fused_computation.18 | convolution fusion | flops 8913920 | bytes 1310848 | tf_op jit(solution)/shard_map/ask,asij->kisj/dot_general | solution.py:27
  2.8 0.0 copy-start.2
  2.8 0.3 slice.9
  3.1 0.0 copy-done
  3.1 3.1 %bitcast_convert_fusion = bf16[32,48,1024]{2,1,0:T(8,128)(2,1)} fusion(bf16[32,48,4,64]{3,0,1,2:T(8,128)(2,1)S(1)} %slice.9, bf16[4,64,1024]{2,1,0:T(8,128)(2,1)S(1)} %copy-done), kind=kOutput, calls=%fused_computation.14 | convolution fusion | flops 806879232 | bytes 4456448 | tf_op jit(solution)/shard_map/kisj,sjx->kix/dot_general | solution.py:32
  6.2 0.0 copy-start.7
  6.2 0.0 copy-start.6
  6.2 0.0 copy-start.8
  6.2 0.0 copy-start.9
  6.2 14.0 %all-to-all-start = ((bf16[32,48,1024]{2,1,0:T(8,128)(2,1)}), bf16[32,48,1024]{2,1,0:T(8,128)(2,1)}, u32[]{:S(2)}, u32[]{:S(2)}) async-start(bf16[32,48,1024]{2,1,0:T(8,128)(2,1)} %bitcast_convert_fusion), calls=%async_computation | async-start | bytes 6291456 | tf_op jit(solution)/shard_map/all_to_all | solution.py:84
  20.2 0.0 copy-done.2
  20.2 0.0 copy-done.7
  20.2 0.1 copy.25
  20.3 0.1 convert_reduce_fusion
  20.4 0.0 copy-done.6
  20.4 0.3 convolution_convert_fusion
  20.7 0.9 copy.37
  21.6 0.9 copy.48
  22.5 0.1 reduce_sum.38
  22.6 0.1 reduce_sum.39
  22.8 0.0 copy-done.8
  22.8 0.1 convolution_convert_fusion.1
  22.9 0.0 copy-done.9
  22.9 0.8 fusion.14
  23.8 0.0 slice-start
  23.8 4.4 %copy.27 = f32[32,4,64,64]{3,2,1,0:T(8,128)} copy(f32[32,4,64,64]{3,0,2,1:T(8,128)S(1)} %fusion.14) | data formatting | bytes 4194304 | tf_op jit(solution)/shard_map/convert.2
  28.2 0.0 slice-done
  28.2 1.5 bitcast_convert_fusion.2
  29.7 62.0 %all-to-all-done = bf16[32,48,1024]{2,1,0:T(8,128)(2,1)} async-done(((bf16[32,48,1024]{2,1,0:T(8,128)(2,1)}), bf16[32,48,1024]{2,1,0:T(8,128)(2,1)}, u32[]{:S(2)}, u32[]{:S(2)}) %all-to-all-start) | async-done | bytes 3145760 | tf_op jit(solution)/shard_map/all_to_all | solution.py:84
  91.7 9.2 %reshape.49 = bf16[32,48,16,64,1]{3,2,1,0,4:T(8,128)(2,1)} reshape(bf16[32,48,1024]{2,1,0:T(8,128)(2,1)} %all-to-all-done) | data formatting | bytes 6291456 | tf_op jit(solution)/shard_map/reshape | solution.py:67
  100.9 9.0 %all-to-all-start.1 = ((bf16[32,16,1024]{2,1,0:T(8,128)(2,1)}), bf16[32,16,1024]{2,1,0:T(8,128)(2,1)}, u32[]{:S(2)}, u32[]{:S(2)}) async-start(bf16[32,16,1024]{2,1,0:T(8,128)(2,1)} %bitcast_convert_fusion.2), calls=%async_computation.1 | async-start | bytes 2097152 | tf_op jit(solution)/shard_map/all_to_all | solution.py:96
  109.9 0.0 copy-start.3
  109.9 13.8 %convert_bitcast_fusion = bf16[32,4,48,16,64]{4,3,1,2,0:T(8,128)(2,1)} fusion(bf16[32,4,16,16,1]{3,2,1,4,0:T(8,128)(2,1)S(1)} %copy.48, bf16[32,48,16,64,1]{3,2,1,0,4:T(8,128)(2,1)} %reshape.49), kind=kOutput, calls=%fused_computation.3 | convolution fusion | flops 207618048 | bytes 15794176 | tf_op jit(solution)/shard_map/itpq,ilqr->itlpr/dot_general | solution.py:68
  123.7 0.0 copy-done.3
  123.7 19.8 %fusion.20 = bf16[4,48,16,64]{3,1,2,0:T(8,128)(2,1)} fusion(bf16[32,4,48,16,64]{4,3,1,2,0:T(8,128)(2,1)} %convert_bitcast_fusion, f32[32,4,64,64]{3,2,1,0:T(8,128)S(1)} %copy-done.3, f32[32,4]{0,1:T(4,128)S(1)} %get-tuple-element.9), kind=kOutput, calls=%fused_computation.22 | convolution fusion | flops 3225616384 | bytes 15073792 | tf_op jit(solution)/shard_map/itlpr,itdmr->dlpm/dot_general | solution.py:71
  143.5 0.0 all-to-all-done.1
  143.5 3.2 %reshape.40 = bf16[32,16,16,64]{3,2,1,0:T(8,128)(2,1)S(1)} reshape(bf16[32,16,1024]{2,1,0:T(8,128)(2,1)} %all-to-all-done.1) | data formatting | bytes 2097152 | tf_op jit(solution)/shard_map/reshape | solution.py:67
  146.7 0.0 copy-start.4
  146.7 2.3 %convert_bitcast_fusion.1 = bf16[32,4,16,16,64,1]{4,3,1,0,2,5:T(8,128)(2,1)S(1)} fusion(bf16[32,4,16,16]{3,2,1,0:T(8,128)(2,1)S(1)} %copy.37, bf16[32,16,16,64]{3,2,1,0:T(8,128)(2,1)S(1)} %reshape.40), kind=kOutput, calls=%fused_computation.8 | convolution fusion | flops 69206016 | bytes 5308416 | tf_op jit(solution)/shard_map/itpq,ilqr->itlpr/dot_general | solution.py:68
  149.0 0.0 copy-done.4
  149.0 0.0 copy-start.5
  149.0 0.0 copy-start.1
  149.1 5.0 %fusion.35 = bf16[4,16,16,64]{3,1,2,0:T(8,128)(2,1)S(1)} fusion(bf16[32,4,16,16,64,1]{4,3,1,0,2,5:T(8,128)(2,1)S(1)} %convert_bitcast_fusion.1, f32[32,4,64,64]{3,2,1,0:T(8,128)S(1)} %copy-done.4, f32[32,4]{0,1:T(4,128)S(1)} %get-tuple-element.9), kind=kOutput, calls=%fused_computation.26 | convolution fusion | flops 1078001664 | bytes 6423040 | tf_op jit(solution)/shard_map/itlpr,itdmr->dlpm/dot_general | solution.py:71
  154.1 0.0 copy-done.5
  154.1 0.3 pad_maximum_fusion
  154.4 0.7 copy.39
  155.1 0.6 convert_element_type.76
  155.7 0.2 copy.40
  155.9 25.5 %all_to_all.15 = bf16[16,4,4,1024]{3,2,1,0:T(4,128)(2,1)S(1)} all-to-all(bf16[16,4,4,1024]{3,2,1,0:T(4,128)(2,1)S(1)} %copy.40), channel_id=1, replica_groups=mesh['op'=16,'sec'=32] {'op'}, dimensions={0} | all-to-all | bytes 1048576 | tf_op jit(solution)/shard_map/all_to_all | solution.py:103
  181.4 0.8 reduce_sum.41
  182.2 0.0 copy-done.1
  (3 shorter events, 0.0 us)
Async XLA Ops:
  0.0 3.1 %copy-start = (bf16[4,64,1024]{2,1,0:T(8,128)(2,1)S(1)}, bf16[4,64,1024]{2,1,0:T(8,128)(2,1)}, u32[]{:S(2)}) copy-start(bf16[4,64,1024]{2,1,0:T(8,128)(2,1)} %param.6) | copy-start | bytes 1572868
  2.8 17.4 %copy-start.2 = (bf16[32,64,4,64]{3,0,1,2:T(8,128)(2,1)}, bf16[32,64,4,64]{3,0,1,2:T(8,128)(2,1)S(1)}, u32[]{:S(2)}) copy-start(bf16[32,64,4,64]{3,0,1,2:T(8,128)(2,1)S(1)} %convert_bitcast_fusion.2) | copy-start | bytes 3145732
  6.2 14.0 %copy-start.7 = (s32[8,128]{1,0:T(8,128)S(1)}, s32[8,128]{1,0:T(8,128)}, u32[]{:S(2)}) copy-start(s32[8,128]{1,0:T(8,128)} %param.10) | copy-start | bytes 12292
  6.2 14.2 %copy-start.6 = (bf16[8,4,16,16]{3,2,1,0:T(8,128)(2,1)S(1)}, bf16[8,4,16,16]{3,2,1,0:T(8,128)(2,1)}, u32[]{:S(2)}) copy-start(bf16[8,4,16,16]{3,2,1,0:T(8,128)(2,1)} %param.9) | copy-start | bytes 49156
  6.2 16.6 %copy-start.8 = (s32[8,4]{0,1:T(4,128)S(1)}, s32[8,4]{0,1:T(4,128)}, u32[]{:S(2)}) copy-start(s32[8,4]{0,1:T(4,128)} %param.11) | copy-start | bytes 388
  6.2 16.7 %copy-start.9 = (bf16[4,4,64,64]{3,2,1,0:T(8,128)(2,1)S(1)}, bf16[4,4,64,64]{3,2,1,0:T(8,128)(2,1)}, u32[]{:S(2)}) copy-start(bf16[4,4,64,64]{3,2,1,0:T(8,128)(2,1)} %param.8) | copy-start | bytes 393220
  6.2 85.5 %all-to-all-start = ((bf16[32,48,1024]{2,1,0:T(8,128)(2,1)}), bf16[32,48,1024]{2,1,0:T(8,128)(2,1)}, u32[]{:S(2)}, u32[]{:S(2)}) async-start(bf16[32,48,1024]{2,1,0:T(8,128)(2,1)} %bitcast_convert_fusion), calls=%async_computation | async-start | bytes 6291456 | tf_op jit(solution)/shard_map/all_to_all | solution.py:84
  23.8 4.4 %slice-start = ((bf16[32,64,4,64]{3,0,1,2:T(8,128)(2,1)}), bf16[32,16,4,64]{3,0,1,2:T(8,128)(2,1)S(1)}, s32[]{:S(2)}) async-start(bf16[32,64,4,64]{3,0,1,2:T(8,128)(2,1)} %copy-done.2), calls=%async_computation.3 | async-start | bytes 1048576 | tf_op jit(solution)/shard_map/slice | solution.py:34
  100.9 42.7 %all-to-all-start.1 = ((bf16[32,16,1024]{2,1,0:T(8,128)(2,1)}), bf16[32,16,1024]{2,1,0:T(8,128)(2,1)}, u32[]{:S(2)}, u32[]{:S(2)}) async-start(bf16[32,16,1024]{2,1,0:T(8,128)(2,1)} %bitcast_convert_fusion.2), calls=%async_computation.1 | async-start | bytes 2097152 | tf_op jit(solution)/shard_map/all_to_all | solution.py:96
  109.9 13.8 %copy-start.3 = (f32[32,4,64,64]{3,2,1,0:T(8,128)S(1)}, f32[32,4,64,64]{3,2,1,0:T(8,128)}, u32[]{:S(2)}) copy-start(f32[32,4,64,64]{3,2,1,0:T(8,128)} %copy.27) | copy-start | bytes 6291460
  146.7 2.3 %copy-start.4 = (f32[32,4,64,64]{3,2,1,0:T(8,128)S(1)}, f32[32,4,64,64]{3,2,1,0:T(8,128)}, u32[]{:S(2)}) copy-start(f32[32,4,64,64]{3,2,1,0:T(8,128)} %copy.27) | copy-start | bytes 6291460
  149.0 5.0 %copy-start.5 = (bf16[4,48,16,64]{3,1,2,0:T(8,128)(2,1)S(1)}, bf16[4,48,16,64]{3,1,2,0:T(8,128)(2,1)}, u32[]{:S(2)}) copy-start(bf16[4,48,16,64]{3,1,2,0:T(8,128)(2,1)} %fusion.20) | copy-start | bytes 1179652
  149.0 33.2 %copy-start.1 = (bf16[4,64,1024]{2,1,0:T(8,128)(2,1)S(1)}, bf16[4,64,1024]{2,1,0:T(8,128)(2,1)}, u32[]{:S(2)}) copy-start(bf16[4,64,1024]{2,1,0:T(8,128)(2,1)} %param.6) | copy-start | bytes 1572868
